TPU v7x, 32 devices: a whole 2x2x4 slice. The times are simulated.
32 devices in a mesh: dp: 8 (over z, y), pair: 4 (over x, core).
Axes of the slice: x: 2, y: 2, z: 4, core: 2. Of those that a mesh axis runs over, the one named last changes fastest.
Arguments:
- embeddings: float32 [4096, 1024], P(('dp', 'pair'))
- labels: int32 [4096], P(('dp', 'pair')), may hold values from 0 to 31, as said below
Outputs:
- closest: float32 [4096], P(('dp', 'pair'))
Inputs may be any that keep to these rules, and one draw needn't show every extreme that they name: labels // 4 is the owning index of dp of a cluster. In each aligned block of 128 documents (the documents of one device) at most 40 documents belong to one owning index; one owning index, drawn from the seed, gets exactly 40 documents of every block.
All inputs are finite; a program needn't handle non-finite values.
Results may differ from a plain program's by a relative error of at most 0.0003.
Values may be sent and summed in bfloat16 or wider, within the bound.
No kernel may reach another device: no remote copies, remote signals or barrier semaphores. Data moves between devices by JAX's collectives and lax.ppermute only.
A program may use at most 64 MiB of HBM per device.

v0:
```python
import jax
import jax.numpy as jnp
from jax import lax
from jax.sharding import PartitionSpec as P

CPO = 4


floor_value = -2.0


def scored(left, left_labels, right, right_labels):
    score = jnp.einsum("id,jd->ij", left, right, preferred_element_type=jnp.float32)
    same = (left_labels[:, None] == right_labels[None, :]) & (left_labels[:, None] >= 0)
    return (score, same)


def shards(embeddings, labels):
    rows, width = embeddings.shape
    groups = lax.axis_size("dp")
    capacity = 5 * rows // (2 * groups)
    slots = groups * capacity
    norm = jnp.sqrt(jnp.sum(embeddings * embeddings, axis=1, keepdims=True) + 1e-06)
    unit = (embeddings / norm).astype(jnp.bfloat16)
    owner = labels // CPO
    onehot = (owner[:, None] == jnp.arange(groups, dtype=jnp.int32)[None, :]).astype(jnp.int32)
    rank = jnp.sum(jnp.cumsum(onehot, axis=0) * onehot, axis=1) - 1
    slot = owner * capacity + rank
    outgoing = jnp.zeros((slots, width), jnp.bfloat16).at[slot].set(unit)
    out_labels = jnp.full((slots,), -1, jnp.int32).at[slot].set(labels)
    block, block_labels = (
        lax.all_to_all(
            outgoing.reshape(groups, capacity, width), "dp", split_axis=0, concat_axis=0, tiled=True
        ),
        lax.all_to_all(
            out_labels.reshape(groups, capacity), "dp", split_axis=0, concat_axis=0, tiled=True
        ),
    )
    block = block.reshape(slots, width)
    block_labels = block_labels.reshape(slots)
    lane = jnp.arange(slots, dtype=jnp.int32)
    empty = jnp.full((slots,), floor_value, jnp.float32)
    own_index = lax.axis_index("pair") * slots + lane
    other = lax.all_gather(block, "pair", axis=0, tiled=True)
    other_labels = lax.all_gather(block_labels, "pair", axis=0, tiled=True)
    score, same = scored(block, block_labels, other, other_labels)
    other_index = jnp.arange(other.shape[0], dtype=jnp.int32)
    same = same & (own_index[:, None] != other_index[None, :])
    best = jnp.maximum(empty, jnp.max(jnp.where(same, score, floor_value), axis=1))
    returned = lax.all_to_all(
        best.reshape(groups, capacity), "dp", split_axis=0, concat_axis=0, tiled=True
    ).reshape(slots)
    return returned[slot]


def solution(mesh):
    in_specs = (P(("dp", "pair"), None), P(("dp", "pair")))
    out_specs = P(("dp", "pair"))
    return jax.shard_map(shards, mesh=mesh, in_specs=in_specs, out_specs=out_specs, check_vma=False)
```

profile of v0, /device:TPU:0, one launch (start us, length us, event | category | flops | bytes accessed | tf_op | source)
XLA Modules:
  0.0 86.8 jit_solution(12749950310563899110)
XLA Ops:
  6.5 0.0 all-gather.2.cloned.1.call-start
  6.5 0.7 and_select_fusion
  7.2 0.1 fusion.5
  7.3 0.2 reduce_window_sum.11
  7.5 0.2 select_reduce_fusion
  7.6 0.7 compare_select_fusion
  8.3 1.2 %multiply_reduce_fusion = f32[128]{0:T(128)S(1)} fusion(f32[128,1024]{1,0:T(8,128)} %param.2), kind=kLoop, calls=%fused_computation.8 | loop fusion | flops 262016 | bytes 524800 | tf_op jit(solution)/shard_map/reduce_sum | solution.py:23
  9.5 0.0 copy-start
  9.5 1.9 %scatter_custom_fusion.1 = bf16[320,1024]{1,0:T(8,128)(2,1)S(1)} fusion(s32[128]{0:T(128)S(1)} %compare_select_fusion, bf16[]{:T(256)} %constant.41.clone.1, f32[128,1024]{1,0:T(8,128)} %param.2, f32[128]{0:T(128)S(1)} %add_sqrt_fusion), kind=kCustom, calls=%fused_computation.9 | custom fusion | flops 262144 | bytes 1180162 | tf_op jit(solution)/shard_map/scatter | solution.py:29
  11.4 24.9 %all_to_all.20 = bf16[8,40,1024]{2,1,0:T(8,128)(2,1)} all-to-all(bf16[8,40,1024]{2,1,0:T(8,128)(2,1)S(1)} %bitcast.7), channel_id=1, replica_groups=mesh['dp'=8,'pair'=4] {'dp'}, dimensions={0} | all-to-all | bytes 1310720 | tf_op jit(solution)/shard_map/all_to_all | solution.py:32
  36.3 0.0 all-gather.2.cloned.1.call-update
  36.4 1.1 %scatter_custom_fusion = s32[320]{0:T(512)S(1)} fusion(s32[128]{0:T(128)S(1)} %compare_select_fusion, s32[128]{0:T(128)} %param.3, s32[]{:T(128)} %constant.13.clone.1), kind=kCustom, calls=%fused_computation.24 | custom fusion | bytes 1792 | tf_op jit(solution)/shard_map/scatter | solution.py:30
  37.5 0.7 all_to_all.13
  38.2 3.3 %all-to-all-start = ((s32[8,1,40]{2,1,0:T(1,128)}), s32[8,1,40]{2,1,0:T(1,128)S(1)}, u32[]{:S(2)}, u32[]{:S(2)}) async-start(s32[8,1,40]{2,1,0:T(1,128)} %all_to_all.13), calls=%async_computation | async-start | bytes 8192 | tf_op jit(solution)/shard_map/all_to_all | solution.py:35
  41.4 0.0 copy-done
  41.4 0.6 dynamic-slice
  42.7 5.1 %all-to-all-done = s32[8,1,40]{2,1,0:T(1,128)S(1)} async-done(((s32[8,1,40]{2,1,0:T(1,128)}), s32[8,1,40]{2,1,0:T(1,128)S(1)}, u32[]{:S(2)}, u32[]{:S(2)}) %all-to-all-start) | async-done | bytes 1312 | tf_op jit(solution)/shard_map/all_to_all | solution.py:35
  47.8 0.5 broadcast.64
  48.3 0.7 reduce.6
  49.0 0.1 reshape.84
  49.1 0.3 dynamic-update-slice
  49.4 5.1 %all-reduce = s32[1280]{0:T(1024)S(1)} all-reduce(s32[1280]{0:T(1024)S(1)} %dynamic-update-slice), channel_id=1, replica_groups=mesh['dp'=8,'pair'=4] {'pair'}, use_global_device_ids=true, to_apply=%add | all-reduce | flops 1280 | bytes 10240
  54.5 6.4 %all-gather.2.cloned.1.call-done = bf16[1280,1024]{1,0:T(8,128)(2,1)} async-done(((bf16[320,1024]{1,0:T(8,128)(2,1)}), bf16[1280,1024]{1,0:T(8,128)(2,1)}) %all-gather.2.cloned.1.call-update) | async-done | bytes 2621456 | tf_op jit(solution)/shard_map/all_gather | solution.py:44
  60.9 3.3 %fusion.1 = f32[320]{0:T(512)S(1)} fusion(bf16[320,1024]{1,0:T(8,128)(2,1)} %bitcast.6, bf16[1280,1024]{1,0:T(8,128)(2,1)} %all-gather.2.cloned.1.call-done, s32[320]{0:T(512)S(1)} %iota_add_fusion, s32[1280]{0:T(1024)S(1)} %all-reduce, s32[320]{0:T(512)S(1)} %reshape.84, pred[320]{0:T(512)(128)(4,1)S(1)} %broadcast_compare_fusion), kind=kOutput, calls=%fused_computation.6 | convolution fusion | flops 841318080 | bytes 3286080 | tf_op jit(solution)/shard_map/id,jd->ij/dot_general | solution.py:13
  64.2 0.7 max_broadcast_in_dim.15
  64.9 5.5 %all-to-all-start.2 = ((f32[8,1,40]{2,1,0:T(1,128)}), f32[8,1,40]{2,1,0:T(1,128)S(1)}, u32[]{:S(2)}, u32[]{:S(2)}) async-start(f32[8,1,40]{2,1,0:T(1,128)} %max_broadcast_in_dim.15), calls=%async_computation.2 | async-start | bytes 8192 | tf_op jit(solution)/shard_map/all_to_all | solution.py:50
  70.4 6.5 %all-to-all-done.2 = f32[8,1,40]{2,1,0:T(1,128)S(1)} async-done(((f32[8,1,40]{2,1,0:T(1,128)}), f32[8,1,40]{2,1,0:T(1,128)S(1)}, u32[]{:S(2)}, u32[]{:S(2)}) %all-to-all-start.2) | async-done | bytes 1312 | tf_op jit(solution)/shard_map/all_to_all | solution.py:50
  76.9 0.5 broadcast.65
  77.4 0.7 reduce.7
  78.1 0.1 reshape.56
  78.2 1.8 %gather_fusion = f32[128]{0:T(128)} fusion(f32[320]{0:T(512)S(1)} %reshape.56, s32[1024]{0:T(1024)S(1)} %pad_clamp_fusion), kind=kCustom, calls=%fused_computation | custom fusion | bytes 1536 | tf_op jit(solution)/shard_map/gather | solution.py:53
  (6 shorter events, 0.0 us)
Async XLA Ops:
  6.5 54.4 %all-gather.2.cloned.1.call-start = ((), (), s32[]{:S(2)}) async-start(), calls=%async_computation.3 | async-start | bytes 3276800 | tf_op jit(solution)/shard_map/all_gather | solution.py:44
  9.5 32.0 %copy-start = (u32[32]{0:T(128)S(1)}, u32[32]{0:T(128)}, u32[]{:S(2)}) copy-start(u32[32]{0:T(128)} %constant.48) | copy-start | bytes 388
  38.2 9.7 %all-to-all-start = ((s32[8,1,40]{2,1,0:T(1,128)}), s32[8,1,40]{2,1,0:T(1,128)S(1)}, u32[]{:S(2)}, u32[]{:S(2)}) async-start(s32[8,1,40]{2,1,0:T(1,128)} %all_to_all.13), calls=%async_computation | async-start | bytes 8192 | tf_op jit(solution)/shard_map/all_to_all | solution.py:35
  64.9 12.0 %all-to-all-start.2 = ((f32[8,1,40]{2,1,0:T(1,128)}), f32[8,1,40]{2,1,0:T(1,128)S(1)}, u32[]{:S(2)}, u32[]{:S(2)}) async-start(f32[8,1,40]{2,1,0:T(1,128)} %max_broadcast_in_dim.15), calls=%async_computation.2 | async-start | bytes 8192 | tf_op jit(solution)/shard_map/all_to_all | solution.py:50
Sparse Core Ops, SparseCore 0:
  36.5 24.3 all-gather.1
where the time goes:
time: 87.2 us; the launch traced here: 86.8 us
  blocking collectives  30 us (34%)
  waiting for transfers between devices  18 us (21%)
  between operations  14.2 us (16%)
  starting transfers between devices  8.78 us (10%)
  local copies, waits for them, and re-layouts  6.29 us (7%)
  other arithmetic  6.21 us (7%)
  matrix products  3.33 us (4%)
    all_to_all x1, blocking collectives, shards(): lax.all_to_all(outgoing.reshape(groups, capacity, width), 'dp', split_axi...  24.9 us
    all_to_all x1, waiting for transfers between devices, shards(): lax.all_to_all(best.reshape(groups, capacity), 'dp', split_axis=0, concat...  6.46 us
    all_gather x1, waiting for transfers between devices, shards(): other = lax.all_gather(block, 'pair', axis=0, tiled=True)  6.39 us
    all_to_all x1, starting transfers between devices, shards(): lax.all_to_all(best.reshape(groups, capacity), 'dp', split_axis=0, concat...  5.52 us
    all_to_all x1, waiting for transfers between devices, shards(): lax.all_to_all(out_labels.reshape(groups, capacity), 'dp', split_axis=0,...  5.14 us
    unnamed x1, blocking collectives  5.12 us
    dot_general x1, matrix products, scored(): jnp.einsum('id,jd->ij', left, right, preferred_element_type=jnp.float32)  3.33 us
    all_to_all x1, starting transfers between devices, shards(): lax.all_to_all(out_labels.reshape(groups, capacity), 'dp', split_axis=0,...  3.26 us
  transfers between devices with their start and end apart: 3, of which 3 were waited for; matrix products, arithmetic and copies ran while one was open for 4% of the time, Pallas kernels for 0%

commit v1 on v0

v1 whole, which is shorter than its diff:
```python
import jax
import jax.numpy as jnp
from jax import lax
from jax.sharding import PartitionSpec as P

CPO = 4


floor_value = -2.0


def shards(embeddings, labels):
    rows, width = embeddings.shape
    groups = lax.axis_size("dp")
    peers = lax.axis_size("pair")
    capacity = 5 * rows // (2 * groups)
    chunk = capacity + 1
    norm = jnp.sqrt(jnp.sum(embeddings * embeddings, axis=1, keepdims=True) + 1e-06)
    unit = (embeddings / norm).astype(jnp.bfloat16)
    owner = labels // CPO
    local = labels - owner * CPO
    onehot = (owner[:, None] == jnp.arange(groups, dtype=jnp.int32)[None, :]).astype(jnp.int32)
    rank = jnp.sum(jnp.cumsum(onehot, axis=0) * onehot, axis=1) - 1
    tag = jnp.full((groups, width), -1.0, jnp.bfloat16)
    tag = tag.at[owner, rank].set(local.astype(jnp.bfloat16))
    outgoing = jnp.zeros((groups, chunk, width), jnp.bfloat16).at[owner, rank].set(unit)
    outgoing = outgoing.at[:, capacity, :].set(tag)
    block = lax.all_to_all(outgoing, "dp", split_axis=0, concat_axis=0, tiled=True)
    tiled_block = jnp.broadcast_to(block[None], (peers,) + block.shape).reshape(
        (peers * groups, chunk, width)
    )
    other = lax.all_to_all(tiled_block, "pair", split_axis=0, concat_axis=0, tiled=True)
    other = other.reshape(peers, groups, chunk, width)
    block_labels = block[:, capacity, :chunk].astype(jnp.int32).reshape(groups * chunk)
    other_labels = other[:, :, capacity, :chunk].astype(jnp.int32).reshape(peers * groups * chunk)
    left = block.reshape(groups * chunk, width)
    right = other.reshape(peers * groups * chunk, width)
    score = jnp.einsum("id,jd->ij", left, right, preferred_element_type=jnp.float32)
    lane = jnp.arange(groups * chunk, dtype=jnp.int32)
    own_index = lax.axis_index("pair") * (groups * chunk) + lane
    other_index = jnp.arange(peers * groups * chunk, dtype=jnp.int32)
    same = (
        (block_labels[:, None] == other_labels[None, :])
        & (block_labels[:, None] >= 0)
        & (own_index[:, None] != other_index[None, :])
    )
    best = jnp.max(jnp.where(same, score, floor_value), axis=1)
    returned = lax.all_to_all(
        best.reshape(groups, chunk), "dp", split_axis=0, concat_axis=0, tiled=True
    )
    return returned[owner, rank]


def solution(mesh):
    in_specs = (P(("dp", "pair"), None), P(("dp", "pair")))
    out_specs = P(("dp", "pair"))
    return jax.shard_map(shards, mesh=mesh, in_specs=in_specs, out_specs=out_specs, check_vma=False)
```

time: 87.2 us -> 108 us (1.24)
  local copies, waits for them, and re-layouts: 6.29 us -> 25.2 us
  waiting for transfers between devices: 18 us -> 33.9 us
  between operations: 14.2 us -> 0.11 us
  blocking collectives: 30 us -> 37.1 us
  starting transfers between devices: 8.78 us -> 3.7 us
  other arithmetic: 6.21 us -> 4.23 us
    all_to_all x2 -> x1, waiting for transfers between devices: 11.6 us -> 33.9 us  [shards(): lax.all_to_all(tiled_block, 'pair', split_axis=0, concat_axis=0, tiled=True)]
    scatter x1 -> x4, local copies, waits for them, and re-layouts: 1.11 us -> 15.8 us  [the longest x1 8.45 us: shards(): jnp.zeros((groups, chunk, width), jnp.bfloat16).at[owner, rank].set(unit)]
    all_to_all x1 -> x2, blocking collectives: 24.9 us -> 37.1 us  [the longest x1 27.2 us: shards(): lax.all_to_all(outgoing, 'dp', split_axis=0, concat_axis=0, tiled=True)]
    all_gather x1 -> x0, waiting for transfers between devices: 6.39 us -> none  [shards(): other = lax.all_gather(block, 'pair', axis=0, tiled=True)]
    unnamed x1 -> x0, blocking collectives: 5.12 us -> none
    all_to_all x2 -> x1, starting transfers between devices: 8.77 us -> 3.7 us  [shards(): lax.all_to_all(tiled_block, 'pair', split_axis=0, concat_axis=0, tiled=True)]
    convert_element_type x0 -> x4, other arithmetic: none -> 2.61 us  [the longest x1 1.14 us: shards(): unit = (embeddings / norm).astype(jnp.bfloat16)]
    broadcast_in_dim x0 -> x3, local copies, waits for them, and re-layouts: none -> 2.14 us  [the longest x1 2.06 us: shards(): jnp.broadcast_to(block[None], (peers,) + block.shape)]
  transfers between devices with their start and end apart: 3 -> 1, of which waited for: 3 -> 1; matrix products, arithmetic and copies ran while one was open for 4% -> 3% of each run, Pallas kernels for 0% -> 0%
where the time goes in v1:
time: 108 us
  blocking collectives  37.1 us (34%)
  waiting for transfers between devices  33.9 us (31%)
  local copies, waits for them, and re-layouts  25.2 us (23%)
  other arithmetic  4.23 us (4%)
  starting transfers between devices  3.7 us (3%)
  matrix products  3.5 us (3%)
    all_to_all x1, waiting for transfers between devices, shards(): lax.all_to_all(tiled_block, 'pair', split_axis=0, concat_axis=0, tiled=True)  33.9 us
    all_to_all x1, blocking collectives, shards(): lax.all_to_all(outgoing, 'dp', split_axis=0, concat_axis=0, tiled=True)  27.2 us
    all_to_all x1, blocking collectives, shards(): lax.all_to_all(best.reshape(groups, chunk), 'dp', split_axis=0, concat_ax...  9.85 us
    scatter x1, local copies, waits for them, and re-layouts, shards(): jnp.zeros((groups, chunk, width), jnp.bfloat16).at[owner, rank].set(unit)  8.45 us
    scatter x1, local copies, waits for them, and re-layouts, shards(): tag = tag.at[owner, rank].set(local.astype(jnp.bfloat16))  6.96 us
    all_to_all x1, starting transfers between devices, shards(): lax.all_to_all(tiled_block, 'pair', split_axis=0, concat_axis=0, tiled=True)  3.7 us
    dot_general x1, matrix products, shards(): jnp.einsum('id,jd->ij', left, right, preferred_element_type=jnp.float32)  3.5 us
    another operation x1, local copies, waits for them, and re-layouts, shards(): right = other.reshape(peers * groups * chunk, width)  2.42 us
  transfers between devices with their start and end apart: 1, of which 1 were waited for; matrix products, arithmetic and copies ran while one was open for 3% of the time, Pallas kernels for 0%

profile of v1, /device:TPU:0, one launch (start us, length us, event | category | flops | bytes accessed | tf_op | source)
XLA Modules:
  0.0 107.7 jit_solution(17339560749700790452)
XLA Ops:
  0.0 1.2 %multiply_reduce_fusion = f32[128]{0:T(128)S(1)} fusion(f32[128,1024]{1,0:T(8,128)} %param.4), kind=kLoop, calls=%fused_computation.8 | loop fusion | flops 262016 | bytes 524800 | tf_op jit(solution)/shard_map/reduce_sum | solution.py:18
  1.2 0.7 subtract_convert_fusion
  1.8 0.1 fusion.2
  1.9 0.2 reduce_window_sum.11
  2.1 0.2 select_reduce_fusion
  2.3 1.1 %divide_convert_fusion = bf16[128,1024]{1,0:T(8,128)(2,1)S(1)} fusion(f32[128,1024]{1,0:T(8,128)} %param.4, f32[128]{0:T(128)S(1)} %add_sqrt_fusion), kind=kLoop, calls=%fused_computation.7 | loop fusion | flops 262144 | bytes 786944 | tf_op jit(solution)/shard_map/convert_element_type | solution.py:19
  3.5 7.0 %scatter_fusion.1 = bf16[8,1024]{1,0:T(8,128)(2,1)S(1)} fusion(bf16[8,1024]{1,0:T(8,128)(2,1)S(1)} %broadcast_in_dim.13, s32[128]{0:T(128)S(1)} %get-tuple-element.21, bf16[128]{0:T(256)(128)(2,1)S(1)} %get-tuple-element.17), kind=kCustom, calls=%fused_computation.2 | custom fusion | bytes 1792 | tf_op jit(solution)/shard_map/scatter | solution.py:25
  10.4 0.1 broadcast_in_dim.11
  10.5 8.5 %scatter_fusion = bf16[8,41,1024]{2,0,1:T(8,128)(2,1)S(1)} fusion(bf16[8,41,1024]{2,0,1:T(8,128)(2,1)S(1)} %broadcast_in_dim.11, s32[128]{0:T(128)S(1)} %get-tuple-element.20, bf16[128,1024]{1,0:T(8,128)(2,1)S(1)} %divide_convert_fusion), kind=kCustom, calls=%fused_computation.1 | custom fusion | bytes 787456 | tf_op jit(solution)/shard_map/scatter | solution.py:26
  19.0 0.4 copy.6
  19.4 27.2 %all_to_all.22 = bf16[8,41,1024]{2,1,0:T(8,128)(2,1)S(1)} all-to-all(bf16[8,41,1024]{2,1,0:T(8,128)(2,1)S(1)} %copy.6), channel_id=1, replica_groups=mesh['dp'=8,'pair'=4] {'dp'}, dimensions={0} | all-to-all | bytes 1343488 | tf_op jit(solution)/shard_map/all_to_all | solution.py:28
  46.6 0.0 copy-start
  46.6 0.9 copy-done
  47.5 2.1 %broadcast_in_dim.14 = bf16[4,8,41,1024]{3,2,1,0:T(8,128)(2,1)} broadcast(bf16[8,41,1024]{2,1,0:T(8,128)(2,1)S(1)} %all_to_all.22), dimensions={1,2,3} | broadcast | bytes 3358720 | tf_op jit(solution)/shard_map/broadcast_in_dim | solution.py:29
  49.5 3.7 %all-to-all-start.1 = ((bf16[32,41,1024]{2,1,0:T(8,128)(2,1)}), bf16[32,41,1024]{2,1,0:T(8,128)(2,1)S(1)}, u32[]{:S(2)}, u32[]{:S(2)}) async-start(bf16[32,41,1024]{2,1,0:T(8,128)(2,1)} %bitcast.56), calls=%async_computation.1 | async-start | bytes 6291456 | tf_op jit(solution)/shard_map/all_to_all | solution.py:32
  53.3 0.7 fusion.4
  54.0 0.1 reshape.114
  54.1 2.2 %reshape.113 = bf16[328,1024]{1,0:T(8,128)(2,1)} reshape(bf16[8,41,1024]{2,1,0:T(8,128)(2,1)} %copy-done) | data formatting | bytes 1343488 | tf_op jit(solution)/shard_map/reshape | solution.py:36
  56.3 33.9 %all-to-all-done.1 = bf16[32,41,1024]{2,1,0:T(8,128)(2,1)S(1)} async-done(((bf16[32,41,1024]{2,1,0:T(8,128)(2,1)}), bf16[32,41,1024]{2,1,0:T(8,128)(2,1)S(1)}, u32[]{:S(2)}, u32[]{:S(2)}) %all-to-all-start.1) | async-done | bytes 2687008 | tf_op jit(solution)/shard_map/all_to_all | solution.py:32
  90.2 0.1 fusion.3
  90.2 0.1 reshape.115
  90.3 2.4 %reshape_reshape.3 = bf16[1312,1024]{1,0:T(8,128)(2,1)} reshape(bf16[32,41,1024]{2,1,0:T(8,128)(2,1)S(1)} %all-to-all-done.1) | data formatting | bytes 5373952 | tf_op jit(solution)/shard_map/reshape;reshape | solution.py:37
  92.7 3.5 %fusion.1 = f32[328]{0:T(512)S(1)} fusion(bf16[328,1024]{1,0:T(8,128)(2,1)} %reshape.113, bf16[1312,1024]{1,0:T(8,128)(2,1)} %reshape_reshape.3, s32[328]{0:T(512)S(1)} %iota_add_fusion, s32[1312]{0:T(1024)S(1)} %reshape.115, s32[328]{0:T(512)S(1)} %reshape.114, pred[328]{0:T(512)(128)(4,1)S(1)} %broadcast_compare_fusion), kind=kOutput, calls=%fused_computation.6 | convolution fusion | flops 883909824 | bytes 3368232 | tf_op jit(solution)/shard_map/id,jd->ij/dot_general | solution.py:38
  96.2 0.1 all_to_all.16
  96.3 9.8 %all_to_all.23 = f32[8,1,41]{2,1,0:T(1,128)S(1)} all-to-all(f32[8,1,41]{2,1,0:T(1,128)S(1)} %all_to_all.16), channel_id=1, replica_groups=mesh['dp'=8,'pair'=4] {'dp'}, dimensions={0} | all-to-all | bytes 2624 | tf_op jit(solution)/shard_map/all_to_all | solution.py:48
  106.2 1.5 %gather_fusion = f32[128]{0:T(128)} fusion(f32[8,41]{1,0:T(8,128)S(1)} %bitcast.54, s32[128]{0:T(128)S(1)} %get-tuple-element.19), kind=kCustom, calls=%fused_computation | custom fusion | bytes 2048 | tf_op jit(solution)/shard_map/gather | solution.py:51
  (6 shorter events, 0.0 us)
Async XLA Ops:
  46.6 0.9 copy-start
  49.5 40.6 %all-to-all-start.1 = ((bf16[32,41,1024]{2,1,0:T(8,128)(2,1)}), bf16[32,41,1024]{2,1,0:T(8,128)(2,1)S(1)}, u32[]{:S(2)}, u32[]{:S(2)}) async-start(bf16[32,41,1024]{2,1,0:T(8,128)(2,1)} %bitcast.56), calls=%async_computation.1 | async-start | bytes 6291456 | tf_op jit(solution)/shard_map/all_to_all | solution.py:32

commit v2 on v1

v2 whole, which is shorter than its diff:
```python
import jax
import jax.numpy as jnp
from jax import lax
from jax.sharding import PartitionSpec as P

CPO = 4


floor_value = -2.0


def piece_best(left, left_labels, right, right_labels, exclude_self):
    score = jnp.einsum("id,jd->ij", left, right, preferred_element_type=jnp.float32)
    same = (left_labels[:, None] == right_labels[None, :]) & (left_labels[:, None] >= 0)
    if exclude_self:
        lane = jnp.arange(left.shape[0], dtype=jnp.int32)
        same = same & (lane[:, None] != lane[None, :])
    return jnp.max(jnp.where(same, score, floor_value), axis=1)


def chunk_labels(block, capacity, chunk):
    groups = block.shape[0]
    return block[:, capacity, :chunk].astype(jnp.int32).reshape(groups * chunk)


def shards(embeddings, labels):
    rows, width = embeddings.shape
    groups = lax.axis_size("dp")
    peers = lax.axis_size("pair")
    capacity = 5 * rows // (2 * groups)
    chunk = -(-(capacity + 1) // 16) * 16
    slots = groups * chunk
    norm = jnp.sqrt(jnp.sum(embeddings * embeddings, axis=1, keepdims=True) + 1e-06)
    unit = (embeddings / norm).astype(jnp.bfloat16)
    owner = labels // CPO
    local = labels - owner * CPO
    onehot = (owner[:, None] == jnp.arange(groups, dtype=jnp.int32)[None, :]).astype(jnp.int32)
    rank = jnp.sum(jnp.cumsum(onehot, axis=0) * onehot, axis=1) - 1
    slot = owner * chunk + rank
    place = slot[None, :] == jnp.arange(slots, dtype=jnp.int32)[:, None]
    outgoing = jnp.dot(place.astype(jnp.bfloat16), unit, preferred_element_type=jnp.float32)
    outgoing = outgoing.astype(jnp.bfloat16).reshape(groups, chunk, width)
    tag = jnp.sum(jnp.where(place, local[None, :] + 1, 0), axis=1) - 1
    tag_row = jnp.full((groups, width), -1, jnp.int32).at[:, :chunk].set(tag.reshape(groups, chunk))
    row_id = jnp.arange(chunk, dtype=jnp.int32)
    outgoing = jnp.where(
        (row_id == capacity)[None, :, None], tag_row.astype(jnp.bfloat16)[:, None, :], outgoing
    )
    block = lax.all_to_all(outgoing, "dp", split_axis=0, concat_axis=0, tiled=True)
    pieces = [block]
    bit = peers // 2
    while bit >= 1:
        perm = [(p, p ^ bit) for p in range(peers)]
        pieces = pieces + [lax.ppermute(x, "pair", perm) for x in pieces]
        bit //= 2
    left = block.reshape(slots, width)
    left_labels = chunk_labels(block, capacity, chunk)
    best = None
    for index, piece in enumerate(pieces):
        piece_max = piece_best(
            left,
            left_labels,
            piece.reshape(slots, width),
            chunk_labels(piece, capacity, chunk),
            index == 0,
        )
        best = piece_max if best is None else jnp.maximum(best, piece_max)
    returned = lax.all_to_all(
        best.reshape(groups, chunk), "dp", split_axis=0, concat_axis=0, tiled=True
    ).reshape(slots)
    return jnp.sum(jnp.where(place, returned[:, None], 0.0), axis=0)


def solution(mesh):
    in_specs = (P(("dp", "pair"), None), P(("dp", "pair")))
    out_specs = P(("dp", "pair"))
    return jax.shard_map(shards, mesh=mesh, in_specs=in_specs, out_specs=out_specs, check_vma=False)
```

time: 108 us -> 67.4 us (0.62)
  local copies, waits for them, and re-layouts: 25.2 us -> 1.09 us
  waiting for transfers between devices: 33.9 us -> 16.5 us
  starting transfers between devices: 3.7 us -> 1.5 us
  other arithmetic: 4.23 us -> 5.96 us
    all_to_all x1 -> x0, waiting for transfers between devices: 33.9 us -> none  [shards(): lax.all_to_all(tiled_block, 'pair', split_axis=0, concat_axis=0, tiled=True)]
    ppermute x0 -> x3, waiting for transfers between devices: none -> 16.5 us  [shards(): pieces = pieces + [lax.ppermute(x, 'pair', perm) for x in pieces]]
    scatter x4 -> x1, local copies, waits for them, and re-layouts: 15.8 us -> 0.01 us  [shards(): jnp.full((groups, width), -1, jnp.int32).at[:, :chunk]]
    all_to_all x1 -> x0, starting transfers between devices: 3.7 us -> none  [shards(): lax.all_to_all(tiled_block, 'pair', split_axis=0, concat_axis=0, tiled=True)]
    another operation x1, local copies, waits for them, and re-layouts: 2.42 us -> 0.09 us  [shards(): right = other.reshape(peers * groups * chunk, width)]
    reshape x1 -> x0, local copies, waits for them, and re-layouts: 2.19 us -> none  [shards(): left = block.reshape(groups * chunk, width)]
    broadcast_in_dim x3 -> x1, local copies, waits for them, and re-layouts: 2.14 us -> 0.08 us  [shards(): return jnp.sum(jnp.where(place, returned[:, None], 0.0), axis=0)]
    convert_element_type x4, other arithmetic: 2.61 us -> 0.79 us  [chunk_labels(): return block[:, capacity, :chunk].astype(jnp.int32).reshape(groups * chunk)]
  transfers between devices with their start and end apart: 1 -> 3, of which waited for: 1 -> 1; matrix products, arithmetic and copies ran while one was open for 3% -> 6% of each run, Pallas kernels for 0% -> 0%
where the time goes in v2:
time: 67.4 us; the launch traced here: 67.1 us
  blocking collectives  37.8 us (56%)
  waiting for transfers between devices  16.5 us (24%)
  other arithmetic  5.96 us (9%)
  matrix products  4.04 us (6%)
  starting transfers between devices  1.5 us (2%)
  local copies, waits for them, and re-layouts  1.09 us (2%)
    all_to_all x1, blocking collectives, shards(): lax.all_to_all(outgoing, 'dp', split_axis=0, concat_axis=0, tiled=True)  27.2 us
    ppermute x3, waiting for transfers between devices, shards(): pieces = pieces + [lax.ppermute(x, 'pair', perm) for x in pieces]  16.5 us
    all_to_all x1, blocking collectives, shards(): lax.all_to_all(best.reshape(groups, chunk), 'dp', split_axis=0, concat_ax...  10.6 us
    dot_general x4, matrix products, piece_best(): jnp.einsum('id,jd->ij', left, right, preferred_element_type=jnp.float32)  3.6 us
    ppermute x3, starting transfers between devices, shards(): pieces = pieces + [lax.ppermute(x, 'pair', perm) for x in pieces]  1.5 us
  transfers between devices with their start and end apart: 3, of which 1 were waited for; matrix products, arithmetic and copies ran while one was open for 6% of the time, Pallas kernels for 0%

profile of v2, /device:TPU:0, one launch (start us, length us, event | category | flops | bytes accessed | tf_op | source)
XLA Modules:
  0.0 67.1 jit_solution(10550859859509900793)
XLA Ops:
  0.0 0.0 copy-start
  0.0 0.6 compare_reduce_fusion
  0.6 1.2 %multiply_reduce_fusion = f32[128]{0:T(128)S(1)} fusion(f32[128,1024]{1,0:T(8,128)} %param.4), kind=kLoop, calls=%fused_computation.13 | loop fusion | flops 262016 | bytes 524800 | tf_op jit(solution)/shard_map/reduce_sum | solution.py:33
  1.8 0.7 %subtract_add_fusion = (s32[128]{0:T(128)S(1)}, s32[128]{0:T(128)S(1)}) fusion(s32[128]{0:T(128)} %param.5), kind=kLoop, calls=%fused_computation.39 | loop fusion | flops 2304 | bytes 1536 | tf_op jit(solution)/shard_map/add | solution.py:43
  2.5 0.1 fusion.7
  2.6 0.2 reduce_window_sum.11
  2.8 0.2 select_reduce_fusion.2
  2.9 0.0 copy-done
  3.0 0.4 convolution_convert_fusion
  3.4 0.1 select_reduce_fusion.1
  3.5 0.7 select_convert_fusion
  4.2 0.1 reshape.156
  4.3 0.1 broadcast_select_fusion
  4.4 27.2 %all_to_all.11 = bf16[8,48,1024]{2,1,0:T(8,128)(2,1)S(1)} all-to-all(bf16[8,48,1024]{2,1,0:T(8,128)(2,1)S(1)} %broadcast_select_fusion), channel_id=1, replica_groups=mesh['dp'=8,'pair'=4] {'dp'}, dimensions={0} | all-to-all | bytes 1572864 | tf_op jit(solution)/shard_map/all_to_all | solution.py:49
  31.7 1.5 %collective-permute-start = (bf16[8,48,1024]{2,1,0:T(8,128)(2,1)S(1)}, bf16[8,48,1024]{2,1,0:T(8,128)(2,1)S(1)}, u32[]{:S(2)}, u32[]{:S(2)}) collective-permute-start(bf16[8,48,1024]{2,1,0:T(8,128)(2,1)S(1)} %all_to_all.11), channel_id=1, source_target_pairs={{0,2},{1,3},{2,0},{3,1},{4,6},{5,7},{6,4},{7,5},{8,10},{9,11},{10,... | collective-permute-start | bytes 2359304 | tf_op jit(solution)/shard_map/ppermute | solution.py:54
  33.2 0.0 collective-permute-start.1
  33.2 0.1 reshape.162
  33.3 16.5 %collective-permute-done = bf16[8,48,1024]{2,1,0:T(8,128)(2,1)S(1)} collective-permute-done((bf16[8,48,1024]{2,1,0:T(8,128)(2,1)S(1)}, bf16[8,48,1024]{2,1,0:T(8,128)(2,1)S(1)}, u32[]{:S(2)}, u32[]{:S(2)}) %collective-permute-start) | collective-permute-done | bytes 786464 | tf_op jit(solution)/shard_map/ppermute | solution.py:54
  49.8 0.0 collective-permute-start.2
  49.8 0.6 fusion
  50.4 0.0 collective-permute-done.1
  50.4 0.7 %fusion.9 = s32[8,48]{1,0:T(8,128)S(1)} fusion(bf16[8,48,1024]{2,1,0:T(8,128)(2,1)} %collective-permute-done.1), kind=kLoop, calls=%fused_computation.25 | loop fusion | flops 384 | bytes 2304 | tf_op jit(solution)/shard_map/convert_element_type | solution.py:23
  51.2 0.1 reshape.164
  51.3 0.1 reshape.163
  51.4 1.7 %fusion.2 = f32[384]{0:T(512)S(1)} fusion(bf16[384,1024]{1,0:T(8,128)(2,1)S(1)} %bitcast.14, bf16[384,1024]{1,0:T(8,128)(2,1)} %bitcast.3, s32[384]{0:T(512)S(1)} %reshape.162, s32[384]{0:T(512)S(1)} %reshape.164, pred[384]{0:T(512)(128)(4,1)S(1)} %broadcast_compare_fusion), kind=kOutput, calls=%fused_computation.7 | convolution fusion | flops 302579328 | bytes 1577856 | tf_op jit(solution)/shard_map/id,jd->ij/dot_general | solution.py:13
  53.1 0.6 fusion.1
  53.7 0.0 collective-permute-done.2
  53.8 0.1 reshape.165
  53.9 0.6 fusion.3
  54.5 0.1 max.41
  54.6 10.6 %all_to_all.12 = f32[8,1,48]{2,1,0:T(1,128)S(1)} all-to-all(f32[8,1,48]{2,1,0:T(1,128)S(1)} %max.41), channel_id=1, replica_groups=mesh['dp'=8,'pair'=4] {'dp'}, dimensions={0} | all-to-all | bytes 3072 | tf_op jit(solution)/shard_map/all_to_all | solution.py:68
  65.2 0.5 broadcast.104
  65.7 0.7 reduce.27
  66.4 0.1 broadcast_in_dim.65
  66.5 0.7 select_reduce_fusion
  (9 shorter events, 0.1 us)
Async XLA Ops:
  0.0 2.9 %copy-start = (f32[128,1024]{1,0:T(8,128)S(1)}, f32[128,1024]{1,0:T(8,128)}, u32[]{:S(2)}) copy-start(f32[128,1024]{1,0:T(8,128)} %param.4) | copy-start | bytes 1572868
  31.7 18.2 %collective-permute-start = (bf16[8,48,1024]{2,1,0:T(8,128)(2,1)S(1)}, bf16[8,48,1024]{2,1,0:T(8,128)(2,1)S(1)}, u32[]{:S(2)}, u32[]{:S(2)}) collective-permute-start(bf16[8,48,1024]{2,1,0:T(8,128)(2,1)S(1)} %all_to_all.11), channel_id=1, source_target_pairs={{0,2},{1,3},{2,0},{3,1},{4,6},{5,7},{6,4},{7,5},{8,10},{9,11},{10,... | collective-permute-start | bytes 2359304 | tf_op jit(solution)/shard_map/ppermute | solution.py:54
  33.2 17.3 %collective-permute-start.1 = (bf16[8,48,1024]{2,1,0:T(8,128)(2,1)S(1)}, bf16[8,48,1024]{2,1,0:T(8,128)(2,1)}, u32[]{:S(2)}, u32[]{:S(2)}) collective-permute-start(bf16[8,48,1024]{2,1,0:T(8,128)(2,1)S(1)} %all_to_all.11), channel_id=1, source_target_pairs={{0,1},{1,0},{2,3},{3,2},{4,5},{5,4},{6,7},{7,6},{8,9},{9,8},{10,11... | collective-permute-start | bytes 2359304 | tf_op jit(solution)/shard_map/ppermute | solution.py:54
  49.8 3.9 %collective-permute-start.2 = (bf16[8,48,1024]{2,1,0:T(8,128)(2,1)S(1)}, bf16[8,48,1024]{2,1,0:T(8,128)(2,1)S(1)}, u32[]{:S(2)}, u32[]{:S(2)}) collective-permute-start(bf16[8,48,1024]{2,1,0:T(8,128)(2,1)S(1)} %collective-permute-done), channel_id=1, source_target_pairs={{0,1},{1,0},{2,3},{3,2},{4,5},{5,4},{6,7},{7,6},{8,9},{9,8},{10,11... | collective-permute-start | bytes 2359304 | tf_op jit(solution)/shard_map/ppermute | solution.py:54

commit v3 on v2

--- a/solution.py
+++ b/solution.py
@@ -23,6 +23,24 @@
     return block[:, capacity, :chunk].astype(jnp.int32).reshape(groups * chunk)
 
 
+def dp_exchange(chunks, groups, direction):
+    out = [chunks[0]]
+    for k in range(1, groups):
+        perm = [(d, (d + direction * k) % groups) for d in range(groups)]
+        out.append(lax.ppermute(chunks[k], "dp", perm))
+    return out
+
+
+def pair_gather(x, peers):
+    pieces = [x]
+    bit = peers // 2
+    while bit >= 1:
+        perm = [(p, p ^ bit) for p in range(peers)]
+        pieces = pieces + [lax.ppermute(y, "pair", perm) for y in pieces]
+        bit //= 2
+    return pieces
+
+
 def shards(embeddings, labels):
     rows, width = embeddings.shape
     groups = lax.axis_size("dp")
@@ -30,13 +48,18 @@
     capacity = 5 * rows // (2 * groups)
     chunk = -(-(capacity + 1) // 16) * 16
     slots = groups * chunk
+    by_permute = groups <= 16
     norm = jnp.sqrt(jnp.sum(embeddings * embeddings, axis=1, keepdims=True) + 1e-06)
     unit = (embeddings / norm).astype(jnp.bfloat16)
     owner = labels // CPO
     local = labels - owner * CPO
     onehot = (owner[:, None] == jnp.arange(groups, dtype=jnp.int32)[None, :]).astype(jnp.int32)
     rank = jnp.sum(jnp.cumsum(onehot, axis=0) * onehot, axis=1) - 1
-    slot = owner * chunk + rank
+    if by_permute:
+        dest = (owner - lax.axis_index("dp")) % groups
+    else:
+        dest = owner
+    slot = dest * chunk + rank
     place = slot[None, :] == jnp.arange(slots, dtype=jnp.int32)[:, None]
     outgoing = jnp.dot(place.astype(jnp.bfloat16), unit, preferred_element_type=jnp.float32)
     outgoing = outgoing.astype(jnp.bfloat16).reshape(groups, chunk, width)
@@ -46,13 +69,14 @@
     outgoing = jnp.where(
         (row_id == capacity)[None, :, None], tag_row.astype(jnp.bfloat16)[:, None, :], outgoing
     )
-    block = lax.all_to_all(outgoing, "dp", split_axis=0, concat_axis=0, tiled=True)
-    pieces = [block]
-    bit = peers // 2
-    while bit >= 1:
-        perm = [(p, p ^ bit) for p in range(peers)]
-        pieces = pieces + [lax.ppermute(x, "pair", perm) for x in pieces]
-        bit //= 2
+    if by_permute:
+        arrived = dp_exchange([outgoing[k] for k in range(groups)], groups, 1)
+        gathered = [pair_gather(c, peers) for c in arrived]
+        block = jnp.stack(arrived)
+        pieces = [jnp.stack([g[j] for g in gathered]) for j in range(len(gathered[0]))]
+    else:
+        block = lax.all_to_all(outgoing, "dp", split_axis=0, concat_axis=0, tiled=True)
+        pieces = pair_gather(block, peers)
     left = block.reshape(slots, width)
     left_labels = chunk_labels(block, capacity, chunk)
     best = None
@@ -65,9 +89,12 @@
             index == 0,
         )
         best = piece_max if best is None else jnp.maximum(best, piece_max)
-    returned = lax.all_to_all(
-        best.reshape(groups, chunk), "dp", split_axis=0, concat_axis=0, tiled=True
-    ).reshape(slots)
+    best = best.reshape(groups, chunk)
+    if by_permute:
+        returned = jnp.stack(dp_exchange([best[k] for k in range(groups)], groups, -1))
+    else:
+        returned = lax.all_to_all(best, "dp", split_axis=0, concat_axis=0, tiled=True)
+    returned = returned.reshape(slots)
     return jnp.sum(jnp.where(place, returned[:, None], 0.0), axis=0)
 
 

time: 67.4 us -> 78.6 us (1.17)
  starting transfers between devices: 1.5 us -> 45 us
  blocking collectives: 37.8 us -> 0 us
  waiting for transfers between devices: 16.5 us -> 22.1 us
  other arithmetic: 5.96 us -> 4.59 us
  local copies, waits for them, and re-layouts: 1.09 us -> 2.31 us
    ppermute x3 -> x38, starting transfers between devices: 1.5 us -> 45 us  [the longest x14 34.9 us: dp_exchange(): out.append(lax.ppermute(chunks[k], 'dp', perm))]
    all_to_all x2 -> x0, blocking collectives: 37.8 us -> none  [the longest x1 27.2 us: shards(): lax.all_to_all(outgoing, 'dp', split_axis=0, concat_axis=0, tiled=True)]
    ppermute x3 -> x38, waiting for transfers between devices: 16.5 us -> 22.1 us  [the longest x24 12.5 us: pair_gather(): pieces = pieces + [lax.ppermute(y, 'pair', perm) for y in pieces]]
    unnamed x2 -> x35, local copies, waits for them, and re-layouts: 0.01 us -> 1.62 us
  transfers between devices with their start and end apart: 3 -> 38, of which waited for: 1 -> 20; matrix products, arithmetic and copies ran while one was open for 6% -> 4% of each run, Pallas kernels for 0% -> 0%
where the time goes in v3:
time: 78.6 us; the launch traced here: 78.3 us
  starting transfers between devices  45 us (57%)
  waiting for transfers between devices  22.1 us (28%)
  other arithmetic  4.59 us (6%)
  matrix products  4.02 us (5%)
  local copies, waits for them, and re-layouts  2.31 us (3%)
    ppermute x14, starting transfers between devices, dp_exchange(): out.append(lax.ppermute(chunks[k], 'dp', perm))  34.9 us
    ppermute x24, waiting for transfers between devices, pair_gather(): pieces = pieces + [lax.ppermute(y, 'pair', perm) for y in pieces]  12.5 us
    ppermute x24, starting transfers between devices, pair_gather(): pieces = pieces + [lax.ppermute(y, 'pair', perm) for y in pieces]  10.1 us
    ppermute x14, waiting for transfers between devices, dp_exchange(): out.append(lax.ppermute(chunks[k], 'dp', perm))  9.68 us
    dot_general x4, matrix products, piece_best(): jnp.einsum('id,jd->ij', left, right, preferred_element_type=jnp.float32)  3.58 us
    unnamed x35, local copies, waits for them, and re-layouts  1.62 us
  transfers between devices with their start and end apart: 38, of which 20 were waited for; matrix products, arithmetic and copies ran while one was open for 4% of the time, Pallas kernels for 0%

profile of v3, /device:TPU:0, one launch (start us, length us, event | category | flops | bytes accessed | tf_op | source)
XLA Modules:
  0.0 78.3 jit_solution(17287539471673171388)
XLA Ops:
  0.0 0.6 compare_reduce_fusion
  0.6 0.7 subtract_add_fusion
  1.9 0.7 select_convert_fusion
  2.7 1.2 %multiply_reduce_fusion = f32[128]{0:T(128)S(1)} fusion(f32[128,1024]{1,0:T(8,128)} %param.4), kind=kLoop, calls=%fused_computation.13 | loop fusion | flops 262016 | bytes 524800 | tf_op jit(solution)/shard_map/reduce_sum | solution.py:52
  3.9 0.4 convolution_convert_fusion
  4.5 3.0 %collective-permute-start = (bf16[48,1024]{1,0:T(8,128)(2,1)S(1)}, bf16[48,1024]{1,0:T(8,128)(2,1)S(1)}, u32[]{:S(2)}, u32[]{:S(2)}) collective-permute-start(bf16[48,1024]{1,0:T(8,128)(2,1)S(1)} %get-tuple-element.26), channel_id=1, source_target_pairs={{0,4},{4,8},{8,12},{12,16},{16,20},{20,24},{24,28},{28,0},{1,5},{5... | collective-permute-start | bytes 294920 | tf_op jit(solution)/shard_map/ppermute | solution.py:30
  7.5 1.5 %collective-permute-start.7 = (bf16[48,1024]{1,0:T(8,128)(2,1)S(1)}, bf16[48,1024]{1,0:T(8,128)(2,1)S(1)}, u32[]{:S(2)}, u32[]{:S(2)}) collective-permute-start(bf16[48,1024]{1,0:T(8,128)(2,1)S(1)} %get-tuple-element.19), channel_id=1, source_target_pairs={{0,2},{1,3},{2,0},{3,1},{4,6},{5,7},{6,4},{7,5},{8,10},{9,11},{10,... | collective-permute-start | bytes 294920 | tf_op jit(solution)/shard_map/ppermute | solution.py:39
  9.0 1.6 %collective-permute-start.1 = (bf16[48,1024]{1,0:T(8,128)(2,1)S(1)}, bf16[48,1024]{1,0:T(8,128)(2,1)S(1)}, u32[]{:S(2)}, u32[]{:S(2)}) collective-permute-start(bf16[48,1024]{1,0:T(8,128)(2,1)S(1)} %get-tuple-element.25), channel_id=1, source_target_pairs={{0,8},{4,12},{8,16},{12,20},{16,24},{20,28},{24,0},{28,4},{1,9},{5... | collective-permute-start | bytes 294920 | tf_op jit(solution)/shard_map/ppermute | solution.py:30
  10.6 2.5 %collective-permute-start.2 = (bf16[48,1024]{1,0:T(8,128)(2,1)S(1)}, bf16[48,1024]{1,0:T(8,128)(2,1)S(1)}, u32[]{:S(2)}, u32[]{:S(2)}) collective-permute-start(bf16[48,1024]{1,0:T(8,128)(2,1)S(1)} %get-tuple-element.24), channel_id=1, source_target_pairs={{0,12},{4,16},{8,20},{12,24},{16,28},{20,0},{24,4},{28,8},{1,13},{... | collective-permute-start | bytes 294920 | tf_op jit(solution)/shard_map/ppermute | solution.py:30
  13.4 1.0 %collective-permute-start.3 = (bf16[48,1024]{1,0:T(8,128)(2,1)S(1)}, bf16[48,1024]{1,0:T(8,128)(2,1)S(1)}, u32[]{:S(2)}, u32[]{:S(2)}) collective-permute-start(bf16[48,1024]{1,0:T(8,128)(2,1)S(1)} %get-tuple-element.23), channel_id=1, source_target_pairs={{0,16},{4,20},{8,24},{12,28},{16,0},{20,4},{24,8},{28,12},{1,17},{... | collective-permute-start | bytes 294920 | tf_op jit(solution)/shard_map/ppermute | solution.py:30
  14.4 1.7 %collective-permute-done.1 = bf16[48,1024]{1,0:T(8,128)(2,1)S(1)} collective-permute-done((bf16[48,1024]{1,0:T(8,128)(2,1)S(1)}, bf16[48,1024]{1,0:T(8,128)(2,1)S(1)}, u32[]{:S(2)}, u32[]{:S(2)}) %collective-permute-start.1) | collective-permute-done | bytes 98336 | tf_op jit(solution)/shard_map/ppermute | solution.py:30
  16.1 7.3 %collective-permute-start.4 = (bf16[48,1024]{1,0:T(8,128)(2,1)S(1)}, bf16[48,1024]{1,0:T(8,128)(2,1)S(1)}, u32[]{:S(2)}, u32[]{:S(2)}) collective-permute-start(bf16[48,1024]{1,0:T(8,128)(2,1)S(1)} %get-tuple-element.22), channel_id=1, source_target_pairs={{0,20},{4,24},{8,28},{12,0},{16,4},{20,8},{24,12},{28,16},{1,21},{... | collective-permute-start | bytes 294920 | tf_op jit(solution)/shard_map/ppermute | solution.py:30
  23.5 6.1 %collective-permute-start.5 = (bf16[48,1024]{1,0:T(8,128)(2,1)S(1)}, bf16[48,1024]{1,0:T(8,128)(2,1)S(1)}, u32[]{:S(2)}, u32[]{:S(2)}) collective-permute-start(bf16[48,1024]{1,0:T(8,128)(2,1)S(1)} %get-tuple-element.21), channel_id=1, source_target_pairs={{0,24},{4,28},{8,0},{12,4},{16,8},{20,12},{24,16},{28,20},{1,25},{... | collective-permute-start | bytes 294920 | tf_op jit(solution)/shard_map/ppermute | solution.py:30
  29.6 1.7 %collective-permute-start.6 = (bf16[48,1024]{1,0:T(8,128)(2,1)S(1)}, bf16[48,1024]{1,0:T(8,128)(2,1)S(1)}, u32[]{:S(2)}, u32[]{:S(2)}) collective-permute-start(bf16[48,1024]{1,0:T(8,128)(2,1)S(1)} %get-tuple-element.20), channel_id=1, source_target_pairs={{0,28},{4,0},{8,4},{12,8},{16,12},{20,16},{24,20},{28,24},{1,29},{... | collective-permute-start | bytes 294920 | tf_op jit(solution)/shard_map/ppermute | solution.py:30
  31.4 1.0 %collective-permute-done.5 = bf16[48,1024]{1,0:T(8,128)(2,1)S(1)} collective-permute-done((bf16[48,1024]{1,0:T(8,128)(2,1)S(1)}, bf16[48,1024]{1,0:T(8,128)(2,1)S(1)}, u32[]{:S(2)}, u32[]{:S(2)}) %collective-permute-start.5) | collective-permute-done | bytes 98336 | tf_op jit(solution)/shard_map/ppermute | solution.py:30
  32.4 1.9 %collective-permute-done.6 = bf16[48,1024]{1,0:T(8,128)(2,1)S(1)} collective-permute-done((bf16[48,1024]{1,0:T(8,128)(2,1)S(1)}, bf16[48,1024]{1,0:T(8,128)(2,1)S(1)}, u32[]{:S(2)}, u32[]{:S(2)}) %collective-permute-start.6) | collective-permute-done | bytes 98336 | tf_op jit(solution)/shard_map/ppermute | solution.py:30
  34.4 0.6 fusion
  35.1 0.6 collective-permute-start.8
  35.7 1.5 %collective-permute-start.9 = (bf16[48,1024]{1,0:T(8,128)(2,1)S(1)}, bf16[48,1024]{1,0:T(8,128)(2,1)S(1)}, u32[]{:S(2)}, u32[]{:S(2)}) collective-permute-start(bf16[48,1024]{1,0:T(8,128)(2,1)S(1)} %collective-permute-done.1), channel_id=1, source_target_pairs={{0,2},{1,3},{2,0},{3,1},{4,6},{5,7},{6,4},{7,5},{8,10},{9,11},{10,... | collective-permute-start | bytes 294920 | tf_op jit(solution)/shard_map/ppermute | solution.py:39
  37.1 0.5 collective-permute-start.10
  37.7 1.5 %collective-permute-start.11 = (bf16[48,1024]{1,0:T(8,128)(2,1)S(1)}, bf16[48,1024]{1,0:T(8,128)(2,1)S(1)}, u32[]{:S(2)}, u32[]{:S(2)}) collective-permute-start(bf16[48,1024]{1,0:T(8,128)(2,1)S(1)} %collective-permute-done.3), channel_id=1, source_target_pairs={{0,2},{1,3},{2,0},{3,1},{4,6},{5,7},{6,4},{7,5},{8,10},{9,11},{10,... | collective-permute-start | bytes 294920 | tf_op jit(solution)/shard_map/ppermute | solution.py:39
  39.2 0.5 collective-permute-start.12
  39.7 1.1 %collective-permute-done.8 = bf16[48,1024]{1,0:T(8,128)(2,1)S(1)} collective-permute-done((bf16[48,1024]{1,0:T(8,128)(2,1)S(1)}, bf16[48,1024]{1,0:T(8,128)(2,1)S(1)}, u32[]{:S(2)}, u32[]{:S(2)}) %collective-permute-start.8) | collective-permute-done | bytes 98336 | tf_op jit(solution)/shard_map/ppermute | solution.py:39
  40.9 0.4 collective-permute-start.13
  41.3 1.7 %collective-permute-done.9 = bf16[48,1024]{1,0:T(8,128)(2,1)S(1)} collective-permute-done((bf16[48,1024]{1,0:T(8,128)(2,1)S(1)}, bf16[48,1024]{1,0:T(8,128)(2,1)S(1)}, u32[]{:S(2)}, u32[]{:S(2)}) %collective-permute-start.9) | collective-permute-done | bytes 98336 | tf_op jit(solution)/shard_map/ppermute | solution.py:39
  43.0 0.4 collective-permute-start.14
  43.4 1.7 %collective-permute-done.10 = bf16[48,1024]{1,0:T(8,128)(2,1)S(1)} collective-permute-done((bf16[48,1024]{1,0:T(8,128)(2,1)S(1)}, bf16[48,1024]{1,0:T(8,128)(2,1)S(1)}, u32[]{:S(2)}, u32[]{:S(2)}) %collective-permute-start.10) | collective-permute-done | bytes 98336 | tf_op jit(solution)/shard_map/ppermute | solution.py:39
  45.1 2.1 %collective-permute-done.11 = bf16[48,1024]{1,0:T(8,128)(2,1)S(1)} collective-permute-done((bf16[48,1024]{1,0:T(8,128)(2,1)S(1)}, bf16[48,1024]{1,0:T(8,128)(2,1)S(1)}, u32[]{:S(2)}, u32[]{:S(2)}) %collective-permute-start.11) | collective-permute-done | bytes 98336 | tf_op jit(solution)/shard_map/ppermute | solution.py:39
  47.2 2.1 %collective-permute-done.12 = bf16[48,1024]{1,0:T(8,128)(2,1)S(1)} collective-permute-done((bf16[48,1024]{1,0:T(8,128)(2,1)S(1)}, bf16[48,1024]{1,0:T(8,128)(2,1)S(1)}, u32[]{:S(2)}, u32[]{:S(2)}) %collective-permute-start.12) | collective-permute-done | bytes 98336 | tf_op jit(solution)/shard_map/ppermute | solution.py:39
  49.3 1.1 %collective-permute-done.13 = bf16[48,1024]{1,0:T(8,128)(2,1)S(1)} collective-permute-done((bf16[48,1024]{1,0:T(8,128)(2,1)S(1)}, bf16[48,1024]{1,0:T(8,128)(2,1)S(1)}, u32[]{:S(2)}, u32[]{:S(2)}) %collective-permute-start.13) | collective-permute-done | bytes 98336 | tf_op jit(solution)/shard_map/ppermute | solution.py:39
  50.4 1.0 %collective-permute-done.14 = bf16[48,1024]{1,0:T(8,128)(2,1)S(1)} collective-permute-done((bf16[48,1024]{1,0:T(8,128)(2,1)S(1)}, bf16[48,1024]{1,0:T(8,128)(2,1)S(1)}, u32[]{:S(2)}, u32[]{:S(2)}) %collective-permute-start.14) | collective-permute-done | bytes 98336 | tf_op jit(solution)/shard_map/ppermute | solution.py:39
  51.5 0.6 collective-permute-start.21
  52.1 0.5 collective-permute-start.23
  53.4 1.7 %fusion.1 = f32[384]{0:T(512)S(1)} fusion(bf16[384,1024]{1,0:T(8,128)(2,1)S(1)} %bitcast.102, bf16[384,1024]{1,0:T(8,128)(2,1)} %bitcast.106, s32[384]{0:T(512)S(1)} %reshape.130, s32[384]{0:T(512)S(1)} %reshape.131, pred[384]{0:T(512)(128)(4,1)S(1)} %broadcast_compare_fusion), kind=kOutput, calls=%fused_computation.6 | convolution fusion | flops 302579328 | bytes 1577856 | tf_op jit(solution)/shard_map/id,jd->ij/dot_general | solution.py:13
  55.4 0.4 collective-permute-start.25
  57.8 0.4 collective-permute-done.30
  58.2 0.9 %copy-done.2 = bf16[8,48,1024]{2,1,0:T(8,128)(2,1)} copy-done((bf16[8,48,1024]{2,1,0:T(8,128)(2,1)}, bf16[8,48,1024]{2,1,0:T(8,128)(2,1)S(1)}, u32[]{:S(2)}) %copy-start.2) | copy-done | bytes 786456
  59.3 0.6 fusion.2
  59.9 0.5 copy-done.3
  60.5 0.6 fusion.3
  61.2 5.2 %collective-permute-start.31 = (f32[48]{0:T(128)S(1)}, f32[48]{0:T(128)S(1)}, u32[]{:S(2)}, u32[]{:S(2)}) collective-permute-start(f32[48]{0:T(128)S(1)} %get-tuple-element.34), channel_id=1, source_target_pairs={{0,28},{4,0},{8,4},{12,8},{16,12},{20,16},{24,20},{28,24},{1,29},{... | collective-permute-start | bytes 584 | tf_op jit(solution)/shard_map/ppermute | solution.py:30
  66.4 3.0 %collective-permute-start.34 = (f32[48]{0:T(128)S(1)}, f32[48]{0:T(128)S(1)}, u32[]{:S(2)}, u32[]{:S(2)}) collective-permute-start(f32[48]{0:T(128)S(1)} %get-tuple-element.31), channel_id=1, source_target_pairs={{0,16},{4,20},{8,24},{12,28},{16,0},{20,4},{24,8},{28,12},{1,17},{... | collective-permute-start | bytes 584 | tf_op jit(solution)/shard_map/ppermute | solution.py:30
  69.3 2.0 %collective-permute-start.36 = (f32[48]{0:T(128)S(1)}, f32[48]{0:T(128)S(1)}, u32[]{:S(2)}, u32[]{:S(2)}) collective-permute-start(f32[48]{0:T(128)S(1)} %get-tuple-element.29), channel_id=1, source_target_pairs={{0,8},{4,12},{8,16},{12,20},{16,24},{20,28},{24,0},{28,4},{1,9},{5... | collective-permute-start | bytes 584 | tf_op jit(solution)/shard_map/ppermute | solution.py:30
  71.3 1.5 %collective-permute-start.37 = (f32[48]{0:T(128)S(1)}, f32[48]{0:T(128)S(1)}, u32[]{:S(2)}, u32[]{:S(2)}) collective-permute-start(f32[48]{0:T(128)S(1)} %get-tuple-element.28), channel_id=1, source_target_pairs={{0,4},{4,8},{8,12},{12,16},{16,20},{20,24},{24,28},{28,0},{1,5},{5... | collective-permute-start | bytes 584 | tf_op jit(solution)/shard_map/ppermute | solution.py:30
  72.8 1.9 %collective-permute-done.35 = f32[48]{0:T(128)S(1)} collective-permute-done((f32[48]{0:T(128)S(1)}, f32[48]{0:T(128)S(1)}, u32[]{:S(2)}, u32[]{:S(2)}) %collective-permute-start.35) | collective-permute-done | bytes 224 | tf_op jit(solution)/shard_map/ppermute | solution.py:30
  74.7 1.4 %collective-permute-done.36 = f32[48]{0:T(128)S(1)} collective-permute-done((f32[48]{0:T(128)S(1)}, f32[48]{0:T(128)S(1)}, u32[]{:S(2)}, u32[]{:S(2)}) %collective-permute-start.36) | collective-permute-done | bytes 224 | tf_op jit(solution)/shard_map/ppermute | solution.py:30
  76.1 1.5 %collective-permute-done.37 = f32[48]{0:T(128)S(1)} collective-permute-done((f32[48]{0:T(128)S(1)}, f32[48]{0:T(128)S(1)}, u32[]{:S(2)}, u32[]{:S(2)}) %collective-permute-start.37) | collective-permute-done | bytes 224 | tf_op jit(solution)/shard_map/ppermute | solution.py:30
  77.7 0.7 select_reduce_fusion
  (100 shorter events, 4.9 us)
Async XLA Ops:
  0.0 3.8 %copy-start = (f32[128,1024]{1,0:T(8,128)S(1)}, f32[128,1024]{1,0:T(8,128)}, u32[]{:S(2)}) copy-start(f32[128,1024]{1,0:T(8,128)} %param.4) | copy-start | bytes 1572868
  4.5 8.9 %collective-permute-start = (bf16[48,1024]{1,0:T(8,128)(2,1)S(1)}, bf16[48,1024]{1,0:T(8,128)(2,1)S(1)}, u32[]{:S(2)}, u32[]{:S(2)}) collective-permute-start(bf16[48,1024]{1,0:T(8,128)(2,1)S(1)} %get-tuple-element.26), channel_id=1, source_target_pairs={{0,4},{4,8},{8,12},{12,16},{16,20},{20,24},{24,28},{28,0},{1,5},{5... | collective-permute-start | bytes 294920 | tf_op jit(solution)/shard_map/ppermute | solution.py:30
  7.5 26.9 %collective-permute-start.7 = (bf16[48,1024]{1,0:T(8,128)(2,1)S(1)}, bf16[48,1024]{1,0:T(8,128)(2,1)S(1)}, u32[]{:S(2)}, u32[]{:S(2)}) collective-permute-start(bf16[48,1024]{1,0:T(8,128)(2,1)S(1)} %get-tuple-element.19), channel_id=1, source_target_pairs={{0,2},{1,3},{2,0},{3,1},{4,6},{5,7},{6,4},{7,5},{8,10},{9,11},{10,... | collective-permute-start | bytes 294920 | tf_op jit(solution)/shard_map/ppermute | solution.py:39
  9.0 30.1 %collective-permute-start.15 = (bf16[48,1024]{1,0:T(8,128)(2,1)S(1)}, bf16[48,1024]{1,0:T(8,128)(2,1)S(1)}, u32[]{:S(2)}, u32[]{:S(2)}) collective-permute-start(bf16[48,1024]{1,0:T(8,128)(2,1)S(1)} %get-tuple-element.19), channel_id=1, source_target_pairs={{0,1},{1,0},{2,3},{3,2},{4,5},{5,4},{6,7},{7,6},{8,9},{9,8},{10,11... | collective-permute-start | bytes 294920 | tf_op jit(solution)/shard_map/ppermute | solution.py:39
  9.0 7.1 %collective-permute-start.1 = (bf16[48,1024]{1,0:T(8,128)(2,1)S(1)}, bf16[48,1024]{1,0:T(8,128)(2,1)S(1)}, u32[]{:S(2)}, u32[]{:S(2)}) collective-permute-start(bf16[48,1024]{1,0:T(8,128)(2,1)S(1)} %get-tuple-element.25), channel_id=1, source_target_pairs={{0,8},{4,12},{8,16},{12,20},{16,24},{20,28},{24,0},{28,4},{1,9},{5... | collective-permute-start | bytes 294920 | tf_op jit(solution)/shard_map/ppermute | solution.py:30
  10.6 12.9 %collective-permute-start.2 = (bf16[48,1024]{1,0:T(8,128)(2,1)S(1)}, bf16[48,1024]{1,0:T(8,128)(2,1)S(1)}, u32[]{:S(2)}, u32[]{:S(2)}) collective-permute-start(bf16[48,1024]{1,0:T(8,128)(2,1)S(1)} %get-tuple-element.24), channel_id=1, source_target_pairs={{0,12},{4,16},{8,20},{12,24},{16,28},{20,0},{24,4},{28,8},{1,13},{... | collective-permute-start | bytes 294920 | tf_op jit(solution)/shard_map/ppermute | solution.py:30
  13.4 16.2 %collective-permute-start.3 = (bf16[48,1024]{1,0:T(8,128)(2,1)S(1)}, bf16[48,1024]{1,0:T(8,128)(2,1)S(1)}, u32[]{:S(2)}, u32[]{:S(2)}) collective-permute-start(bf16[48,1024]{1,0:T(8,128)(2,1)S(1)} %get-tuple-element.23), channel_id=1, source_target_pairs={{0,16},{4,20},{8,24},{12,28},{16,0},{20,4},{24,8},{28,12},{1,17},{... | collective-permute-start | bytes 294920 | tf_op jit(solution)/shard_map/ppermute | solution.py:30
  16.1 15.2 %collective-permute-start.4 = (bf16[48,1024]{1,0:T(8,128)(2,1)S(1)}, bf16[48,1024]{1,0:T(8,128)(2,1)S(1)}, u32[]{:S(2)}, u32[]{:S(2)}) collective-permute-start(bf16[48,1024]{1,0:T(8,128)(2,1)S(1)} %get-tuple-element.22), channel_id=1, source_target_pairs={{0,20},{4,24},{8,28},{12,0},{16,4},{20,8},{24,12},{28,16},{1,21},{... | collective-permute-start | bytes 294920 | tf_op jit(solution)/shard_map/ppermute | solution.py:30
  23.5 8.9 %collective-permute-start.5 = (bf16[48,1024]{1,0:T(8,128)(2,1)S(1)}, bf16[48,1024]{1,0:T(8,128)(2,1)S(1)}, u32[]{:S(2)}, u32[]{:S(2)}) collective-permute-start(bf16[48,1024]{1,0:T(8,128)(2,1)S(1)} %get-tuple-element.21), channel_id=1, source_target_pairs={{0,24},{4,28},{8,0},{12,4},{16,8},{20,12},{24,16},{28,20},{1,25},{... | collective-permute-start | bytes 294920 | tf_op jit(solution)/shard_map/ppermute | solution.py:30
  29.6 4.7 %collective-permute-start.6 = (bf16[48,1024]{1,0:T(8,128)(2,1)S(1)}, bf16[48,1024]{1,0:T(8,128)(2,1)S(1)}, u32[]{:S(2)}, u32[]{:S(2)}) collective-permute-start(bf16[48,1024]{1,0:T(8,128)(2,1)S(1)} %get-tuple-element.20), channel_id=1, source_target_pairs={{0,28},{4,0},{8,4},{12,8},{16,12},{20,16},{24,20},{28,24},{1,29},{... | collective-permute-start | bytes 294920 | tf_op jit(solution)/shard_map/ppermute | solution.py:30
  35.1 5.8 %collective-permute-start.8 = (bf16[48,1024]{1,0:T(8,128)(2,1)S(1)}, bf16[48,1024]{1,0:T(8,128)(2,1)S(1)}, u32[]{:S(2)}, u32[]{:S(2)}) collective-permute-start(bf16[48,1024]{1,0:T(8,128)(2,1)S(1)} %collective-permute-done), channel_id=1, source_target_pairs={{0,2},{1,3},{2,0},{3,1},{4,6},{5,7},{6,4},{7,5},{8,10},{9,11},{10,... | collective-permute-start | bytes 294920 | tf_op jit(solution)/shard_map/ppermute | solution.py:39
  35.7 7.3 %collective-permute-start.9 = (bf16[48,1024]{1,0:T(8,128)(2,1)S(1)}, bf16[48,1024]{1,0:T(8,128)(2,1)S(1)}, u32[]{:S(2)}, u32[]{:S(2)}) collective-permute-start(bf16[48,1024]{1,0:T(8,128)(2,1)S(1)} %collective-permute-done.1), channel_id=1, source_target_pairs={{0,2},{1,3},{2,0},{3,1},{4,6},{5,7},{6,4},{7,5},{8,10},{9,11},{10,... | collective-permute-start | bytes 294920 | tf_op jit(solution)/shard_map/ppermute | solution.py:39
  37.1 7.9 %collective-permute-start.10 = (bf16[48,1024]{1,0:T(8,128)(2,1)S(1)}, bf16[48,1024]{1,0:T(8,128)(2,1)S(1)}, u32[]{:S(2)}, u32[]{:S(2)}) collective-permute-start(bf16[48,1024]{1,0:T(8,128)(2,1)S(1)} %collective-permute-done.2), channel_id=1, source_target_pairs={{0,2},{1,3},{2,0},{3,1},{4,6},{5,7},{6,4},{7,5},{8,10},{9,11},{10,... | collective-permute-start | bytes 294920 | tf_op jit(solution)/shard_map/ppermute | solution.py:39
  37.7 9.5 %collective-permute-start.11 = (bf16[48,1024]{1,0:T(8,128)(2,1)S(1)}, bf16[48,1024]{1,0:T(8,128)(2,1)S(1)}, u32[]{:S(2)}, u32[]{:S(2)}) collective-permute-start(bf16[48,1024]{1,0:T(8,128)(2,1)S(1)} %collective-permute-done.3), channel_id=1, source_target_pairs={{0,2},{1,3},{2,0},{3,1},{4,6},{5,7},{6,4},{7,5},{8,10},{9,11},{10,... | collective-permute-start | bytes 294920 | tf_op jit(solution)/shard_map/ppermute | solution.py:39
  39.2 10.1 %collective-permute-start.12 = (bf16[48,1024]{1,0:T(8,128)(2,1)S(1)}, bf16[48,1024]{1,0:T(8,128)(2,1)S(1)}, u32[]{:S(2)}, u32[]{:S(2)}) collective-permute-start(bf16[48,1024]{1,0:T(8,128)(2,1)S(1)} %collective-permute-done.4), channel_id=1, source_target_pairs={{0,2},{1,3},{2,0},{3,1},{4,6},{5,7},{6,4},{7,5},{8,10},{9,11},{10,... | collective-permute-start | bytes 294920 | tf_op jit(solution)/shard_map/ppermute | solution.py:39
  40.9 9.5 %collective-permute-start.13 = (bf16[48,1024]{1,0:T(8,128)(2,1)S(1)}, bf16[48,1024]{1,0:T(8,128)(2,1)S(1)}, u32[]{:S(2)}, u32[]{:S(2)}) collective-permute-start(bf16[48,1024]{1,0:T(8,128)(2,1)S(1)} %collective-permute-done.5), channel_id=1, source_target_pairs={{0,2},{1,3},{2,0},{3,1},{4,6},{5,7},{6,4},{7,5},{8,10},{9,11},{10,... | collective-permute-start | bytes 294920 | tf_op jit(solution)/shard_map/ppermute | solution.py:39
  43.0 8.5 %collective-permute-start.14 = (bf16[48,1024]{1,0:T(8,128)(2,1)S(1)}, bf16[48,1024]{1,0:T(8,128)(2,1)S(1)}, u32[]{:S(2)}, u32[]{:S(2)}) collective-permute-start(bf16[48,1024]{1,0:T(8,128)(2,1)S(1)} %collective-permute-done.6), channel_id=1, source_target_pairs={{0,2},{1,3},{2,0},{3,1},{4,6},{5,7},{6,4},{7,5},{8,10},{9,11},{10,... | collective-permute-start | bytes 294920 | tf_op jit(solution)/shard_map/ppermute | solution.py:39
  45.1 6.4 %collective-permute-start.16 = (bf16[48,1024]{1,0:T(8,128)(2,1)S(1)}, bf16[48,1024]{1,0:T(8,128)(2,1)S(1)}, u32[]{:S(2)}, u32[]{:S(2)}) collective-permute-start(bf16[48,1024]{1,0:T(8,128)(2,1)S(1)} %collective-permute-done), channel_id=1, source_target_pairs={{0,1},{1,0},{2,3},{3,2},{4,5},{5,4},{6,7},{7,6},{8,9},{9,8},{10,11... | collective-permute-start | bytes 294920 | tf_op jit(solution)/shard_map/ppermute | solution.py:39
  47.2 4.9 %collective-permute-start.17 = (bf16[48,1024]{1,0:T(8,128)(2,1)S(1)}, bf16[48,1024]{1,0:T(8,128)(2,1)S(1)}, u32[]{:S(2)}, u32[]{:S(2)}) collective-permute-start(bf16[48,1024]{1,0:T(8,128)(2,1)S(1)} %collective-permute-done.1), channel_id=1, source_target_pairs={{0,1},{1,0},{2,3},{3,2},{4,5},{5,4},{6,7},{7,6},{8,9},{9,8},{10,11... | collective-permute-start | bytes 294920 | tf_op jit(solution)/shard_map/ppermute | solution.py:39
  49.3 2.9 %collective-permute-start.18 = (bf16[48,1024]{1,0:T(8,128)(2,1)S(1)}, bf16[48,1024]{1,0:T(8,128)(2,1)S(1)}, u32[]{:S(2)}, u32[]{:S(2)}) collective-permute-start(bf16[48,1024]{1,0:T(8,128)(2,1)S(1)} %collective-permute-done.2), channel_id=1, source_target_pairs={{0,1},{1,0},{2,3},{3,2},{4,5},{5,4},{6,7},{7,6},{8,9},{9,8},{10,11... | collective-permute-start | bytes 294920 | tf_op jit(solution)/shard_map/ppermute | solution.py:39
  50.4 2.3 %collective-permute-start.19 = (bf16[48,1024]{1,0:T(8,128)(2,1)S(1)}, bf16[48,1024]{1,0:T(8,128)(2,1)S(1)}, u32[]{:S(2)}, u32[]{:S(2)}) collective-permute-start(bf16[48,1024]{1,0:T(8,128)(2,1)S(1)} %collective-permute-done.3), channel_id=1, source_target_pairs={{0,1},{1,0},{2,3},{3,2},{4,5},{5,4},{6,7},{7,6},{8,9},{9,8},{10,11... | collective-permute-start | bytes 294920 | tf_op jit(solution)/shard_map/ppermute | solution.py:39
  51.4 1.3 %collective-permute-start.20 = (bf16[48,1024]{1,0:T(8,128)(2,1)S(1)}, bf16[48,1024]{1,0:T(8,128)(2,1)S(1)}, u32[]{:S(2)}, u32[]{:S(2)}) collective-permute-start(bf16[48,1024]{1,0:T(8,128)(2,1)S(1)} %collective-permute-done.4), channel_id=1, source_target_pairs={{0,1},{1,0},{2,3},{3,2},{4,5},{5,4},{6,7},{7,6},{8,9},{9,8},{10,11... | collective-permute-start | bytes 294920 | tf_op jit(solution)/shard_map/ppermute | solution.py:39
  51.4 1.5 %copy-start.1 = (bf16[8,48,1024]{2,1,0:T(8,128)(2,1)}, bf16[8,48,1024]{2,1,0:T(8,128)(2,1)S(1)}, u32[]{:S(2)}) copy-start(bf16[8,48,1024]{2,1,0:T(8,128)(2,1)S(1)} %bitcast_dynamic-update-slice_fusion.16) | copy-start | bytes 2359300
  51.5 1.5 %collective-permute-start.21 = (bf16[48,1024]{1,0:T(8,128)(2,1)S(1)}, bf16[48,1024]{1,0:T(8,128)(2,1)S(1)}, u32[]{:S(2)}, u32[]{:S(2)}) collective-permute-start(bf16[48,1024]{1,0:T(8,128)(2,1)S(1)} %collective-permute-done.5), channel_id=1, source_target_pairs={{0,1},{1,0},{2,3},{3,2},{4,5},{5,4},{6,7},{7,6},{8,9},{9,8},{10,11... | collective-permute-start | bytes 294920 | tf_op jit(solution)/shard_map/ppermute | solution.py:39
  52.0 1.4 %collective-permute-start.22 = (bf16[48,1024]{1,0:T(8,128)(2,1)S(1)}, bf16[48,1024]{1,0:T(8,128)(2,1)S(1)}, u32[]{:S(2)}, u32[]{:S(2)}) collective-permute-start(bf16[48,1024]{1,0:T(8,128)(2,1)S(1)} %collective-permute-done.6), channel_id=1, source_target_pairs={{0,1},{1,0},{2,3},{3,2},{4,5},{5,4},{6,7},{7,6},{8,9},{9,8},{10,11... | collective-permute-start | bytes 294920 | tf_op jit(solution)/shard_map/ppermute | solution.py:39
  52.1 4.1 %collective-permute-start.23 = (bf16[48,1024]{1,0:T(8,128)(2,1)S(1)}, bf16[48,1024]{1,0:T(8,128)(2,1)S(1)}, u32[]{:S(2)}, u32[]{:S(2)}) collective-permute-start(bf16[48,1024]{1,0:T(8,128)(2,1)S(1)} %collective-permute-done.7), channel_id=1, source_target_pairs={{0,1},{1,0},{2,3},{3,2},{4,5},{5,4},{6,7},{7,6},{8,9},{9,8},{10,11... | collective-permute-start | bytes 294920 | tf_op jit(solution)/shard_map/ppermute | solution.py:39
  55.2 1.4 %collective-permute-start.24 = (bf16[48,1024]{1,0:T(8,128)(2,1)S(1)}, bf16[48,1024]{1,0:T(8,128)(2,1)S(1)}, u32[]{:S(2)}, u32[]{:S(2)}) collective-permute-start(bf16[48,1024]{1,0:T(8,128)(2,1)S(1)} %collective-permute-done.8), channel_id=1, source_target_pairs={{0,1},{1,0},{2,3},{3,2},{4,5},{5,4},{6,7},{7,6},{8,9},{9,8},{10,11... | collective-permute-start | bytes 294920 | tf_op jit(solution)/shard_map/ppermute | solution.py:39
  55.4 1.5 %collective-permute-start.25 = (bf16[48,1024]{1,0:T(8,128)(2,1)S(1)}, bf16[48,1024]{1,0:T(8,128)(2,1)S(1)}, u32[]{:S(2)}, u32[]{:S(2)}) collective-permute-start(bf16[48,1024]{1,0:T(8,128)(2,1)S(1)} %collective-permute-done.9), channel_id=1, source_target_pairs={{0,1},{1,0},{2,3},{3,2},{4,5},{5,4},{6,7},{7,6},{8,9},{9,8},{10,11... | collective-permute-start | bytes 294920 | tf_op jit(solution)/shard_map/ppermute | solution.py:39
  55.7 1.4 %collective-permute-start.26 = (bf16[48,1024]{1,0:T(8,128)(2,1)S(1)}, bf16[48,1024]{1,0:T(8,128)(2,1)S(1)}, u32[]{:S(2)}, u32[]{:S(2)}) collective-permute-start(bf16[48,1024]{1,0:T(8,128)(2,1)S(1)} %collective-permute-done.10), channel_id=1, source_target_pairs={{0,1},{1,0},{2,3},{3,2},{4,5},{5,4},{6,7},{7,6},{8,9},{9,8},{10,11... | collective-permute-start | bytes 294920 | tf_op jit(solution)/shard_map/ppermute | solution.py:39
  55.9 1.3 %collective-permute-start.27 = (bf16[48,1024]{1,0:T(8,128)(2,1)S(1)}, bf16[48,1024]{1,0:T(8,128)(2,1)S(1)}, u32[]{:S(2)}, u32[]{:S(2)}) collective-permute-start(bf16[48,1024]{1,0:T(8,128)(2,1)S(1)} %collective-permute-done.11), channel_id=1, source_target_pairs={{0,1},{1,0},{2,3},{3,2},{4,5},{5,4},{6,7},{7,6},{8,9},{9,8},{10,11... | collective-permute-start | bytes 294920 | tf_op jit(solution)/shard_map/ppermute | solution.py:39
  56.3 1.3 %collective-permute-start.28 = (bf16[48,1024]{1,0:T(8,128)(2,1)S(1)}, bf16[48,1024]{1,0:T(8,128)(2,1)S(1)}, u32[]{:S(2)}, u32[]{:S(2)}) collective-permute-start(bf16[48,1024]{1,0:T(8,128)(2,1)S(1)} %collective-permute-done.12), channel_id=1, source_target_pairs={{0,1},{1,0},{2,3},{3,2},{4,5},{5,4},{6,7},{7,6},{8,9},{9,8},{10,11... | collective-permute-start | bytes 294920 | tf_op jit(solution)/shard_map/ppermute | solution.py:39
  56.5 1.3 %collective-permute-start.29 = (bf16[48,1024]{1,0:T(8,128)(2,1)S(1)}, bf16[48,1024]{1,0:T(8,128)(2,1)S(1)}, u32[]{:S(2)}, u32[]{:S(2)}) collective-permute-start(bf16[48,1024]{1,0:T(8,128)(2,1)S(1)} %collective-permute-done.13), channel_id=1, source_target_pairs={{0,1},{1,0},{2,3},{3,2},{4,5},{5,4},{6,7},{7,6},{8,9},{9,8},{10,11... | collective-permute-start | bytes 294920 | tf_op jit(solution)/shard_map/ppermute | solution.py:39
  56.9 1.4 %collective-permute-start.30 = (bf16[48,1024]{1,0:T(8,128)(2,1)S(1)}, bf16[48,1024]{1,0:T(8,128)(2,1)S(1)}, u32[]{:S(2)}, u32[]{:S(2)}) collective-permute-start(bf16[48,1024]{1,0:T(8,128)(2,1)S(1)} %collective-permute-done.14), channel_id=1, source_target_pairs={{0,1},{1,0},{2,3},{3,2},{4,5},{5,4},{6,7},{7,6},{8,9},{9,8},{10,11... | collective-permute-start | bytes 294920 | tf_op jit(solution)/shard_map/ppermute | solution.py:39
  58.2 0.9 %copy-start.2 = (bf16[8,48,1024]{2,1,0:T(8,128)(2,1)}, bf16[8,48,1024]{2,1,0:T(8,128)(2,1)S(1)}, u32[]{:S(2)}) copy-start(bf16[8,48,1024]{2,1,0:T(8,128)(2,1)S(1)} %bitcast_dynamic-update-slice_fusion) | copy-start | bytes 2359300
  59.3 1.1 %copy-start.3 = (bf16[8,48,1024]{2,1,0:T(8,128)(2,1)S(1)}, bf16[8,48,1024]{2,1,0:T(8,128)(2,1)}, u32[]{:S(2)}) copy-start(bf16[8,48,1024]{2,1,0:T(8,128)(2,1)} %copy-done.2) | copy-start | bytes 2359300
  61.2 8.2 %collective-permute-start.31 = (f32[48]{0:T(128)S(1)}, f32[48]{0:T(128)S(1)}, u32[]{:S(2)}, u32[]{:S(2)}) collective-permute-start(f32[48]{0:T(128)S(1)} %get-tuple-element.34), channel_id=1, source_target_pairs={{0,28},{4,0},{8,4},{12,8},{16,12},{20,16},{24,20},{28,24},{1,29},{... | collective-permute-start | bytes 584 | tf_op jit(solution)/shard_map/ppermute | solution.py:30
  66.4 5.0 %collective-permute-start.32 = (f32[48]{0:T(128)S(1)}, f32[48]{0:T(128)S(1)}, u32[]{:S(2)}, u32[]{:S(2)}) collective-permute-start(f32[48]{0:T(128)S(1)} %get-tuple-element.33), channel_id=1, source_target_pairs={{0,24},{4,28},{8,0},{12,4},{16,8},{20,12},{24,16},{28,20},{1,25},{... | collective-permute-start | bytes 584 | tf_op jit(solution)/shard_map/ppermute | solution.py:30
  66.4 6.4 %collective-permute-start.33 = (f32[48]{0:T(128)S(1)}, f32[48]{0:T(128)S(1)}, u32[]{:S(2)}, u32[]{:S(2)}) collective-permute-start(f32[48]{0:T(128)S(1)} %get-tuple-element.32), channel_id=1, source_target_pairs={{0,20},{4,24},{8,28},{12,0},{16,4},{20,8},{24,12},{28,16},{1,21},{... | collective-permute-start | bytes 584 | tf_op jit(solution)/shard_map/ppermute | solution.py:30
  66.4 6.4 %collective-permute-start.34 = (f32[48]{0:T(128)S(1)}, f32[48]{0:T(128)S(1)}, u32[]{:S(2)}, u32[]{:S(2)}) collective-permute-start(f32[48]{0:T(128)S(1)} %get-tuple-element.31), channel_id=1, source_target_pairs={{0,16},{4,20},{8,24},{12,28},{16,0},{20,4},{24,8},{28,12},{1,17},{... | collective-permute-start | bytes 584 | tf_op jit(solution)/shard_map/ppermute | solution.py:30
  69.3 5.3 %collective-permute-start.35 = (f32[48]{0:T(128)S(1)}, f32[48]{0:T(128)S(1)}, u32[]{:S(2)}, u32[]{:S(2)}) collective-permute-start(f32[48]{0:T(128)S(1)} %get-tuple-element.30), channel_id=1, source_target_pairs={{0,12},{4,16},{8,20},{12,24},{16,28},{20,0},{24,4},{28,8},{1,13},{... | collective-permute-start | bytes 584 | tf_op jit(solution)/shard_map/ppermute | solution.py:30
  69.3 6.7 %collective-permute-start.36 = (f32[48]{0:T(128)S(1)}, f32[48]{0:T(128)S(1)}, u32[]{:S(2)}, u32[]{:S(2)}) collective-permute-start(f32[48]{0:T(128)S(1)} %get-tuple-element.29), channel_id=1, source_target_pairs={{0,8},{4,12},{8,16},{12,20},{16,24},{20,28},{24,0},{28,4},{1,9},{5... | collective-permute-start | bytes 584 | tf_op jit(solution)/shard_map/ppermute | solution.py:30
  71.3 6.2 %collective-permute-start.37 = (f32[48]{0:T(128)S(1)}, f32[48]{0:T(128)S(1)}, u32[]{:S(2)}, u32[]{:S(2)}) collective-permute-start(f32[48]{0:T(128)S(1)} %get-tuple-element.28), channel_id=1, source_target_pairs={{0,4},{4,8},{8,12},{12,16},{16,20},{20,24},{24,28},{28,0},{1,5},{5... | collective-permute-start | bytes 584 | tf_op jit(solution)/shard_map/ppermute | solution.py:30

commit v4 on v2

v4 whole, which is shorter than its diff:
```python
import jax
import jax.numpy as jnp
from jax import lax
from jax.sharding import PartitionSpec as P

CPO = 4


floor_value = -2.0


def same_cluster(left_labels, right_labels, exclude_self):
    same = (left_labels[:, None] == right_labels[None, :]) & (left_labels[:, None] >= 0)
    if exclude_self:
        lane = jnp.arange(left_labels.shape[0], dtype=jnp.int32)
        same = same & (lane[:, None] != lane[None, :])
    return same


def chunk_labels(block, capacity, chunk):
    groups = block.shape[0]
    return block[:, capacity, :chunk].astype(jnp.int32).reshape(groups * chunk)


def pair_gather(x, peers):
    pieces = [x]
    bit = peers // 2
    while bit >= 1:
        perm = [(p, p ^ bit) for p in range(peers)]
        pieces = pieces + [lax.ppermute(y, "pair", perm) for y in pieces]
        bit //= 2
    return pieces


def shards(embeddings, labels):
    rows, width = embeddings.shape
    groups = lax.axis_size("dp")
    peers = lax.axis_size("pair")
    capacity = 5 * rows // (2 * groups)
    chunk = -(-(capacity + 1) // 16) * 16
    slots = groups * chunk
    half = width // 2
    me = lax.axis_index("dp")
    norm = jnp.sqrt(jnp.sum(embeddings * embeddings, axis=1, keepdims=True) + 1e-06)
    unit = (embeddings / norm).astype(jnp.bfloat16)
    owner = labels // CPO
    local = labels - owner * CPO
    onehot = (owner[:, None] == jnp.arange(groups, dtype=jnp.int32)[None, :]).astype(jnp.int32)
    rank = jnp.sum(jnp.cumsum(onehot, axis=0) * onehot, axis=1) - 1
    slot = owner * chunk + rank
    place = slot[None, :] == jnp.arange(slots, dtype=jnp.int32)[:, None]
    outgoing = jnp.dot(place.astype(jnp.bfloat16), unit, preferred_element_type=jnp.float32)
    outgoing = outgoing.astype(jnp.bfloat16).reshape(groups, chunk, width)
    tag = jnp.sum(jnp.where(place, local[None, :] + 1, 0), axis=1) - 1
    tag_row = jnp.full((groups, width), -1, jnp.int32).at[:, :chunk].set(tag.reshape(groups, chunk))
    row_id = jnp.arange(chunk, dtype=jnp.int32)
    outgoing = jnp.where(
        (row_id == capacity)[None, :, None], tag_row.astype(jnp.bfloat16)[:, None, :], outgoing
    )
    score = None
    pieces_labels = None
    for part in range(2):
        sent = outgoing[:, :, part * half:(part + 1) * half]
        block = lax.all_to_all(sent, "dp", split_axis=0, concat_axis=0, tiled=True)
        pieces = pair_gather(block, peers)
        if part == 0:
            pieces_labels = [chunk_labels(x, capacity, chunk) for x in pieces]
        left = block.reshape(slots, half)
        part_score = [
            jnp.einsum(
                "id,jd->ij", left, x.reshape(slots, half), preferred_element_type=jnp.float32
            )
            for x in pieces
        ]
        score = part_score if score is None else [a + b for a, b in zip(score, part_score)]
    best = None
    for index, (piece_score, right_labels) in enumerate(zip(score, pieces_labels)):
        same = same_cluster(pieces_labels[0], right_labels, index == 0)
        piece_max = jnp.max(jnp.where(same, piece_score, floor_value), axis=1)
        best = piece_max if best is None else jnp.maximum(best, piece_max)
    mine = jnp.arange(groups, dtype=jnp.int32)[:, None, None] == me
    contribution = jnp.where(mine, best.reshape(1, groups, chunk), 0.0)
    returned = lax.psum(contribution, "dp")[:, me, :].reshape(slots)
    return jnp.sum(jnp.where(place, returned[:, None], 0.0), axis=0)


def solution(mesh):
    in_specs = (P(("dp", "pair"), None), P(("dp", "pair")))
    out_specs = P(("dp", "pair"))
    return jax.shard_map(shards, mesh=mesh, in_specs=in_specs, out_specs=out_specs, check_vma=False)
```

time: 67.4 us -> 91.9 us (1.36)
  blocking collectives: 37.8 us -> 56.8 us
  starting transfers between devices: 1.5 us -> 7.49 us
  waiting for transfers between devices: 16.5 us -> 14.3 us
  matrix products: 4.04 us -> 5.63 us
  local copies, waits for them, and re-layouts: 1.09 us -> 2.46 us
  other arithmetic: 5.96 us -> 4.67 us
    psum x0 -> x1, blocking collectives: none -> 37.6 us  [shards(): returned = lax.psum(contribution, 'dp')[:, me, :].reshape(slots)]
    all_to_all x2 -> x1, blocking collectives: 37.8 us -> 19.2 us  [shards(): block = lax.all_to_all(sent, 'dp', split_axis=0, concat_axis=0, tiled=True)]
    ppermute x3 -> x6, waiting for transfers between devices: 16.5 us -> 5.04 us  [pair_gather(): pieces = pieces + [lax.ppermute(y, 'pair', perm) for y in pieces]]
    all_to_all x0 -> x1, waiting for transfers between devices: none -> 9.29 us  [shards(): block = lax.all_to_all(sent, 'dp', split_axis=0, concat_axis=0, tiled=True)]
    all_to_all x0 -> x1, starting transfers between devices: none -> 3.45 us  [shards(): block = lax.all_to_all(sent, 'dp', split_axis=0, concat_axis=0, tiled=True)]
    ppermute x3 -> x6, starting transfers between devices: 1.5 us -> 4.04 us  [pair_gather(): pieces = pieces + [lax.ppermute(y, 'pair', perm) for y in pieces]]
    dot_general x4 -> x8, matrix products: 3.6 us -> 5.2 us  [shards(): jnp.einsum('id,jd->ij', left, x.reshape(slots, half), preferred_element_t...]
    unnamed x2 -> x6, local copies, waits for them, and re-layouts: 0.01 us -> 1.04 us
  transfers between devices with their start and end apart: 3 -> 7, of which waited for: 1 -> 3; matrix products, arithmetic and copies ran while one was open for 6% -> 4% of each run, Pallas kernels for 0% -> 0%
where the time goes in v4:
time: 91.9 us; the launch traced here: 91.6 us
  blocking collectives  56.8 us (62%)
  waiting for transfers between devices  14.3 us (16%)
  starting transfers between devices  7.49 us (8%)
  matrix products  5.63 us (6%)
  other arithmetic  4.67 us (5%)
  local copies, waits for them, and re-layouts  2.46 us (3%)
    psum x1, blocking collectives, shards(): returned = lax.psum(contribution, 'dp')[:, me, :].reshape(slots)  37.6 us
    all_to_all x1, blocking collectives, shards(): block = lax.all_to_all(sent, 'dp', split_axis=0, concat_axis=0, tiled=True)  19.2 us
    all_to_all x1, waiting for transfers between devices, shards(): block = lax.all_to_all(sent, 'dp', split_axis=0, concat_axis=0, tiled=True)  9.29 us
    dot_general x8, matrix products, shards(): jnp.einsum('id,jd->ij', left, x.reshape(slots, half), preferred_element_t...  5.2 us
    ppermute x6, waiting for transfers between devices, pair_gather(): pieces = pieces + [lax.ppermute(y, 'pair', perm) for y in pieces]  5.04 us
    ppermute x6, starting transfers between devices, pair_gather(): pieces = pieces + [lax.ppermute(y, 'pair', perm) for y in pieces]  4.04 us
    all_to_all x1, starting transfers between devices, shards(): block = lax.all_to_all(sent, 'dp', split_axis=0, concat_axis=0, tiled=True)  3.45 us
  transfers between devices with their start and end apart: 7, of which 3 were waited for; matrix products, arithmetic and copies ran while one was open for 4% of the time, Pallas kernels for 0%

profile of v4, /device:TPU:0, one launch (start us, length us, event | category | flops | bytes accessed | tf_op | source)
XLA Modules:
  0.0 91.6 jit_solution(16860209761277596025)
XLA Ops:
  0.0 0.6 compare_reduce_fusion
  0.6 1.2 %multiply_reduce_fusion = f32[128]{0:T(128)S(1)} fusion(f32[128,1024]{1,0:T(8,128)} %param.4), kind=kLoop, calls=%fused_computation.17 | loop fusion | flops 262016 | bytes 524800 | tf_op jit(solution)/shard_map/reduce_sum | solution.py:44
  1.8 0.7 subtract_add_fusion
  2.5 0.1 fusion.11
  2.6 0.2 reduce_window_sum.11
  2.8 0.2 select_reduce_fusion.2
  2.9 0.0 copy-done
  3.0 0.4 convolution_convert_fusion
  3.4 0.1 select_reduce_fusion.1
  3.5 0.7 select_convert_fusion
  4.2 0.1 reshape.149
  4.3 0.1 broadcast_select_fusion
  4.4 0.8 fusion.16
  5.3 19.2 %all_to_all.10 = bf16[8,48,512]{2,1,0:T(8,128)(2,1)S(1)} all-to-all(bf16[8,48,512]{2,1,0:T(8,128)(2,1)S(1)} %get-tuple-element.19), channel_id=1, replica_groups=mesh['dp'=8,'pair'=4] {'dp'}, dimensions={0} | all-to-all | bytes 786432 | tf_op jit(solution)/shard_map/all_to_all | solution.py:64
  24.4 3.5 %all-to-all-start.1 = ((bf16[8,48,512]{2,1,0:T(8,128)(2,1)}), bf16[8,48,512]{2,1,0:T(8,128)(2,1)S(1)}, u32[]{:S(2)}, u32[]{:S(2)}) async-start(bf16[8,48,512]{2,1,0:T(8,128)(2,1)} %get-tuple-element.20), calls=%async_computation.1 | async-start | bytes 786432 | tf_op jit(solution)/shard_map/all_to_all | solution.py:64
  27.9 0.1 reshape.159
  28.0 1.5 %collective-permute-start = (bf16[8,48,512]{2,1,0:T(8,128)(2,1)S(1)}, bf16[8,48,512]{2,1,0:T(8,128)(2,1)S(1)}, u32[]{:S(2)}, u32[]{:S(2)}) collective-permute-start(bf16[8,48,512]{2,1,0:T(8,128)(2,1)S(1)} %all_to_all.10), channel_id=1, source_target_pairs={{0,2},{1,3},{2,0},{3,1},{4,6},{5,7},{6,4},{7,5},{8,10},{9,11},{10,... | collective-permute-start | bytes 1179656 | tf_op jit(solution)/shard_map/ppermute | solution.py:30
  29.5 0.4 fusion.17
  29.9 9.3 %all-to-all-done.1 = bf16[8,48,512]{2,1,0:T(8,128)(2,1)S(1)} async-done(((bf16[8,48,512]{2,1,0:T(8,128)(2,1)}), bf16[8,48,512]{2,1,0:T(8,128)(2,1)S(1)}, u32[]{:S(2)}, u32[]{:S(2)}) %all-to-all-start.1) | async-done | bytes 393248 | tf_op jit(solution)/shard_map/all_to_all | solution.py:64
  39.2 1.5 %collective-permute-start.1 = (bf16[8,48,512]{2,1,0:T(8,128)(2,1)S(1)}, bf16[8,48,512]{2,1,0:T(8,128)(2,1)S(1)}, u32[]{:S(2)}, u32[]{:S(2)}) collective-permute-start(bf16[8,48,512]{2,1,0:T(8,128)(2,1)S(1)} %all-to-all-done.1), channel_id=1, source_target_pairs={{0,2},{1,3},{2,0},{3,1},{4,6},{5,7},{6,4},{7,5},{8,10},{9,11},{10,... | collective-permute-start | bytes 1179656 | tf_op jit(solution)/shard_map/ppermute | solution.py:30
  40.7 0.0 collective-permute-start.3
  40.7 0.5 collective-permute-start.2
  41.2 0.4 fusion.4
  41.6 0.8 collective-permute-done.3
  42.4 0.4 fusion.19
  42.8 4.3 %collective-permute-done.1 = bf16[8,48,512]{2,1,0:T(8,128)(2,1)S(1)} collective-permute-done((bf16[8,48,512]{2,1,0:T(8,128)(2,1)S(1)}, bf16[8,48,512]{2,1,0:T(8,128)(2,1)S(1)}, u32[]{:S(2)}, u32[]{:S(2)}) %collective-permute-start.1) | collective-permute-done | bytes 393248 | tf_op jit(solution)/shard_map/ppermute | solution.py:30
  47.1 0.0 collective-permute-start.5
  47.1 0.0 collective-permute-done.2
  47.1 0.4 fusion.18
  47.5 0.0 collective-permute-done
  47.5 0.3 copy-done.1
  47.8 0.1 reshape.161
  47.9 0.1 reshape.160
  48.0 0.5 collective-permute-start.4
  48.5 1.4 %fusion.6 = f32[384]{0:T(512)S(1)} fusion(f32[384,384]{0,1:T(8,128)S(1)} %fusion.19, bf16[384,512]{1,0:T(8,128)(2,1)S(1)} %bitcast.30, bf16[384,512]{1,0:T(8,128)(2,1)} %bitcast.38, s32[384]{0:T(512)S(1)} %reshape.159, s32[384]{0:T(512)S(1)} %reshape.161, pred[384]{0:T(512)(128)(4,1)S(1)} %broadcast_compare_fusion), kind=kOutput, calls=%fused_computation.11 | convolution fusion | flops 151731840 | bytes 1381248 | tf_op jit(solution)/shard_map/id,jd->ij/dot_general | solution.py:70
  49.9 0.4 fusion.5
  50.3 0.0 collective-permute-done.5
  50.3 0.4 fusion.20
  50.7 0.0 collective-permute-done.4
  50.7 0.0 copy-start.2
  50.8 0.7 copy-done.2
  51.5 0.1 reshape.162
  51.6 1.4 %fusion.7 = f32[384]{0:T(512)S(1)} fusion(f32[384,384]{0,1:T(8,128)S(1)} %fusion.20, bf16[384,512]{1,0:T(8,128)(2,1)S(1)} %bitcast.32, bf16[384,512]{1,0:T(8,128)(2,1)} %bitcast.39, s32[384]{0:T(512)S(1)} %reshape.159, s32[384]{0:T(512)S(1)} %reshape.162, pred[384]{0:T(512)(128)(4,1)S(1)} %broadcast_compare_fusion), kind=kOutput, calls=%fused_computation.12 | convolution fusion | flops 151731840 | bytes 1381248 | tf_op jit(solution)/shard_map/id,jd->ij/dot_general | solution.py:70
  53.0 0.1 max.29
  53.1 0.1 broadcast_select_fusion.1
  53.2 37.6 %psum.7 = f32[8,8,48]{2,1,0:T(8,128)S(1)} all-reduce(f32[8,8,48]{2,1,0:T(8,128)S(1)} %broadcast_select_fusion.1), channel_id=1, replica_groups=mesh['dp'=8,'pair'=4] {'dp'}, use_global_device_ids=true, to_apply=%region_9.10 | all-reduce | flops 3072 | bytes 24576 | tf_op jit(solution)/shard_map/psum | solution.py:83
  90.8 0.1 broadcast_in_dim.89
  90.9 0.7 select_reduce_fusion
  (14 shorter events, 0.2 us)
Async XLA Ops:
  0.0 2.9 %copy-start = (f32[128,1024]{1,0:T(8,128)S(1)}, f32[128,1024]{1,0:T(8,128)}, u32[]{:S(2)}) copy-start(f32[128,1024]{1,0:T(8,128)} %param.4) | copy-start | bytes 1572868
  24.4 14.8 %all-to-all-start.1 = ((bf16[8,48,512]{2,1,0:T(8,128)(2,1)}), bf16[8,48,512]{2,1,0:T(8,128)(2,1)S(1)}, u32[]{:S(2)}, u32[]{:S(2)}) async-start(bf16[8,48,512]{2,1,0:T(8,128)(2,1)} %get-tuple-element.20), calls=%async_computation.1 | async-start | bytes 786432 | tf_op jit(solution)/shard_map/all_to_all | solution.py:64
  28.0 19.5 %collective-permute-start = (bf16[8,48,512]{2,1,0:T(8,128)(2,1)S(1)}, bf16[8,48,512]{2,1,0:T(8,128)(2,1)S(1)}, u32[]{:S(2)}, u32[]{:S(2)}) collective-permute-start(bf16[8,48,512]{2,1,0:T(8,128)(2,1)S(1)} %all_to_all.10), channel_id=1, source_target_pairs={{0,2},{1,3},{2,0},{3,1},{4,6},{5,7},{6,4},{7,5},{8,10},{9,11},{10,... | collective-permute-start | bytes 1179656 | tf_op jit(solution)/shard_map/ppermute | solution.py:30
  39.2 7.9 %collective-permute-start.1 = (bf16[8,48,512]{2,1,0:T(8,128)(2,1)S(1)}, bf16[8,48,512]{2,1,0:T(8,128)(2,1)S(1)}, u32[]{:S(2)}, u32[]{:S(2)}) collective-permute-start(bf16[8,48,512]{2,1,0:T(8,128)(2,1)S(1)} %all-to-all-done.1), channel_id=1, source_target_pairs={{0,2},{1,3},{2,0},{3,1},{4,6},{5,7},{6,4},{7,5},{8,10},{9,11},{10,... | collective-permute-start | bytes 1179656 | tf_op jit(solution)/shard_map/ppermute | solution.py:30
  40.7 1.7 %collective-permute-start.3 = (bf16[8,48,512]{2,1,0:T(8,128)(2,1)S(1)}, bf16[8,48,512]{2,1,0:T(8,128)(2,1)S(1)}, u32[]{:S(2)}, u32[]{:S(2)}) collective-permute-start(bf16[8,48,512]{2,1,0:T(8,128)(2,1)S(1)} %all-to-all-done.1), channel_id=1, source_target_pairs={{0,1},{1,0},{2,3},{3,2},{4,5},{5,4},{6,7},{7,6},{8,9},{9,8},{10,11... | collective-permute-start | bytes 1179656 | tf_op jit(solution)/shard_map/ppermute | solution.py:30
  40.7 6.4 %collective-permute-start.2 = (bf16[8,48,512]{2,1,0:T(8,128)(2,1)S(1)}, bf16[8,48,512]{2,1,0:T(8,128)(2,1)S(1)}, u32[]{:S(2)}, u32[]{:S(2)}) collective-permute-start(bf16[8,48,512]{2,1,0:T(8,128)(2,1)S(1)} %all_to_all.10), channel_id=1, source_target_pairs={{0,1},{1,0},{2,3},{3,2},{4,5},{5,4},{6,7},{7,6},{8,9},{9,8},{10,11... | collective-permute-start | bytes 1179656 | tf_op jit(solution)/shard_map/ppermute | solution.py:30
  47.1 3.3 %collective-permute-start.5 = (bf16[8,48,512]{2,1,0:T(8,128)(2,1)S(1)}, bf16[8,48,512]{2,1,0:T(8,128)(2,1)S(1)}, u32[]{:S(2)}, u32[]{:S(2)}) collective-permute-start(bf16[8,48,512]{2,1,0:T(8,128)(2,1)S(1)} %collective-permute-done.1), channel_id=1, source_target_pairs={{0,1},{1,0},{2,3},{3,2},{4,5},{5,4},{6,7},{7,6},{8,9},{9,8},{10,11... | collective-permute-start | bytes 1179656 | tf_op jit(solution)/shard_map/ppermute | solution.py:30
  47.1 0.7 copy-start.1
  48.0 2.8 %collective-permute-start.4 = (bf16[8,48,512]{2,1,0:T(8,128)(2,1)S(1)}, bf16[8,48,512]{2,1,0:T(8,128)(2,1)S(1)}, u32[]{:S(2)}, u32[]{:S(2)}) collective-permute-start(bf16[8,48,512]{2,1,0:T(8,128)(2,1)S(1)} %collective-permute-done), channel_id=1, source_target_pairs={{0,1},{1,0},{2,3},{3,2},{4,5},{5,4},{6,7},{7,6},{8,9},{9,8},{10,11... | collective-permute-start | bytes 1179656 | tf_op jit(solution)/shard_map/ppermute | solution.py:30
  50.7 0.7 copy-start.2

commit v5 on v4

--- a/solution.py
+++ b/solution.py
@@ -39,8 +39,7 @@
     capacity = 5 * rows // (2 * groups)
     chunk = -(-(capacity + 1) // 16) * 16
     slots = groups * chunk
-    half = width // 2
-    me = lax.axis_index("dp")
+    bounds = (0, 3 * width // 4, width) if groups <= 16 else (0, width)
     norm = jnp.sqrt(jnp.sum(embeddings * embeddings, axis=1, keepdims=True) + 1e-06)
     unit = (embeddings / norm).astype(jnp.bfloat16)
     owner = labels // CPO
@@ -59,16 +58,20 @@
     )
     score = None
     pieces_labels = None
-    for part in range(2):
-        sent = outgoing[:, :, part * half:(part + 1) * half]
+    block = None
+    for part in range(len(bounds) - 1):
+        start, stop = bounds[part], bounds[part + 1]
+        sent = outgoing[:, :, start:stop]
+        if block is not None:
+            sent, block = lax.optimization_barrier((sent, block))
         block = lax.all_to_all(sent, "dp", split_axis=0, concat_axis=0, tiled=True)
         pieces = pair_gather(block, peers)
         if part == 0:
             pieces_labels = [chunk_labels(x, capacity, chunk) for x in pieces]
-        left = block.reshape(slots, half)
+        left = block.reshape(slots, stop - start)
         part_score = [
             jnp.einsum(
-                "id,jd->ij", left, x.reshape(slots, half), preferred_element_type=jnp.float32
+                "id,jd->ij", left, x.reshape(slots, stop - start), preferred_element_type=jnp.float32
             )
             for x in pieces
         ]
@@ -78,9 +81,9 @@
         same = same_cluster(pieces_labels[0], right_labels, index == 0)
         piece_max = jnp.max(jnp.where(same, piece_score, floor_value), axis=1)
         best = piece_max if best is None else jnp.maximum(best, piece_max)
-    mine = jnp.arange(groups, dtype=jnp.int32)[:, None, None] == me
-    contribution = jnp.where(mine, best.reshape(1, groups, chunk), 0.0)
-    returned = lax.psum(contribution, "dp")[:, me, :].reshape(slots)
+    returned = lax.all_to_all(
+        best.reshape(groups, chunk), "dp", split_axis=0, concat_axis=0, tiled=True
+    ).reshape(slots)
     return jnp.sum(jnp.where(place, returned[:, None], 0.0), axis=0)
 
 

time: 91.9 us -> 72.9 us (0.79)
  blocking collectives: 56.8 us -> 12 us
  waiting for transfers between devices: 14.3 us -> 30.5 us
  starting transfers between devices: 7.49 us -> 14.5 us
  other arithmetic: 4.67 us -> 5.96 us
  local copies, waits for them, and re-layouts: 2.46 us -> 3.45 us
    psum x1 -> x0, blocking collectives: 37.6 us -> none  [shards(): returned = lax.psum(contribution, 'dp')[:, me, :].reshape(slots)]
    all_to_all x1 -> x2, waiting for transfers between devices: 9.29 us -> 21.7 us  [shards(): block = lax.all_to_all(sent, 'dp', split_axis=0, concat_axis=0, tiled=True)]
    all_to_all x1 -> x2, starting transfers between devices: 3.45 us -> 10.9 us  [shards(): block = lax.all_to_all(sent, 'dp', split_axis=0, concat_axis=0, tiled=True)]
    all_to_all x1, blocking collectives: 19.2 us -> 12 us  [shards(): lax.all_to_all(best.reshape(groups, chunk), 'dp', split_axis=0, concat_ax...]
    ppermute x6, waiting for transfers between devices: 5.04 us -> 8.81 us  [pair_gather(): pieces = pieces + [lax.ppermute(y, 'pair', perm) for y in pieces]]
  transfers between devices with their start and end apart: 7 -> 8, of which waited for: 3 -> 3; matrix products, arithmetic and copies ran while one was open for 4% -> 8% of each run, Pallas kernels for 0% -> 0%
where the time goes in v5:
time: 72.9 us; the launch traced here: 72.3 us
  waiting for transfers between devices  30.5 us (42%)
  starting transfers between devices  14.5 us (20%)
  blocking collectives  12 us (16%)
  other arithmetic  5.96 us (8%)
  matrix products  5.79 us (8%)
  local copies, waits for them, and re-layouts  3.45 us (5%)
    all_to_all x2, waiting for transfers between devices, shards(): block = lax.all_to_all(sent, 'dp', split_axis=0, concat_axis=0, tiled=True)  21.7 us
    all_to_all x1, blocking collectives, shards(): lax.all_to_all(best.reshape(groups, chunk), 'dp', split_axis=0, concat_ax...  12 us
    all_to_all x2, starting transfers between devices, shards(): block = lax.all_to_all(sent, 'dp', split_axis=0, concat_axis=0, tiled=True)  10.9 us
    ppermute x6, waiting for transfers between devices, pair_gather(): pieces = pieces + [lax.ppermute(y, 'pair', perm) for y in pieces]  8.81 us
    dot_general x8, matrix products, shards(): jnp.einsum('id,jd->ij', left, x.reshape(slots, stop - start), preferred_e...  5.35 us
    ppermute x6, starting transfers between devices, pair_gather(): pieces = pieces + [lax.ppermute(y, 'pair', perm) for y in pieces]  3.6 us
    slice x2, local copies, waits for them, and re-layouts, shards(): sent = outgoing[:, :, start:stop]  1.56 us
  transfers between devices with their start and end apart: 8, of which 3 were waited for; matrix products, arithmetic and copies ran while one was open for 8% of the time, Pallas kernels for 0%

profile of v5, /device:TPU:0, one launch (start us, length us, event | category | flops | bytes accessed | tf_op | source)
XLA Modules:
  0.0 72.3 jit_solution(13101105456044359398)
XLA Ops:
  0.0 0.6 compare_reduce_fusion
  0.6 1.2 %multiply_reduce_fusion = f32[128]{0:T(128)S(1)} fusion(f32[128,1024]{1,0:T(8,128)} %param.4), kind=kLoop, calls=%fused_computation.17 | loop fusion | flops 262016 | bytes 524800 | tf_op jit(solution)/shard_map/reduce_sum | solution.py:43
  1.8 0.7 subtract_add_fusion
  2.5 0.1 fusion.11
  2.6 0.2 reduce_window_sum.11
  2.8 0.2 select_reduce_fusion.2
  3.0 0.4 convolution_convert_fusion
  3.4 0.1 select_reduce_fusion.1
  3.5 0.7 select_convert_fusion
  4.2 0.1 reshape.169
  4.3 0.1 broadcast_select_fusion
  4.4 0.9 %slice.40 = bf16[8,48,768]{2,1,0:T(8,128)(2,1)} slice(bf16[8,48,1024]{2,1,0:T(8,128)(2,1)S(1)} %broadcast_select_fusion), slice={[0:8], [0:48], [0:768]} | slice | bytes 1179648 | tf_op jit(solution)/shard_map/slice | solution.py:64
  5.3 7.3 %all-to-all-start = ((bf16[8,48,768]{2,1,0:T(8,128)(2,1)}), bf16[8,48,768]{2,1,0:T(8,128)(2,1)S(1)}, u32[]{:S(2)}, u32[]{:S(2)}) async-start(bf16[8,48,768]{2,1,0:T(8,128)(2,1)} %slice.40), calls=%async_computation | async-start | bytes 1179648 | tf_op jit(solution)/shard_map/all_to_all | solution.py:67
  12.6 0.7 slice.42
  13.3 15.2 %all-to-all-done = bf16[8,48,768]{2,1,0:T(8,128)(2,1)S(1)} async-done(((bf16[8,48,768]{2,1,0:T(8,128)(2,1)}), bf16[8,48,768]{2,1,0:T(8,128)(2,1)S(1)}, u32[]{:S(2)}, u32[]{:S(2)}) %all-to-all-start) | async-done | bytes 589856 | tf_op jit(solution)/shard_map/all_to_all | solution.py:67
  28.5 3.6 %all-to-all-start.1 = ((bf16[8,48,256]{2,1,0:T(8,128)(2,1)}), bf16[8,48,256]{2,1,0:T(8,128)(2,1)S(1)}, u32[]{:S(2)}, u32[]{:S(2)}) async-start(bf16[8,48,256]{2,1,0:T(8,128)(2,1)} %slice.42), calls=%async_computation.1 | async-start | bytes 393216 | tf_op jit(solution)/shard_map/all_to_all | solution.py:67
  32.1 0.1 reshape.179
  32.2 1.5 %collective-permute-start = (bf16[8,48,768]{2,1,0:T(8,128)(2,1)S(1)}, bf16[8,48,768]{2,1,0:T(8,128)(2,1)S(1)}, u32[]{:S(2)}, u32[]{:S(2)}) collective-permute-start(bf16[8,48,768]{2,1,0:T(8,128)(2,1)S(1)} %all-to-all-done), channel_id=1, source_target_pairs={{0,2},{1,3},{2,0},{3,1},{4,6},{5,7},{6,4},{7,5},{8,10},{9,11},{10,... | collective-permute-start | bytes 1769480 | tf_op jit(solution)/shard_map/ppermute | solution.py:30
  33.7 0.0 collective-permute-start.2
  33.7 6.5 %all-to-all-done.1 = bf16[8,48,256]{2,1,0:T(8,128)(2,1)S(1)} async-done(((bf16[8,48,256]{2,1,0:T(8,128)(2,1)}), bf16[8,48,256]{2,1,0:T(8,128)(2,1)S(1)}, u32[]{:S(2)}, u32[]{:S(2)}) %all-to-all-start.1) | async-done | bytes 196640 | tf_op jit(solution)/shard_map/all_to_all | solution.py:67
  40.2 0.3 fusion.16
  40.5 1.6 %collective-permute-start.1 = (bf16[8,48,256]{2,1,0:T(8,128)(2,1)S(1)}, bf16[8,48,256]{2,1,0:T(8,128)(2,1)S(1)}, u32[]{:S(2)}, u32[]{:S(2)}) collective-permute-start(bf16[8,48,256]{2,1,0:T(8,128)(2,1)S(1)} %all-to-all-done.1), channel_id=1, source_target_pairs={{0,2},{1,3},{2,0},{3,1},{4,6},{5,7},{6,4},{7,5},{8,10},{9,11},{10,... | collective-permute-start | bytes 589832 | tf_op jit(solution)/shard_map/ppermute | solution.py:30
  42.1 0.0 collective-permute-start.3
  42.1 0.5 fusion.7
  42.6 8.8 %collective-permute-done.1 = bf16[8,48,256]{2,1,0:T(8,128)(2,1)S(1)} collective-permute-done((bf16[8,48,256]{2,1,0:T(8,128)(2,1)S(1)}, bf16[8,48,256]{2,1,0:T(8,128)(2,1)S(1)}, u32[]{:S(2)}, u32[]{:S(2)}) %collective-permute-start.1) | collective-permute-done | bytes 196640 | tf_op jit(solution)/shard_map/ppermute | solution.py:30
  51.4 0.0 collective-permute-start.5
  51.4 0.0 collective-permute-done.3
  51.4 0.3 fusion.18
  51.7 0.3 fusion.17
  52.0 0.0 collective-permute-done.2
  52.0 0.7 %fusion.13 = s32[8,48]{1,0:T(8,128)S(1)} fusion(bf16[8,48,768]{2,1,0:T(8,128)(2,1)} %collective-permute-done.2), kind=kLoop, calls=%fused_computation.29 | loop fusion | flops 384 | bytes 2304 | tf_op jit(solution)/shard_map/convert_element_type | solution.py:22
  52.8 0.1 reshape.181
  52.9 0.1 reshape.180
  52.9 0.5 collective-permute-start.4
  53.5 1.6 %fusion.5 = f32[384]{0:T(512)S(1)} fusion(f32[384,384]{0,1:T(8,128)S(1)} %fusion.18, bf16[384,768]{1,0:T(8,128)(2,1)S(1)} %bitcast.31, bf16[384,768]{1,0:T(8,128)(2,1)} %bitcast.5, s32[384]{0:T(512)S(1)} %reshape.179, s32[384]{0:T(512)S(1)} %reshape.181, pred[384]{0:T(512)(128)(4,1)S(1)} %broadcast_compare_fusion), kind=kOutput, calls=%fused_computation.10 | convolution fusion | flops 227229312 | bytes 1774464 | tf_op jit(solution)/shard_map/id,jd->ij/dot_general | solution.py:73
  55.0 0.5 fusion.6
  55.6 0.0 collective-permute-done.5
  55.6 0.3 fusion.19
  55.9 0.0 collective-permute-done.4
  55.9 0.8 %copy-done.1 = bf16[8,48,768]{2,1,0:T(8,128)(2,1)} copy-done((bf16[8,48,768]{2,1,0:T(8,128)(2,1)}, bf16[8,48,768]{2,1,0:T(8,128)(2,1)S(1)}, u32[]{:S(2)}) %copy-start.1) | copy-done | bytes 589848
  56.7 0.1 reshape.182
  56.8 1.6 %fusion.4 = f32[384]{0:T(512)S(1)} fusion(f32[384,384]{0,1:T(8,128)S(1)} %fusion.19, bf16[384,768]{1,0:T(8,128)(2,1)S(1)} %bitcast.33, bf16[384,768]{1,0:T(8,128)(2,1)} %bitcast.38, s32[384]{0:T(512)S(1)} %reshape.179, s32[384]{0:T(512)S(1)} %reshape.182, pred[384]{0:T(512)(128)(4,1)S(1)} %broadcast_compare_fusion), kind=kOutput, calls=%fused_computation.9 | convolution fusion | flops 227229312 | bytes 1774464 | tf_op jit(solution)/shard_map/id,jd->ij/dot_general | solution.py:73
  58.4 0.1 max.41
  58.5 12.0 %all_to_all.16 = f32[8,1,48]{2,1,0:T(1,128)S(1)} all-to-all(f32[8,1,48]{2,1,0:T(1,128)S(1)} %max.41), channel_id=1, replica_groups=mesh['dp'=8,'pair'=4] {'dp'}, dimensions={0} | all-to-all | bytes 3072 | tf_op jit(solution)/shard_map/all_to_all | solution.py:84
  70.4 0.5 broadcast.104
  71.0 0.7 reduce.27
  71.6 0.1 broadcast_in_dim.65
  71.7 0.7 select_reduce_fusion
  (13 shorter events, 0.1 us)
Async XLA Ops:
  0.0 2.9 %copy-start = (f32[128,1024]{1,0:T(8,128)S(1)}, f32[128,1024]{1,0:T(8,128)}, u32[]{:S(2)}) copy-start(f32[128,1024]{1,0:T(8,128)} %param.4) | copy-start | bytes 1572868
  5.3 23.2 %all-to-all-start = ((bf16[8,48,768]{2,1,0:T(8,128)(2,1)}), bf16[8,48,768]{2,1,0:T(8,128)(2,1)S(1)}, u32[]{:S(2)}, u32[]{:S(2)}) async-start(bf16[8,48,768]{2,1,0:T(8,128)(2,1)} %slice.40), calls=%async_computation | async-start | bytes 1179648 | tf_op jit(solution)/shard_map/all_to_all | solution.py:67
  28.5 11.8 %all-to-all-start.1 = ((bf16[8,48,256]{2,1,0:T(8,128)(2,1)}), bf16[8,48,256]{2,1,0:T(8,128)(2,1)S(1)}, u32[]{:S(2)}, u32[]{:S(2)}) async-start(bf16[8,48,256]{2,1,0:T(8,128)(2,1)} %slice.42), calls=%async_computation.1 | async-start | bytes 393216 | tf_op jit(solution)/shard_map/all_to_all | solution.py:67
  32.2 20.6 %collective-permute-start = (bf16[8,48,768]{2,1,0:T(8,128)(2,1)S(1)}, bf16[8,48,768]{2,1,0:T(8,128)(2,1)S(1)}, u32[]{:S(2)}, u32[]{:S(2)}) collective-permute-start(bf16[8,48,768]{2,1,0:T(8,128)(2,1)S(1)} %all-to-all-done), channel_id=1, source_target_pairs={{0,2},{1,3},{2,0},{3,1},{4,6},{5,7},{6,4},{7,5},{8,10},{9,11},{10,... | collective-permute-start | bytes 1769480 | tf_op jit(solution)/shard_map/ppermute | solution.py:30
  33.7 18.3 %collective-permute-start.2 = (bf16[8,48,768]{2,1,0:T(8,128)(2,1)S(1)}, bf16[8,48,768]{2,1,0:T(8,128)(2,1)}, u32[]{:S(2)}, u32[]{:S(2)}) collective-permute-start(bf16[8,48,768]{2,1,0:T(8,128)(2,1)S(1)} %all-to-all-done), channel_id=1, source_target_pairs={{0,1},{1,0},{2,3},{3,2},{4,5},{5,4},{6,7},{7,6},{8,9},{9,8},{10,11... | collective-permute-start | bytes 1769480 | tf_op jit(solution)/shard_map/ppermute | solution.py:30
  40.5 10.9 %collective-permute-start.1 = (bf16[8,48,256]{2,1,0:T(8,128)(2,1)S(1)}, bf16[8,48,256]{2,1,0:T(8,128)(2,1)S(1)}, u32[]{:S(2)}, u32[]{:S(2)}) collective-permute-start(bf16[8,48,256]{2,1,0:T(8,128)(2,1)S(1)} %all-to-all-done.1), channel_id=1, source_target_pairs={{0,2},{1,3},{2,0},{3,1},{4,6},{5,7},{6,4},{7,5},{8,10},{9,11},{10,... | collective-permute-start | bytes 589832 | tf_op jit(solution)/shard_map/ppermute | solution.py:30
  42.1 9.3 %collective-permute-start.3 = (bf16[8,48,256]{2,1,0:T(8,128)(2,1)S(1)}, bf16[8,48,256]{2,1,0:T(8,128)(2,1)S(1)}, u32[]{:S(2)}, u32[]{:S(2)}) collective-permute-start(bf16[8,48,256]{2,1,0:T(8,128)(2,1)S(1)} %all-to-all-done.1), channel_id=1, source_target_pairs={{0,1},{1,0},{2,3},{3,2},{4,5},{5,4},{6,7},{7,6},{8,9},{9,8},{10,11... | collective-permute-start | bytes 589832 | tf_op jit(solution)/shard_map/ppermute | solution.py:30
  51.4 4.2 %collective-permute-start.5 = (bf16[8,48,256]{2,1,0:T(8,128)(2,1)S(1)}, bf16[8,48,256]{2,1,0:T(8,128)(2,1)S(1)}, u32[]{:S(2)}, u32[]{:S(2)}) collective-permute-start(bf16[8,48,256]{2,1,0:T(8,128)(2,1)S(1)} %collective-permute-done.1), channel_id=1, source_target_pairs={{0,1},{1,0},{2,3},{3,2},{4,5},{5,4},{6,7},{7,6},{8,9},{9,8},{10,11... | collective-permute-start | bytes 589832 | tf_op jit(solution)/shard_map/ppermute | solution.py:30
  52.9 2.9 %collective-permute-start.4 = (bf16[8,48,768]{2,1,0:T(8,128)(2,1)S(1)}, bf16[8,48,768]{2,1,0:T(8,128)(2,1)S(1)}, u32[]{:S(2)}, u32[]{:S(2)}) collective-permute-start(bf16[8,48,768]{2,1,0:T(8,128)(2,1)S(1)} %collective-permute-done), channel_id=1, source_target_pairs={{0,1},{1,0},{2,3},{3,2},{4,5},{5,4},{6,7},{7,6},{8,9},{9,8},{10,11... | collective-permute-start | bytes 1769480 | tf_op jit(solution)/shard_map/ppermute | solution.py:30
  55.9 0.8 %copy-start.1 = (bf16[8,48,768]{2,1,0:T(8,128)(2,1)}, bf16[8,48,768]{2,1,0:T(8,128)(2,1)S(1)}, u32[]{:S(2)}) copy-start(bf16[8,48,768]{2,1,0:T(8,128)(2,1)S(1)} %collective-permute-done.4) | copy-start | bytes 1769476

commit v6 on v2

--- a/solution.py
+++ b/solution.py
@@ -32,8 +32,8 @@
     slots = groups * chunk
     norm = jnp.sqrt(jnp.sum(embeddings * embeddings, axis=1, keepdims=True) + 1e-06)
     unit = (embeddings / norm).astype(jnp.bfloat16)
-    owner = labels // CPO
-    local = labels - owner * CPO
+    owner = lax.shift_right_logical(labels, CPO.bit_length() - 1)
+    local = jnp.bitwise_and(labels, CPO - 1)
     onehot = (owner[:, None] == jnp.arange(groups, dtype=jnp.int32)[None, :]).astype(jnp.int32)
     rank = jnp.sum(jnp.cumsum(onehot, axis=0) * onehot, axis=1) - 1
     slot = owner * chunk + rank
@@ -41,32 +41,45 @@
     outgoing = jnp.dot(place.astype(jnp.bfloat16), unit, preferred_element_type=jnp.float32)
     outgoing = outgoing.astype(jnp.bfloat16).reshape(groups, chunk, width)
     tag = jnp.sum(jnp.where(place, local[None, :] + 1, 0), axis=1) - 1
-    tag_row = jnp.full((groups, width), -1, jnp.int32).at[:, :chunk].set(tag.reshape(groups, chunk))
+    tag_row = jnp.pad(tag.reshape(groups, chunk), ((0, 0), (0, width - chunk)), constant_values=-1)
     row_id = jnp.arange(chunk, dtype=jnp.int32)
     outgoing = jnp.where(
         (row_id == capacity)[None, :, None], tag_row.astype(jnp.bfloat16)[:, None, :], outgoing
     )
     block = lax.all_to_all(outgoing, "dp", split_axis=0, concat_axis=0, tiled=True)
-    pieces = [block]
-    bit = peers // 2
-    while bit >= 1:
-        perm = [(p, p ^ bit) for p in range(peers)]
-        pieces = pieces + [lax.ppermute(x, "pair", perm) for x in pieces]
-        bit //= 2
+    top = peers // 2
+    far = lax.ppermute(block, "pair", [(p, p ^ top) for p in range(peers)]) if top else None
     left = block.reshape(slots, width)
     left_labels = chunk_labels(block, capacity, chunk)
-    best = None
-    for index, piece in enumerate(pieces):
-        piece_max = piece_best(
-            left,
-            left_labels,
-            piece.reshape(slots, width),
-            chunk_labels(piece, capacity, chunk),
-            index == 0,
-        )
-        best = piece_max if best is None else jnp.maximum(best, piece_max)
+
+    def spread(x):
+        pieces = [x]
+        bit = top // 2
+        while bit >= 1:
+            perm = [(p, p ^ bit) for p in range(peers)]
+            pieces = pieces + [lax.ppermute(y, "pair", perm) for y in pieces]
+            bit //= 2
+        return pieces
+
+    def best_over(pieces, first_is_own):
+        best = None
+        for index, piece in enumerate(pieces):
+            piece_max = piece_best(
+                left,
+                left_labels,
+                piece.reshape(slots, width),
+                chunk_labels(piece, capacity, chunk),
+                first_is_own and index == 0,
+            )
+            best = piece_max if best is None else jnp.maximum(best, piece_max)
+        return best
+
+    best = best_over(spread(block), True)
+    if far is not None:
+        far, best = lax.optimization_barrier((far, best))
+        best = jnp.maximum(best, best_over(spread(far), False))
     returned = lax.all_to_all(
-        best.reshape(groups, chunk), "dp", split_axis=0, concat_axis=0, tiled=True
+        best.reshape(groups, 1, chunk), "dp", split_axis=0, concat_axis=0, tiled=True
     ).reshape(slots)
     return jnp.sum(jnp.where(place, returned[:, None], 0.0), axis=0)
 

time: 67.4 us -> 66.2 us (0.982)
  waiting for transfers between devices: 16.5 us -> 18.6 us
  other arithmetic: 5.96 us -> 4.68 us
  matrix products: 4.04 us -> 2.88 us
  blocking collectives: 37.8 us -> 37.1 us
    ppermute x3, waiting for transfers between devices: 16.5 us -> 18.6 us  [the longest x1 16.9 us: shards(): lax.ppermute(block, 'pair', [(p, p ^ top) for p in range(peers)])]
    another operation x2 -> x1, other arithmetic: 1.3 us -> 0.01 us
    dot_general x4, matrix products: 3.6 us -> 2.44 us  [piece_best(): jnp.einsum('id,jd->ij', left, right, preferred_element_type=jnp.float32)]
    all_to_all x1, blocking collectives: 10.6 us -> 9.84 us  [shards(): lax.all_to_all(best.reshape(groups, 1, chunk), 'dp', split_axis=0, concat...]
    convert_element_type x4, other arithmetic: 0.79 us -> 0.08 us  [chunk_labels(): return block[:, capacity, :chunk].astype(jnp.int32).reshape(groups * chunk)]
    shift_right_logical x0 -> x1, other arithmetic: none -> 0.71 us  [shards(): owner = lax.shift_right_logical(labels, CPO.bit_length() - 1)]
  transfers between devices with their start and end apart: 3 -> 3, of which waited for: 1 -> 3; matrix products, arithmetic and copies ran while one was open for 6% -> 3% of each run, Pallas kernels for 0% -> 0%
where the time goes in v6:
time: 66.2 us; the launch traced here: 65.9 us
  blocking collectives  37.1 us (56%)
  waiting for transfers between devices  18.6 us (28%)
  other arithmetic  4.68 us (7%)
  matrix products  2.88 us (4%)
  starting transfers between devices  1.5 us (2%)
  local copies, waits for them, and re-layouts  1.09 us (2%)
    all_to_all x1, blocking collectives, shards(): lax.all_to_all(outgoing, 'dp', split_axis=0, concat_axis=0, tiled=True)  27.2 us
    ppermute x1, waiting for transfers between devices, shards(): lax.ppermute(block, 'pair', [(p, p ^ top) for p in range(peers)])  16.9 us
    all_to_all x1, blocking collectives, shards(): lax.all_to_all(best.reshape(groups, 1, chunk), 'dp', split_axis=0, concat...  9.84 us
    dot_general x4, matrix products, piece_best(): jnp.einsum('id,jd->ij', left, right, preferred_element_type=jnp.float32)  2.44 us
    ppermute x2, waiting for transfers between devices, spread(): pieces = pieces + [lax.ppermute(y, 'pair', perm) for y in pieces]  1.63 us
    ppermute x1, starting transfers between devices, shards(): lax.ppermute(block, 'pair', [(p, p ^ top) for p in range(peers)])  1.49 us
  transfers between devices with their start and end apart: 3, of which 3 were waited for; matrix products, arithmetic and copies ran while one was open for 3% of the time, Pallas kernels for 0%

profile of v6, /device:TPU:0, one launch (start us, length us, event | category | flops | bytes accessed | tf_op | source)
XLA Modules:
  0.0 65.9 jit_solution(17126854907581820384)
XLA Ops:
  0.0 0.0 copy-start
  0.0 0.7 %broadcast_shift-right-logical_fusion = s32[128]{0:T(128)S(1)} fusion(s32[128]{0:T(128)} %param.3), kind=kLoop, calls=%fused_computation.36 | loop fusion | flops 128 | bytes 1024 | tf_op jit(solution)/shard_map/shift_right_logical | solution.py:35
  0.7 0.1 fusion.7
  0.8 0.2 reduce_window_sum.11
  1.0 0.2 select_reduce_fusion.2
  1.2 0.7 %and_add_fusion = (s32[128]{0:T(128)S(1)}, s32[128]{0:T(128)S(1)}) fusion(s32[128]{0:T(128)} %param.3, s32[128]{0:T(128)S(1)} %select_reduce_fusion.2), kind=kLoop, calls=%fused_computation.33 | loop fusion | flops 768 | bytes 2048 | tf_op jit(solution)/shard_map/add | solution.py:43
  1.8 0.1 select_reduce_fusion.1
  2.0 0.1 sub.12
  2.1 1.2 %multiply_reduce_fusion = f32[128]{0:T(128)S(1)} fusion(f32[128,1024]{1,0:T(8,128)} %param.2), kind=kLoop, calls=%fused_computation.13 | loop fusion | flops 262016 | bytes 524800 | tf_op jit(solution)/shard_map/reduce_sum | solution.py:33
  3.3 0.0 copy-done
  3.3 0.4 convolution_convert_fusion
  3.7 0.1 broadcast_select_fusion
  3.8 27.2 %all_to_all.10 = bf16[8,48,1024]{2,1,0:T(8,128)(2,1)S(1)} all-to-all(bf16[8,48,1024]{2,1,0:T(8,128)(2,1)S(1)} %broadcast_select_fusion), channel_id=1, replica_groups=mesh['dp'=8,'pair'=4] {'dp'}, dimensions={0} | all-to-all | bytes 1572864 | tf_op jit(solution)/shard_map/all_to_all | solution.py:49
  31.1 0.0 collective-permute-start.1
  31.1 1.5 %collective-permute-start = (bf16[8,48,1024]{2,1,0:T(8,128)(2,1)S(1)}, bf16[8,48,1024]{2,1,0:T(8,128)(2,1)S(1)}, u32[]{:S(2)}, u32[]{:S(2)}) collective-permute-start(bf16[8,48,1024]{2,1,0:T(8,128)(2,1)S(1)} %all_to_all.10), channel_id=1, source_target_pairs={{0,2},{1,3},{2,0},{3,1},{4,6},{5,7},{6,4},{7,5},{8,10},{9,11},{10,... | collective-permute-start | bytes 2359304 | tf_op jit(solution)/shard_map/ppermute | solution.py:51
  32.6 0.1 reshape.86
  32.7 0.6 fusion
  33.3 0.1 collective-permute-done.1
  33.4 0.1 reshape.87
  33.5 0.6 fusion.1
  34.1 16.9 %collective-permute-done = bf16[8,48,1024]{2,1,0:T(8,128)(2,1)S(1)} collective-permute-done((bf16[8,48,1024]{2,1,0:T(8,128)(2,1)S(1)}, bf16[8,48,1024]{2,1,0:T(8,128)(2,1)S(1)}, u32[]{:S(2)}, u32[]{:S(2)}) %collective-permute-start) | collective-permute-done | bytes 786464 | tf_op jit(solution)/shard_map/ppermute | solution.py:51
  51.0 0.0 collective-permute-start.2
  51.1 0.1 reshape.88
  51.1 0.6 fusion.2
  51.8 1.6 %collective-permute-done.2 = bf16[8,48,1024]{2,1,0:T(8,128)(2,1)S(1)} collective-permute-done((bf16[8,48,1024]{2,1,0:T(8,128)(2,1)S(1)}, bf16[8,48,1024]{2,1,0:T(8,128)(2,1)S(1)}, u32[]{:S(2)}, u32[]{:S(2)}) %collective-permute-start.2) | collective-permute-done | bytes 786464 | tf_op jit(solution)/shard_map/ppermute | solution.py:60
  53.4 0.1 reshape.89
  53.4 0.6 fusion.3
  54.1 0.1 reshape.85
  54.1 9.8 %all_to_all.11 = f32[8,1,48]{2,1,0:T(1,128)S(1)} all-to-all(f32[8,1,48]{2,1,0:T(1,128)S(1)} %reshape.85), channel_id=1, replica_groups=mesh['dp'=8,'pair'=4] {'dp'}, dimensions={0} | all-to-all | bytes 3072 | tf_op jit(solution)/shard_map/all_to_all | solution.py:81
  64.0 0.5 broadcast.59
  64.5 0.7 %reduce.19 = f32[8,48]{1,0:T(8,128)S(1)} reduce(f32[8,1,48]{2,1,0:T(1,128)S(1)} %all_to_all.11, f32[]{:T(128)} %broadcast.59), dimensions={1}, to_apply=%all_to_all.7.reduce_sub_computation.3 | reduce | bytes 3076 | tf_op jit(solution)/shard_map/all_to_all | solution.py:81
  65.2 0.1 broadcast_in_dim.64
  65.2 0.7 select_reduce_fusion
  (11 shorter events, 0.1 us)
Async XLA Ops:
  0.0 3.3 %copy-start = (f32[128,1024]{1,0:T(8,128)S(1)}, f32[128,1024]{1,0:T(8,128)}, u32[]{:S(2)}) copy-start(f32[128,1024]{1,0:T(8,128)} %param.2) | copy-start | bytes 1572868
  31.1 2.3 %collective-permute-start.1 = (bf16[8,48,1024]{2,1,0:T(8,128)(2,1)S(1)}, bf16[8,48,1024]{2,1,0:T(8,128)(2,1)S(1)}, u32[]{:S(2)}, u32[]{:S(2)}) collective-permute-start(bf16[8,48,1024]{2,1,0:T(8,128)(2,1)S(1)} %all_to_all.10), channel_id=1, source_target_pairs={{0,1},{1,0},{2,3},{3,2},{4,5},{5,4},{6,7},{7,6},{8,9},{9,8},{10,11... | collective-permute-start | bytes 2359304 | tf_op jit(solution)/shard_map/ppermute | solution.py:60
  31.1 20.0 %collective-permute-start = (bf16[8,48,1024]{2,1,0:T(8,128)(2,1)S(1)}, bf16[8,48,1024]{2,1,0:T(8,128)(2,1)S(1)}, u32[]{:S(2)}, u32[]{:S(2)}) collective-permute-start(bf16[8,48,1024]{2,1,0:T(8,128)(2,1)S(1)} %all_to_all.10), channel_id=1, source_target_pairs={{0,2},{1,3},{2,0},{3,1},{4,6},{5,7},{6,4},{7,5},{8,10},{9,11},{10,... | collective-permute-start | bytes 2359304 | tf_op jit(solution)/shard_map/ppermute | solution.py:51
  51.0 2.3 %collective-permute-start.2 = (bf16[8,48,1024]{2,1,0:T(8,128)(2,1)S(1)}, bf16[8,48,1024]{2,1,0:T(8,128)(2,1)S(1)}, u32[]{:S(2)}, u32[]{:S(2)}) collective-permute-start(bf16[8,48,1024]{2,1,0:T(8,128)(2,1)S(1)} %collective-permute-done), channel_id=1, source_target_pairs={{0,1},{1,0},{2,3},{3,2},{4,5},{5,4},{6,7},{7,6},{8,9},{9,8},{10,11... | collective-permute-start | bytes 2359304 | tf_op jit(solution)/shard_map/ppermute | solution.py:60

commit v7 on v6

--- a/solution.py
+++ b/solution.py
@@ -78,9 +78,10 @@
     if far is not None:
         far, best = lax.optimization_barrier((far, best))
         best = jnp.maximum(best, best_over(spread(far), False))
-    returned = lax.all_to_all(
-        best.reshape(groups, 1, chunk), "dp", split_axis=0, concat_axis=0, tiled=True
-    ).reshape(slots)
+    lanes = -(-chunk // 128) * 128
+    sent = jnp.pad(best.reshape(groups, 1, chunk), ((0, 0), (0, 7), (0, lanes - chunk)))
+    returned = lax.all_to_all(sent, "dp", split_axis=0, concat_axis=0, tiled=True)
+    returned = returned[:, 0, :chunk].reshape(slots)
     return jnp.sum(jnp.where(place, returned[:, None], 0.0), axis=0)
 
 

time: 66.2 us -> 65.2 us (0.985)
  no operation moved by 1% of the time
where the time goes in v7:
time: 65.2 us; the launch traced here: 65 us
  blocking collectives  37.3 us (57%)
  waiting for transfers between devices  18.6 us (29%)
  other arithmetic  4.02 us (6%)
  matrix products  2.88 us (4%)
  starting transfers between devices  1.5 us (2%)
    all_to_all x1, blocking collectives, shards(): lax.all_to_all(outgoing, 'dp', split_axis=0, concat_axis=0, tiled=True)  27.2 us
    ppermute x1, waiting for transfers between devices, shards(): lax.ppermute(block, 'pair', [(p, p ^ top) for p in range(peers)])  16.9 us
    all_to_all x1, blocking collectives, shards(): lax.all_to_all(sent, 'dp', split_axis=0, concat_axis=0, tiled=True)  10.1 us
    dot_general x4, matrix products, piece_best(): jnp.einsum('id,jd->ij', left, right, preferred_element_type=jnp.float32)  2.44 us
    ppermute x2, waiting for transfers between devices, spread(): pieces = pieces + [lax.ppermute(y, 'pair', perm) for y in pieces]  1.63 us
    ppermute x1, starting transfers between devices, shards(): lax.ppermute(block, 'pair', [(p, p ^ top) for p in range(peers)])  1.49 us
  transfers between devices with their start and end apart: 3, of which 3 were waited for; matrix products, arithmetic and copies ran while one was open for 3% of the time, Pallas kernels for 0%

profile of v7, /device:TPU:0, one launch (start us, length us, event | category | flops | bytes accessed | tf_op | source)
XLA Modules:
  0.0 65.0 jit_solution(2548964942103200732)
XLA Ops:
  0.0 0.0 copy-start
  0.0 0.7 %broadcast_shift-right-logical_fusion = s32[128]{0:T(128)S(1)} fusion(s32[128]{0:T(128)} %param.3), kind=kLoop, calls=%fused_computation.37 | loop fusion | flops 128 | bytes 1024 | tf_op jit(solution)/shard_map/shift_right_logical | solution.py:35
  0.7 0.1 fusion.7
  0.8 0.2 reduce_window_sum.11
  1.0 0.2 select_reduce_fusion.2
  1.2 0.7 %and_add_fusion = (s32[128]{0:T(128)S(1)}, s32[128]{0:T(128)S(1)}) fusion(s32[128]{0:T(128)} %param.3, s32[128]{0:T(128)S(1)} %select_reduce_fusion.2), kind=kLoop, calls=%fused_computation.34 | loop fusion | flops 768 | bytes 2048 | tf_op jit(solution)/shard_map/add | solution.py:43
  1.8 0.1 select_reduce_fusion.1
  2.0 0.1 sub.12
  2.1 1.2 %multiply_reduce_fusion = f32[128]{0:T(128)S(1)} fusion(f32[128,1024]{1,0:T(8,128)} %param.2), kind=kLoop, calls=%fused_computation.13 | loop fusion | flops 262016 | bytes 524800 | tf_op jit(solution)/shard_map/reduce_sum | solution.py:33
  3.3 0.0 copy-done
  3.3 0.4 convolution_convert_fusion
  3.7 0.1 broadcast_select_fusion
  3.8 27.2 %all_to_all.10 = bf16[8,48,1024]{2,1,0:T(8,128)(2,1)S(1)} all-to-all(bf16[8,48,1024]{2,1,0:T(8,128)(2,1)S(1)} %broadcast_select_fusion), channel_id=1, replica_groups=mesh['dp'=8,'pair'=4] {'dp'}, dimensions={0} | all-to-all | bytes 1572864 | tf_op jit(solution)/shard_map/all_to_all | solution.py:49
  31.1 0.0 collective-permute-start.1
  31.1 1.5 %collective-permute-start = (bf16[8,48,1024]{2,1,0:T(8,128)(2,1)S(1)}, bf16[8,48,1024]{2,1,0:T(8,128)(2,1)S(1)}, u32[]{:S(2)}, u32[]{:S(2)}) collective-permute-start(bf16[8,48,1024]{2,1,0:T(8,128)(2,1)S(1)} %all_to_all.10), channel_id=1, source_target_pairs={{0,2},{1,3},{2,0},{3,1},{4,6},{5,7},{6,4},{7,5},{8,10},{9,11},{10,... | collective-permute-start | bytes 2359304 | tf_op jit(solution)/shard_map/ppermute | solution.py:51
  32.6 0.1 reshape.86
  32.7 0.6 fusion
  33.3 0.1 collective-permute-done.1
  33.4 0.1 reshape.87
  33.5 0.6 fusion.1
  34.1 16.9 %collective-permute-done = bf16[8,48,1024]{2,1,0:T(8,128)(2,1)S(1)} collective-permute-done((bf16[8,48,1024]{2,1,0:T(8,128)(2,1)S(1)}, bf16[8,48,1024]{2,1,0:T(8,128)(2,1)S(1)}, u32[]{:S(2)}, u32[]{:S(2)}) %collective-permute-start) | collective-permute-done | bytes 786464 | tf_op jit(solution)/shard_map/ppermute | solution.py:51
  51.0 0.0 collective-permute-start.2
  51.1 0.1 reshape.88
  51.1 0.6 fusion.2
  51.8 1.6 %collective-permute-done.2 = bf16[8,48,1024]{2,1,0:T(8,128)(2,1)S(1)} collective-permute-done((bf16[8,48,1024]{2,1,0:T(8,128)(2,1)S(1)}, bf16[8,48,1024]{2,1,0:T(8,128)(2,1)S(1)}, u32[]{:S(2)}, u32[]{:S(2)}) %collective-permute-start.2) | collective-permute-done | bytes 786464 | tf_op jit(solution)/shard_map/ppermute | solution.py:60
  53.4 0.1 reshape.89
  53.4 0.6 fusion.3
  54.1 0.1 reshape.85
  54.2 10.1 %all_to_all.11 = f32[8,8,128]{2,1,0:T(8,128)S(1)} all-to-all(f32[8,8,128]{2,1,0:T(8,128)S(1)} %pad.10), channel_id=1, replica_groups=mesh['dp'=8,'pair'=4] {'dp'}, dimensions={0} | all-to-all | bytes 65536 | tf_op jit(solution)/shard_map/all_to_all | solution.py:83
  64.2 0.1 broadcast_in_dim.64
  64.3 0.7 %select_reduce_fusion = f32[128]{0:T(128)} fusion(f32[384]{0:T(512)S(1)} %broadcast_in_dim.64, s32[128]{0:T(128)S(1)} %get-tuple-element.10), kind=kLoop, calls=%fused_computation.15 | loop fusion | flops 147328 | bytes 2560 | tf_op jit(solution)/shard_map/reduce_sum | solution.py:85
  (13 shorter events, 0.1 us)
Async XLA Ops:
  0.0 3.3 %copy-start = (f32[128,1024]{1,0:T(8,128)S(1)}, f32[128,1024]{1,0:T(8,128)}, u32[]{:S(2)}) copy-start(f32[128,1024]{1,0:T(8,128)} %param.2) | copy-start | bytes 1572868
  31.1 2.3 %collective-permute-start.1 = (bf16[8,48,1024]{2,1,0:T(8,128)(2,1)S(1)}, bf16[8,48,1024]{2,1,0:T(8,128)(2,1)S(1)}, u32[]{:S(2)}, u32[]{:S(2)}) collective-permute-start(bf16[8,48,1024]{2,1,0:T(8,128)(2,1)S(1)} %all_to_all.10), channel_id=1, source_target_pairs={{0,1},{1,0},{2,3},{3,2},{4,5},{5,4},{6,7},{7,6},{8,9},{9,8},{10,11... | collective-permute-start | bytes 2359304 | tf_op jit(solution)/shard_map/ppermute | solution.py:60
  31.1 20.0 %collective-permute-start = (bf16[8,48,1024]{2,1,0:T(8,128)(2,1)S(1)}, bf16[8,48,1024]{2,1,0:T(8,128)(2,1)S(1)}, u32[]{:S(2)}, u32[]{:S(2)}) collective-permute-start(bf16[8,48,1024]{2,1,0:T(8,128)(2,1)S(1)} %all_to_all.10), channel_id=1, source_target_pairs={{0,2},{1,3},{2,0},{3,1},{4,6},{5,7},{6,4},{7,5},{8,10},{9,11},{10,... | collective-permute-start | bytes 2359304 | tf_op jit(solution)/shard_map/ppermute | solution.py:51
  51.0 2.3 %collective-permute-start.2 = (bf16[8,48,1024]{2,1,0:T(8,128)(2,1)S(1)}, bf16[8,48,1024]{2,1,0:T(8,128)(2,1)S(1)}, u32[]{:S(2)}, u32[]{:S(2)}) collective-permute-start(bf16[8,48,1024]{2,1,0:T(8,128)(2,1)S(1)} %collective-permute-done), channel_id=1, source_target_pairs={{0,1},{1,0},{2,3},{3,2},{4,5},{5,4},{6,7},{7,6},{8,9},{9,8},{10,11... | collective-permute-start | bytes 2359304 | tf_op jit(solution)/shard_map/ppermute | solution.py:60

commit v8 on v7

--- a/solution.py
+++ b/solution.py
@@ -1,6 +1,10 @@
+import functools
+
 import jax
 import jax.numpy as jnp
 from jax import lax
+from jax.experimental import pallas as pl
+from jax.experimental.pallas import tpu as pltpu
 from jax.sharding import PartitionSpec as P
 
 CPO = 4
@@ -23,6 +27,61 @@
     return block[:, capacity, :chunk].astype(jnp.int32).reshape(groups * chunk)
 
 
+def prepare_kernel(emb_ref, lrow_ref, lcol_ref, out_ref, slot_ref, *, groups, chunk, capacity):
+    rows, width = emb_ref.shape
+    slots = groups * chunk
+    shift = CPO.bit_length() - 1
+    e = emb_ref[...]
+    norm = jnp.sqrt(jnp.sum(e * e, axis=1, keepdims=True) + 1e-06)
+    unit = (e / norm).astype(jnp.bfloat16)
+    lrow = lrow_ref[...]
+    lcol = lcol_ref[...]
+    orow = lax.shift_right_logical(lrow, shift)
+    ocol = lax.shift_right_logical(lcol, shift)
+    local_row = jnp.bitwise_and(lrow, CPO - 1)
+    first = lax.broadcasted_iota(jnp.int32, (rows, rows), 0)
+    second = lax.broadcasted_iota(jnp.int32, (rows, rows), 1)
+    same = ocol == orow
+    rank_row = jnp.sum(jnp.where(same & (first < second), 1, 0), axis=0, keepdims=True)
+    rank_col = jnp.sum(jnp.where(same & (second < first), 1, 0), axis=1, keepdims=True)
+    slot_row = orow * chunk + rank_row
+    slot_ref[...] = slot_row
+    place = (lax.broadcasted_iota(jnp.int32, (slots, rows), 0) == slot_row).astype(jnp.bfloat16)
+    placed = jnp.dot(place, unit, preferred_element_type=jnp.float32)
+    weight = jnp.where(
+        lax.broadcasted_iota(jnp.int32, (groups, rows), 0) == orow, local_row + 1, 0
+    ).astype(jnp.bfloat16)
+    at_rank = (lax.broadcasted_iota(jnp.int32, (rows, width), 1) == rank_col).astype(jnp.bfloat16)
+    tags = jnp.dot(weight, at_rank, preferred_element_type=jnp.float32)
+    slot_id = lax.broadcasted_iota(jnp.int32, (slots, groups), 0)
+    of_group = (
+        lax.div(slot_id, chunk) == lax.broadcasted_iota(jnp.int32, (slots, groups), 1)
+    ).astype(jnp.bfloat16)
+    tag_rows = jnp.dot(of_group, tags.astype(jnp.bfloat16), preferred_element_type=jnp.float32)
+    in_chunk = lax.rem(lax.broadcasted_iota(jnp.int32, (slots, width), 0), chunk)
+    out_ref[...] = jnp.where(in_chunk == capacity, tag_rows - 1.0, placed).astype(jnp.bfloat16)
+
+
+def prepare(embeddings, labels, groups, chunk, capacity):
+    rows, width = embeddings.shape
+    slots = groups * chunk
+    vmem = pltpu.MemorySpace.VMEM
+    return pl.pallas_call(
+        functools.partial(prepare_kernel, groups=groups, chunk=chunk, capacity=capacity),
+        out_shape=(
+            jax.ShapeDtypeStruct((slots, width), jnp.bfloat16),
+            jax.ShapeDtypeStruct((1, rows), jnp.int32),
+        ),
+        in_specs=[pl.BlockSpec(memory_space=vmem)] * 3,
+        out_specs=(pl.BlockSpec(memory_space=vmem), pl.BlockSpec(memory_space=vmem)),
+        cost_estimate=pl.CostEstimate(
+            flops=2 * slots * rows * width + 4 * rows * width,
+            transcendentals=rows,
+            bytes_accessed=rows * width * 4 + slots * width * 2,
+        ),
+    )(embeddings, labels[None, :], labels[:, None])
+
+
 def shards(embeddings, labels):
     rows, width = embeddings.shape
     groups = lax.axis_size("dp")
@@ -30,22 +89,28 @@
     capacity = 5 * rows // (2 * groups)
     chunk = -(-(capacity + 1) // 16) * 16
     slots = groups * chunk
-    norm = jnp.sqrt(jnp.sum(embeddings * embeddings, axis=1, keepdims=True) + 1e-06)
-    unit = (embeddings / norm).astype(jnp.bfloat16)
-    owner = lax.shift_right_logical(labels, CPO.bit_length() - 1)
-    local = jnp.bitwise_and(labels, CPO - 1)
-    onehot = (owner[:, None] == jnp.arange(groups, dtype=jnp.int32)[None, :]).astype(jnp.int32)
-    rank = jnp.sum(jnp.cumsum(onehot, axis=0) * onehot, axis=1) - 1
-    slot = owner * chunk + rank
-    place = slot[None, :] == jnp.arange(slots, dtype=jnp.int32)[:, None]
-    outgoing = jnp.dot(place.astype(jnp.bfloat16), unit, preferred_element_type=jnp.float32)
-    outgoing = outgoing.astype(jnp.bfloat16).reshape(groups, chunk, width)
-    tag = jnp.sum(jnp.where(place, local[None, :] + 1, 0), axis=1) - 1
-    tag_row = jnp.pad(tag.reshape(groups, chunk), ((0, 0), (0, width - chunk)), constant_values=-1)
-    row_id = jnp.arange(chunk, dtype=jnp.int32)
-    outgoing = jnp.where(
-        (row_id == capacity)[None, :, None], tag_row.astype(jnp.bfloat16)[:, None, :], outgoing
-    )
+    if groups <= 16:
+        outgoing, slot = prepare(embeddings, labels, groups, chunk, capacity)
+        outgoing = outgoing.reshape(groups, chunk, width)
+        slot = slot.reshape(rows)
+        place = slot[None, :] == jnp.arange(slots, dtype=jnp.int32)[:, None]
+    else:
+        norm = jnp.sqrt(jnp.sum(embeddings * embeddings, axis=1, keepdims=True) + 1e-06)
+        unit = (embeddings / norm).astype(jnp.bfloat16)
+        owner = lax.shift_right_logical(labels, CPO.bit_length() - 1)
+        local = jnp.bitwise_and(labels, CPO - 1)
+        onehot = (owner[:, None] == jnp.arange(groups, dtype=jnp.int32)[None, :]).astype(jnp.int32)
+        rank = jnp.sum(jnp.cumsum(onehot, axis=0) * onehot, axis=1) - 1
+        slot = owner * chunk + rank
+        place = slot[None, :] == jnp.arange(slots, dtype=jnp.int32)[:, None]
+        outgoing = jnp.dot(place.astype(jnp.bfloat16), unit, preferred_element_type=jnp.float32)
+        outgoing = outgoing.astype(jnp.bfloat16).reshape(groups, chunk, width)
+        tag = jnp.sum(jnp.where(place, local[None, :] + 1, 0), axis=1) - 1
+        tag_row = jnp.pad(tag.reshape(groups, chunk), ((0, 0), (0, width - chunk)), constant_values=-1)
+        row_id = jnp.arange(chunk, dtype=jnp.int32)
+        outgoing = jnp.where(
+            (row_id == capacity)[None, :, None], tag_row.astype(jnp.bfloat16)[:, None, :], outgoing
+        )
     block = lax.all_to_all(outgoing, "dp", split_axis=0, concat_axis=0, tiled=True)
     top = peers // 2
     far = lax.ppermute(block, "pair", [(p, p ^ top) for p in range(peers)]) if top else None

time: 65.2 us -> 66.4 us (1.018)
  other arithmetic: 4.02 us -> 0.74 us
  Pallas kernels: 0 us -> 2.8 us
  local copies, waits for them, and re-layouts: 0.6 us -> 2.55 us
    pallas_call x0 -> x1, Pallas kernels: none -> 2.8 us  [prepare(): pl.pallas_call(functools.partial(prepare_kernel, groups=groups, chunk=chu...]
    reduce_sum x3 -> x0, other arithmetic: 1.49 us -> none  [the longest x1 1.17 us: shards(): jnp.sum(embeddings * embeddings, axis=1, keepdims=True) + 1e-06]
    unnamed x2 -> x4, local copies, waits for them, and re-layouts: 0.01 us -> 1.31 us
    broadcast_in_dim x0 -> x1, local copies, waits for them, and re-layouts: none -> 0.73 us  [prepare(): labels[:, None]]
    shift_right_logical x1 -> x0, other arithmetic: 0.71 us -> none  [shards(): owner = lax.shift_right_logical(labels, CPO.bit_length() - 1)]
    add x1 -> x0, other arithmetic: 0.67 us -> none  [shards(): tag = jnp.sum(jnp.where(place, local[None, :] + 1, 0), axis=1) - 1]
where the time goes in v8:
time: 66.4 us; the launch traced here: 66.1 us
  blocking collectives  37.5 us (56%)
  waiting for transfers between devices  18.6 us (28%)
  Pallas kernels  2.8 us (4%)
  local copies, waits for them, and re-layouts  2.55 us (4%)
  matrix products  2.44 us (4%)
  starting transfers between devices  1.5 us (2%)
  other arithmetic  0.74 us (1%)
    all_to_all x1, blocking collectives, shards(): lax.all_to_all(outgoing, 'dp', split_axis=0, concat_axis=0, tiled=True)  27.4 us
    ppermute x1, waiting for transfers between devices, shards(): lax.ppermute(block, 'pair', [(p, p ^ top) for p in range(peers)])  16.9 us
    all_to_all x1, blocking collectives, shards(): lax.all_to_all(sent, 'dp', split_axis=0, concat_axis=0, tiled=True)  10.1 us
    pallas_call x1, Pallas kernels, prepare(): pl.pallas_call(functools.partial(prepare_kernel, groups=groups, chunk=chu...  2.8 us
    dot_general x4, matrix products, piece_best(): jnp.einsum('id,jd->ij', left, right, preferred_element_type=jnp.float32)  2.44 us
    ppermute x2, waiting for transfers between devices, spread(): pieces = pieces + [lax.ppermute(y, 'pair', perm) for y in pieces]  1.63 us
    ppermute x1, starting transfers between devices, shards(): lax.ppermute(block, 'pair', [(p, p ^ top) for p in range(peers)])  1.5 us
  transfers between devices with their start and end apart: 3, of which 3 were waited for; matrix products, arithmetic and copies ran while one was open for 3% of the time, Pallas kernels for 0%

profile of v8, /device:TPU:0, one launch (start us, length us, event | category | flops | bytes accessed | tf_op | source)
XLA Modules:
  0.0 66.1 jit_solution(13417990654151425795)
XLA Ops:
  0.0 0.0 copy-start
  0.0 0.7 copy-done
  0.7 0.7 %copy.4.lcol_ref = s32[128,1]{1,0:T(8,128)} copy(s32[128,1]{0,1:T(1,128)S(1)} %bitcast.22) | data formatting | bytes 1024 | tf_op jit(solution)/shard_map/broadcast_in_dim | solution.py:82
  1.4 2.8 %shard_map.28 = (bf16[384,1024]{1,0:T(8,128)(2,1)}, s32[1,128]{1,0:T(1,128)}) custom-call(f32[128,1024]{1,0:T(8,128)} %emb_ref.1, s32[1,128]{1,0:T(1,128)} %bitcast.21, s32[128,1]{1,0:T(8,128)} %copy.4.lcol_ref), custom_call_target="tpu_custom_call" | custom-call | flops 101187584 | bytes 1310720 | tf_op jit(solution)/shard_map/pallas_call | solution.py:69
  4.2 27.4 %all_to_all.10 = bf16[8,48,1024]{2,1,0:T(8,128)(2,1)S(1)} all-to-all(bf16[8,48,1024]{2,1,0:T(8,128)(2,1)} %bitcast.20), channel_id=1, replica_groups=mesh['dp'=8,'pair'=4] {'dp'}, dimensions={0} | all-to-all | bytes 1572864 | tf_op jit(solution)/shard_map/all_to_all | solution.py:114
  31.6 0.0 collective-permute-start.1
  31.6 1.5 %collective-permute-start = (bf16[8,48,1024]{2,1,0:T(8,128)(2,1)S(1)}, bf16[8,48,1024]{2,1,0:T(8,128)(2,1)S(1)}, u32[]{:S(2)}, u32[]{:S(2)}) collective-permute-start(bf16[8,48,1024]{2,1,0:T(8,128)(2,1)S(1)} %all_to_all.10), channel_id=1, source_target_pairs={{0,2},{1,3},{2,0},{3,1},{4,6},{5,7},{6,4},{7,5},{8,10},{9,11},{10,... | collective-permute-start | bytes 2359304 | tf_op jit(solution)/shard_map/ppermute | solution.py:116
  33.1 0.1 reshape.66
  33.2 0.6 fusion
  33.8 0.1 collective-permute-done.1
  33.9 0.1 reshape.67
  34.0 0.6 fusion.1
  34.6 16.9 %collective-permute-done = bf16[8,48,1024]{2,1,0:T(8,128)(2,1)S(1)} collective-permute-done((bf16[8,48,1024]{2,1,0:T(8,128)(2,1)S(1)}, bf16[8,48,1024]{2,1,0:T(8,128)(2,1)S(1)}, u32[]{:S(2)}, u32[]{:S(2)}) %collective-permute-start) | collective-permute-done | bytes 786464 | tf_op jit(solution)/shard_map/ppermute | solution.py:116
  51.6 0.0 collective-permute-start.2
  51.6 0.1 reshape.68
  51.7 0.6 fusion.2
  52.3 1.6 %collective-permute-done.2 = bf16[8,48,1024]{2,1,0:T(8,128)(2,1)S(1)} collective-permute-done((bf16[8,48,1024]{2,1,0:T(8,128)(2,1)S(1)}, bf16[8,48,1024]{2,1,0:T(8,128)(2,1)S(1)}, u32[]{:S(2)}, u32[]{:S(2)}) %collective-permute-start.2) | collective-permute-done | bytes 786464 | tf_op jit(solution)/shard_map/ppermute | solution.py:125
  53.9 0.1 reshape.69
  54.0 0.6 fusion.3
  54.6 0.1 reshape.65
  54.7 10.1 %all_to_all.11 = f32[8,8,128]{2,1,0:T(8,128)S(1)} all-to-all(f32[8,8,128]{2,1,0:T(8,128)S(1)} %pad.4), channel_id=1, replica_groups=mesh['dp'=8,'pair'=4] {'dp'}, dimensions={0} | all-to-all | bytes 65536 | tf_op jit(solution)/shard_map/all_to_all | solution.py:148
  64.8 0.1 broadcast_in_dim.33
  64.8 0.0 copy-start.1
  64.8 0.7 copy-done.1
  65.5 0.6 select_reduce_fusion
  (9 shorter events, 0.1 us)
Async XLA Ops:
  0.0 0.7 copy-start
  31.6 2.3 %collective-permute-start.1 = (bf16[8,48,1024]{2,1,0:T(8,128)(2,1)S(1)}, bf16[8,48,1024]{2,1,0:T(8,128)(2,1)S(1)}, u32[]{:S(2)}, u32[]{:S(2)}) collective-permute-start(bf16[8,48,1024]{2,1,0:T(8,128)(2,1)S(1)} %all_to_all.10), channel_id=1, source_target_pairs={{0,1},{1,0},{2,3},{3,2},{4,5},{5,4},{6,7},{7,6},{8,9},{9,8},{10,11... | collective-permute-start | bytes 2359304 | tf_op jit(solution)/shard_map/ppermute | solution.py:125
  31.6 20.0 %collective-permute-start = (bf16[8,48,1024]{2,1,0:T(8,128)(2,1)S(1)}, bf16[8,48,1024]{2,1,0:T(8,128)(2,1)S(1)}, u32[]{:S(2)}, u32[]{:S(2)}) collective-permute-start(bf16[8,48,1024]{2,1,0:T(8,128)(2,1)S(1)} %all_to_all.10), channel_id=1, source_target_pairs={{0,2},{1,3},{2,0},{3,1},{4,6},{5,7},{6,4},{7,5},{8,10},{9,11},{10,... | collective-permute-start | bytes 2359304 | tf_op jit(solution)/shard_map/ppermute | solution.py:116
  51.6 2.3 %collective-permute-start.2 = (bf16[8,48,1024]{2,1,0:T(8,128)(2,1)S(1)}, bf16[8,48,1024]{2,1,0:T(8,128)(2,1)S(1)}, u32[]{:S(2)}, u32[]{:S(2)}) collective-permute-start(bf16[8,48,1024]{2,1,0:T(8,128)(2,1)S(1)} %collective-permute-done), channel_id=1, source_target_pairs={{0,1},{1,0},{2,3},{3,2},{4,5},{5,4},{6,7},{7,6},{8,9},{9,8},{10,11... | collective-permute-start | bytes 2359304 | tf_op jit(solution)/shard_map/ppermute | solution.py:125
  64.8 0.7 copy-start.1

commit v9 on v8

--- a/solution.py
+++ b/solution.py
@@ -27,7 +27,7 @@
     return block[:, capacity, :chunk].astype(jnp.int32).reshape(groups * chunk)
 
 
-def prepare_kernel(emb_ref, lrow_ref, lcol_ref, out_ref, slot_ref, *, groups, chunk, capacity):
+def prepare_kernel(emb_ref, lrow_ref, out_ref, slot_ref, *, groups, chunk, capacity):
     rows, width = emb_ref.shape
     slots = groups * chunk
     shift = CPO.bit_length() - 1
@@ -35,12 +35,11 @@
     norm = jnp.sqrt(jnp.sum(e * e, axis=1, keepdims=True) + 1e-06)
     unit = (e / norm).astype(jnp.bfloat16)
     lrow = lrow_ref[...]
-    lcol = lcol_ref[...]
     orow = lax.shift_right_logical(lrow, shift)
-    ocol = lax.shift_right_logical(lcol, shift)
     local_row = jnp.bitwise_and(lrow, CPO - 1)
     first = lax.broadcasted_iota(jnp.int32, (rows, rows), 0)
     second = lax.broadcasted_iota(jnp.int32, (rows, rows), 1)
+    ocol = jnp.sum(jnp.where(first == second, orow, 0), axis=1, keepdims=True)
     same = ocol == orow
     rank_row = jnp.sum(jnp.where(same & (first < second), 1, 0), axis=0, keepdims=True)
     rank_col = jnp.sum(jnp.where(same & (second < first), 1, 0), axis=1, keepdims=True)
@@ -52,14 +51,11 @@
         lax.broadcasted_iota(jnp.int32, (groups, rows), 0) == orow, local_row + 1, 0
     ).astype(jnp.bfloat16)
     at_rank = (lax.broadcasted_iota(jnp.int32, (rows, width), 1) == rank_col).astype(jnp.bfloat16)
-    tags = jnp.dot(weight, at_rank, preferred_element_type=jnp.float32)
-    slot_id = lax.broadcasted_iota(jnp.int32, (slots, groups), 0)
-    of_group = (
-        lax.div(slot_id, chunk) == lax.broadcasted_iota(jnp.int32, (slots, groups), 1)
-    ).astype(jnp.bfloat16)
-    tag_rows = jnp.dot(of_group, tags.astype(jnp.bfloat16), preferred_element_type=jnp.float32)
-    in_chunk = lax.rem(lax.broadcasted_iota(jnp.int32, (slots, width), 0), chunk)
-    out_ref[...] = jnp.where(in_chunk == capacity, tag_rows - 1.0, placed).astype(jnp.bfloat16)
+    tags = jnp.dot(weight, at_rank, preferred_element_type=jnp.float32) - 1.0
+    tag_slot = lax.broadcasted_iota(jnp.int32, (slots, groups), 1) * chunk + capacity
+    at_tag = (lax.broadcasted_iota(jnp.int32, (slots, groups), 0) == tag_slot).astype(jnp.bfloat16)
+    placed = placed + jnp.dot(at_tag, tags.astype(jnp.bfloat16), preferred_element_type=jnp.float32)
+    out_ref[...] = placed.astype(jnp.bfloat16)
 
 
 def prepare(embeddings, labels, groups, chunk, capacity):
@@ -72,14 +68,14 @@
             jax.ShapeDtypeStruct((slots, width), jnp.bfloat16),
             jax.ShapeDtypeStruct((1, rows), jnp.int32),
         ),
-        in_specs=[pl.BlockSpec(memory_space=vmem)] * 3,
+        in_specs=[pl.BlockSpec(memory_space=vmem)] * 2,
         out_specs=(pl.BlockSpec(memory_space=vmem), pl.BlockSpec(memory_space=vmem)),
         cost_estimate=pl.CostEstimate(
             flops=2 * slots * rows * width + 4 * rows * width,
             transcendentals=rows,
             bytes_accessed=rows * width * 4 + slots * width * 2,
         ),
-    )(embeddings, labels[None, :], labels[:, None])
+    )(embeddings, labels[None, :])
 
 
 def shards(embeddings, labels):

time: 66.4 us -> 65 us (0.979)
  local copies, waits for them, and re-layouts: 2.55 us -> 1.16 us
    broadcast_in_dim x1 -> x0, local copies, waits for them, and re-layouts: 0.73 us -> none  [prepare(): labels[:, None]]
where the time goes in v9:
time: 65 us; the launch traced here: 64.7 us
  blocking collectives  37.5 us (58%)
  waiting for transfers between devices  18.6 us (29%)
  Pallas kernels  2.78 us (4%)
  matrix products  2.45 us (4%)
  starting transfers between devices  1.51 us (2%)
  local copies, waits for them, and re-layouts  1.16 us (2%)
  other arithmetic  0.74 us (1%)
    all_to_all x1, blocking collectives, shards(): lax.all_to_all(outgoing, 'dp', split_axis=0, concat_axis=0, tiled=True)  27.4 us
    ppermute x1, waiting for transfers between devices, shards(): lax.ppermute(block, 'pair', [(p, p ^ top) for p in range(peers)])  16.9 us
    all_to_all x1, blocking collectives, shards(): lax.all_to_all(sent, 'dp', split_axis=0, concat_axis=0, tiled=True)  10.1 us
    pallas_call x1, Pallas kernels, prepare(): pl.pallas_call(functools.partial(prepare_kernel, groups=groups, chunk=chu...  2.78 us
    dot_general x4, matrix products, piece_best(): jnp.einsum('id,jd->ij', left, right, preferred_element_type=jnp.float32)  2.45 us
    ppermute x2, waiting for transfers between devices, spread(): pieces = pieces + [lax.ppermute(y, 'pair', perm) for y in pieces]  1.62 us
    ppermute x1, starting transfers between devices, shards(): lax.ppermute(block, 'pair', [(p, p ^ top) for p in range(peers)])  1.5 us
  transfers between devices with their start and end apart: 3, of which 3 were waited for; matrix products, arithmetic and copies ran while one was open for 3% of the time, Pallas kernels for 0%

profile of v9, /device:TPU:0, one launch (start us, length us, event | category | flops | bytes accessed | tf_op | source)
XLA Modules:
  0.0 64.7 jit_solution(8038346861362488392)
XLA Ops:
  0.0 2.8 %shard_map.28 = (bf16[384,1024]{1,0:T(8,128)(2,1)}, s32[1,128]{1,0:T(1,128)}) custom-call(f32[128,1024]{1,0:T(8,128)} %emb_ref.1, s32[1,128]{1,0:T(1,128)} %bitcast.20), custom_call_target="tpu_custom_call" | custom-call | flops 101187584 | bytes 1310720 | tf_op jit(solution)/shard_map/pallas_call | solution.py:65
  2.8 27.4 %all_to_all.10 = bf16[8,48,1024]{2,1,0:T(8,128)(2,1)S(1)} all-to-all(bf16[8,48,1024]{2,1,0:T(8,128)(2,1)} %bitcast.19), channel_id=1, replica_groups=mesh['dp'=8,'pair'=4] {'dp'}, dimensions={0} | all-to-all | bytes 1572864 | tf_op jit(solution)/shard_map/all_to_all | solution.py:110
  30.2 0.0 collective-permute-start.1
  30.2 1.5 %collective-permute-start = (bf16[8,48,1024]{2,1,0:T(8,128)(2,1)S(1)}, bf16[8,48,1024]{2,1,0:T(8,128)(2,1)S(1)}, u32[]{:S(2)}, u32[]{:S(2)}) collective-permute-start(bf16[8,48,1024]{2,1,0:T(8,128)(2,1)S(1)} %all_to_all.10), channel_id=1, source_target_pairs={{0,2},{1,3},{2,0},{3,1},{4,6},{5,7},{6,4},{7,5},{8,10},{9,11},{10,... | collective-permute-start | bytes 2359304 | tf_op jit(solution)/shard_map/ppermute | solution.py:112
  31.7 0.1 reshape.66
  31.8 0.6 fusion
  32.4 0.1 collective-permute-done.1
  32.5 0.1 reshape.67
  32.6 0.6 fusion.1
  33.2 16.9 %collective-permute-done = bf16[8,48,1024]{2,1,0:T(8,128)(2,1)S(1)} collective-permute-done((bf16[8,48,1024]{2,1,0:T(8,128)(2,1)S(1)}, bf16[8,48,1024]{2,1,0:T(8,128)(2,1)S(1)}, u32[]{:S(2)}, u32[]{:S(2)}) %collective-permute-start) | collective-permute-done | bytes 786464 | tf_op jit(solution)/shard_map/ppermute | solution.py:112
  50.2 0.0 collective-permute-start.2
  50.2 0.1 reshape.68
  50.3 0.6 fusion.2
  50.9 1.6 %collective-permute-done.2 = bf16[8,48,1024]{2,1,0:T(8,128)(2,1)S(1)} collective-permute-done((bf16[8,48,1024]{2,1,0:T(8,128)(2,1)S(1)}, bf16[8,48,1024]{2,1,0:T(8,128)(2,1)S(1)}, u32[]{:S(2)}, u32[]{:S(2)}) %collective-permute-start.2) | collective-permute-done | bytes 786464 | tf_op jit(solution)/shard_map/ppermute | solution.py:121
  52.5 0.1 reshape.69
  52.6 0.6 fusion.3
  53.2 0.1 reshape.65
  53.3 10.1 %all_to_all.11 = f32[8,8,128]{2,1,0:T(8,128)S(1)} all-to-all(f32[8,8,128]{2,1,0:T(8,128)S(1)} %pad.4), channel_id=1, replica_groups=mesh['dp'=8,'pair'=4] {'dp'}, dimensions={0} | all-to-all | bytes 65536 | tf_op jit(solution)/shard_map/all_to_all | solution.py:144
  63.4 0.1 broadcast_in_dim.29
  63.4 0.0 copy-start
  63.4 0.7 %copy-done = s32[1,128]{1,0:T(1,128)S(1)} copy-done((s32[1,128]{1,0:T(1,128)S(1)}, s32[1,128]{1,0:T(1,128)}, u32[]{:S(2)}) %copy-start) | copy-done | bytes 536
  64.1 0.6 select_reduce_fusion
  (9 shorter events, 0.1 us)
Async XLA Ops:
  30.2 2.3 %collective-permute-start.1 = (bf16[8,48,1024]{2,1,0:T(8,128)(2,1)S(1)}, bf16[8,48,1024]{2,1,0:T(8,128)(2,1)S(1)}, u32[]{:S(2)}, u32[]{:S(2)}) collective-permute-start(bf16[8,48,1024]{2,1,0:T(8,128)(2,1)S(1)} %all_to_all.10), channel_id=1, source_target_pairs={{0,1},{1,0},{2,3},{3,2},{4,5},{5,4},{6,7},{7,6},{8,9},{9,8},{10,11... | collective-permute-start | bytes 2359304 | tf_op jit(solution)/shard_map/ppermute | solution.py:121
  30.2 20.0 %collective-permute-start = (bf16[8,48,1024]{2,1,0:T(8,128)(2,1)S(1)}, bf16[8,48,1024]{2,1,0:T(8,128)(2,1)S(1)}, u32[]{:S(2)}, u32[]{:S(2)}) collective-permute-start(bf16[8,48,1024]{2,1,0:T(8,128)(2,1)S(1)} %all_to_all.10), channel_id=1, source_target_pairs={{0,2},{1,3},{2,0},{3,1},{4,6},{5,7},{6,4},{7,5},{8,10},{9,11},{10,... | collective-permute-start | bytes 2359304 | tf_op jit(solution)/shard_map/ppermute | solution.py:112
  50.2 2.3 %collective-permute-start.2 = (bf16[8,48,1024]{2,1,0:T(8,128)(2,1)S(1)}, bf16[8,48,1024]{2,1,0:T(8,128)(2,1)S(1)}, u32[]{:S(2)}, u32[]{:S(2)}) collective-permute-start(bf16[8,48,1024]{2,1,0:T(8,128)(2,1)S(1)} %collective-permute-done), channel_id=1, source_target_pairs={{0,1},{1,0},{2,3},{3,2},{4,5},{5,4},{6,7},{7,6},{8,9},{9,8},{10,11... | collective-permute-start | bytes 2359304 | tf_op jit(solution)/shard_map/ppermute | solution.py:121
  63.4 0.7 %copy-start = (s32[1,128]{1,0:T(1,128)S(1)}, s32[1,128]{1,0:T(1,128)}, u32[]{:S(2)}) copy-start(s32[1,128]{1,0:T(1,128)} %get-tuple-element.9) | copy-start | bytes 1540

commit v10 on v9

--- a/solution.py
+++ b/solution.py
@@ -33,7 +33,7 @@
     shift = CPO.bit_length() - 1
     e = emb_ref[...]
     norm = jnp.sqrt(jnp.sum(e * e, axis=1, keepdims=True) + 1e-06)
-    unit = (e / norm).astype(jnp.bfloat16)
+    unit = (e * (1.0 / norm)).astype(jnp.bfloat16)
     lrow = lrow_ref[...]
     orow = lax.shift_right_logical(lrow, shift)
     local_row = jnp.bitwise_and(lrow, CPO - 1)
@@ -51,11 +51,10 @@
         lax.broadcasted_iota(jnp.int32, (groups, rows), 0) == orow, local_row + 1, 0
     ).astype(jnp.bfloat16)
     at_rank = (lax.broadcasted_iota(jnp.int32, (rows, width), 1) == rank_col).astype(jnp.bfloat16)
-    tags = jnp.dot(weight, at_rank, preferred_element_type=jnp.float32) - 1.0
-    tag_slot = lax.broadcasted_iota(jnp.int32, (slots, groups), 1) * chunk + capacity
-    at_tag = (lax.broadcasted_iota(jnp.int32, (slots, groups), 0) == tag_slot).astype(jnp.bfloat16)
-    placed = placed + jnp.dot(at_tag, tags.astype(jnp.bfloat16), preferred_element_type=jnp.float32)
+    tags = (jnp.dot(weight, at_rank, preferred_element_type=jnp.float32) - 1.0).astype(jnp.bfloat16)
     out_ref[...] = placed.astype(jnp.bfloat16)
+    for g in range(groups):
+        out_ref[pl.ds(g * chunk + capacity, 1), :] = tags[g:g + 1, :]
 
 
 def prepare(embeddings, labels, groups, chunk, capacity):

time: 65 us -> 64.7 us (level)
  no operation moved by 1% of the time
where the time goes in v10:
time: 64.7 us; the launch traced here: 64.4 us
  blocking collectives  37.5 us (58%)
  waiting for transfers between devices  18.6 us (29%)
  Pallas kernels  2.45 us (4%)
  matrix products  2.44 us (4%)
  starting transfers between devices  1.5 us (2%)
  local copies, waits for them, and re-layouts  1.16 us (2%)
  other arithmetic  0.74 us (1%)
    all_to_all x1, blocking collectives, shards(): lax.all_to_all(outgoing, 'dp', split_axis=0, concat_axis=0, tiled=True)  27.4 us
    ppermute x1, waiting for transfers between devices, shards(): lax.ppermute(block, 'pair', [(p, p ^ top) for p in range(peers)])  16.9 us
    all_to_all x1, blocking collectives, shards(): lax.all_to_all(sent, 'dp', split_axis=0, concat_axis=0, tiled=True)  10.1 us
    pallas_call x1, Pallas kernels, prepare(): pl.pallas_call(functools.partial(prepare_kernel, groups=groups, chunk=chu...  2.45 us
    dot_general x4, matrix products, piece_best(): jnp.einsum('id,jd->ij', left, right, preferred_element_type=jnp.float32)  2.44 us
    ppermute x2, waiting for transfers between devices, spread(): pieces = pieces + [lax.ppermute(y, 'pair', perm) for y in pieces]  1.62 us
    ppermute x1, starting transfers between devices, shards(): lax.ppermute(block, 'pair', [(p, p ^ top) for p in range(peers)])  1.5 us
  transfers between devices with their start and end apart: 3, of which 3 were waited for; matrix products, arithmetic and copies ran while one was open for 3% of the time, Pallas kernels for 0%

profile of v10, /device:TPU:0, one launch (start us, length us, event | category | flops | bytes accessed | tf_op | source)
XLA Modules:
  0.0 64.4 jit_solution(5783084468569986113)
XLA Ops:
  0.0 2.4 %shard_map.28 = (bf16[384,1024]{1,0:T(8,128)(2,1)}, s32[1,128]{1,0:T(1,128)}) custom-call(f32[128,1024]{1,0:T(8,128)} %emb_ref.1, s32[1,128]{1,0:T(1,128)} %bitcast.20), custom_call_target="tpu_custom_call" | custom-call | flops 101187584 | bytes 1310720 | tf_op jit(solution)/shard_map/pallas_call | solution.py:64
  2.4 27.4 %all_to_all.10 = bf16[8,48,1024]{2,1,0:T(8,128)(2,1)S(1)} all-to-all(bf16[8,48,1024]{2,1,0:T(8,128)(2,1)} %bitcast.19), channel_id=1, replica_groups=mesh['dp'=8,'pair'=4] {'dp'}, dimensions={0} | all-to-all | bytes 1572864 | tf_op jit(solution)/shard_map/all_to_all | solution.py:109
  29.9 0.0 collective-permute-start.1
  29.9 1.5 %collective-permute-start = (bf16[8,48,1024]{2,1,0:T(8,128)(2,1)S(1)}, bf16[8,48,1024]{2,1,0:T(8,128)(2,1)S(1)}, u32[]{:S(2)}, u32[]{:S(2)}) collective-permute-start(bf16[8,48,1024]{2,1,0:T(8,128)(2,1)S(1)} %all_to_all.10), channel_id=1, source_target_pairs={{0,2},{1,3},{2,0},{3,1},{4,6},{5,7},{6,4},{7,5},{8,10},{9,11},{10,... | collective-permute-start | bytes 2359304 | tf_op jit(solution)/shard_map/ppermute | solution.py:111
  31.4 0.1 reshape.66
  31.5 0.6 fusion
  32.1 0.1 collective-permute-done.1
  32.2 0.1 reshape.67
  32.3 0.6 fusion.1
  32.9 16.9 %collective-permute-done = bf16[8,48,1024]{2,1,0:T(8,128)(2,1)S(1)} collective-permute-done((bf16[8,48,1024]{2,1,0:T(8,128)(2,1)S(1)}, bf16[8,48,1024]{2,1,0:T(8,128)(2,1)S(1)}, u32[]{:S(2)}, u32[]{:S(2)}) %collective-permute-start) | collective-permute-done | bytes 786464 | tf_op jit(solution)/shard_map/ppermute | solution.py:111
  49.8 0.0 collective-permute-start.2
  49.9 0.1 reshape.68
  49.9 0.6 fusion.2
  50.6 1.6 %collective-permute-done.2 = bf16[8,48,1024]{2,1,0:T(8,128)(2,1)S(1)} collective-permute-done((bf16[8,48,1024]{2,1,0:T(8,128)(2,1)S(1)}, bf16[8,48,1024]{2,1,0:T(8,128)(2,1)S(1)}, u32[]{:S(2)}, u32[]{:S(2)}) %collective-permute-start.2) | collective-permute-done | bytes 786464 | tf_op jit(solution)/shard_map/ppermute | solution.py:120
  52.1 0.1 reshape.69
  52.2 0.6 fusion.3
  52.8 0.1 reshape.65
  52.9 10.1 %all_to_all.11 = f32[8,8,128]{2,1,0:T(8,128)S(1)} all-to-all(f32[8,8,128]{2,1,0:T(8,128)S(1)} %pad.4), channel_id=1, replica_groups=mesh['dp'=8,'pair'=4] {'dp'}, dimensions={0} | all-to-all | bytes 65536 | tf_op jit(solution)/shard_map/all_to_all | solution.py:143
  63.0 0.1 broadcast_in_dim.29
  63.1 0.0 copy-start
  63.1 0.7 %copy-done = s32[1,128]{1,0:T(1,128)S(1)} copy-done((s32[1,128]{1,0:T(1,128)S(1)}, s32[1,128]{1,0:T(1,128)}, u32[]{:S(2)}) %copy-start) | copy-done | bytes 536
  63.8 0.6 select_reduce_fusion
  (9 shorter events, 0.1 us)
Async XLA Ops:
  29.9 2.3 %collective-permute-start.1 = (bf16[8,48,1024]{2,1,0:T(8,128)(2,1)S(1)}, bf16[8,48,1024]{2,1,0:T(8,128)(2,1)S(1)}, u32[]{:S(2)}, u32[]{:S(2)}) collective-permute-start(bf16[8,48,1024]{2,1,0:T(8,128)(2,1)S(1)} %all_to_all.10), channel_id=1, source_target_pairs={{0,1},{1,0},{2,3},{3,2},{4,5},{5,4},{6,7},{7,6},{8,9},{9,8},{10,11... | collective-permute-start | bytes 2359304 | tf_op jit(solution)/shard_map/ppermute | solution.py:120
  29.9 20.0 %collective-permute-start = (bf16[8,48,1024]{2,1,0:T(8,128)(2,1)S(1)}, bf16[8,48,1024]{2,1,0:T(8,128)(2,1)S(1)}, u32[]{:S(2)}, u32[]{:S(2)}) collective-permute-start(bf16[8,48,1024]{2,1,0:T(8,128)(2,1)S(1)} %all_to_all.10), channel_id=1, source_target_pairs={{0,2},{1,3},{2,0},{3,1},{4,6},{5,7},{6,4},{7,5},{8,10},{9,11},{10,... | collective-permute-start | bytes 2359304 | tf_op jit(solution)/shard_map/ppermute | solution.py:111
  49.8 2.3 %collective-permute-start.2 = (bf16[8,48,1024]{2,1,0:T(8,128)(2,1)S(1)}, bf16[8,48,1024]{2,1,0:T(8,128)(2,1)S(1)}, u32[]{:S(2)}, u32[]{:S(2)}) collective-permute-start(bf16[8,48,1024]{2,1,0:T(8,128)(2,1)S(1)} %collective-permute-done), channel_id=1, source_target_pairs={{0,1},{1,0},{2,3},{3,2},{4,5},{5,4},{6,7},{7,6},{8,9},{9,8},{10,11... | collective-permute-start | bytes 2359304 | tf_op jit(solution)/shard_map/ppermute | solution.py:120
  63.1 0.7 %copy-start = (s32[1,128]{1,0:T(1,128)S(1)}, s32[1,128]{1,0:T(1,128)}, u32[]{:S(2)}) copy-start(s32[1,128]{1,0:T(1,128)} %get-tuple-element.9) | copy-start | bytes 1540

commit v11 on v10

--- a/solution.py
+++ b/solution.py
@@ -108,9 +108,16 @@
         )
     block = lax.all_to_all(outgoing, "dp", split_axis=0, concat_axis=0, tiled=True)
     top = peers // 2
-    far = lax.ppermute(block, "pair", [(p, p ^ top) for p in range(peers)]) if top else None
     left = block.reshape(slots, width)
     left_labels = chunk_labels(block, capacity, chunk)
+    lanes = -(-chunk // 128) * 128
+    far = None
+    if top:
+        compact = (
+            block[:, :capacity, :].reshape(groups * capacity, width),
+            block[:, capacity, :lanes],
+        )
+        far = lax.ppermute(compact, "pair", [(p, p ^ top) for p in range(peers)])
 
     def spread(x):
         pieces = [x]
@@ -124,12 +131,14 @@
     def best_over(pieces, first_is_own):
         best = None
         for index, piece in enumerate(pieces):
+            if first_is_own:
+                right = piece.reshape(slots, width)
+                right_labels = chunk_labels(piece, capacity, chunk)
+            else:
+                right = piece[0]
+                right_labels = piece[1][:, :capacity].astype(jnp.int32).reshape(groups * capacity)
             piece_max = piece_best(
-                left,
-                left_labels,
-                piece.reshape(slots, width),
-                chunk_labels(piece, capacity, chunk),
-                first_is_own and index == 0,
+                left, left_labels, right, right_labels, first_is_own and index == 0
             )
             best = piece_max if best is None else jnp.maximum(best, piece_max)
         return best
@@ -138,7 +147,6 @@
     if far is not None:
         far, best = lax.optimization_barrier((far, best))
         best = jnp.maximum(best, best_over(spread(far), False))
-    lanes = -(-chunk // 128) * 128
     sent = jnp.pad(best.reshape(groups, 1, chunk), ((0, 0), (0, 7), (0, lanes - chunk)))
     returned = lax.all_to_all(sent, "dp", split_axis=0, concat_axis=0, tiled=True)
     returned = returned[:, 0, :chunk].reshape(slots)

time: 64.7 us -> 61.9 us (0.957)
  waiting for transfers between devices: 18.6 us -> 14.7 us
  starting transfers between devices: 1.5 us -> 2.67 us
    ppermute x1 -> x2, waiting for transfers between devices: 16.9 us -> 13.7 us  [shards(): far = lax.ppermute(compact, 'pair', [(p, p ^ top) for p in range(peers)])]
    ppermute x2 -> x3, waiting for transfers between devices: 1.62 us -> 0.96 us  [spread(): pieces = pieces + [lax.ppermute(y, 'pair', perm) for y in pieces]]
    ppermute x1 -> x2, starting transfers between devices: 1.5 us -> 2.16 us  [shards(): far = lax.ppermute(compact, 'pair', [(p, p ^ top) for p in range(peers)])]
  transfers between devices with their start and end apart: 3 -> 5, of which waited for: 3 -> 2; matrix products, arithmetic and copies ran while one was open for 3% -> 4% of each run, Pallas kernels for 0% -> 0%
where the time goes in v11:
time: 61.9 us; the launch traced here: 61.6 us
  blocking collectives  37.5 us (61%)
  waiting for transfers between devices  14.7 us (24%)
  starting transfers between devices  2.67 us (4%)
  Pallas kernels  2.45 us (4%)
  matrix products  2.32 us (4%)
  local copies, waits for them, and re-layouts  1.24 us (2%)
  other arithmetic  0.71 us (1%)
    all_to_all x1, blocking collectives, shards(): lax.all_to_all(outgoing, 'dp', split_axis=0, concat_axis=0, tiled=True)  27.4 us
    ppermute x2, waiting for transfers between devices, shards(): far = lax.ppermute(compact, 'pair', [(p, p ^ top) for p in range(peers)])  13.7 us
    all_to_all x1, blocking collectives, shards(): lax.all_to_all(sent, 'dp', split_axis=0, concat_axis=0, tiled=True)  10.1 us
    pallas_call x1, Pallas kernels, prepare(): pl.pallas_call(functools.partial(prepare_kernel, groups=groups, chunk=chu...  2.45 us
    dot_general x4, matrix products, piece_best(): jnp.einsum('id,jd->ij', left, right, preferred_element_type=jnp.float32)  2.32 us
    ppermute x2, starting transfers between devices, shards(): far = lax.ppermute(compact, 'pair', [(p, p ^ top) for p in range(peers)])  2.16 us
  transfers between devices with their start and end apart: 5, of which 2 were waited for; matrix products, arithmetic and copies ran while one was open for 4% of the time, Pallas kernels for 0%

profile of v11, /device:TPU:0, one launch (start us, length us, event | category | flops | bytes accessed | tf_op | source)
XLA Modules:
  0.0 61.6 jit_solution(9547693294993553226)
XLA Ops:
  0.0 2.4 %shard_map.28 = (bf16[384,1024]{1,0:T(8,128)(2,1)}, s32[1,128]{1,0:T(1,128)}) custom-call(f32[128,1024]{1,0:T(8,128)} %emb_ref.1, s32[1,128]{1,0:T(1,128)} %bitcast.24), custom_call_target="tpu_custom_call" | custom-call | flops 101187584 | bytes 1310720 | tf_op jit(solution)/shard_map/pallas_call | solution.py:64
  2.4 27.4 %all_to_all.10 = bf16[8,48,1024]{2,1,0:T(8,128)(2,1)S(1)} all-to-all(bf16[8,48,1024]{2,1,0:T(8,128)(2,1)} %bitcast.21), channel_id=1, replica_groups=mesh['dp'=8,'pair'=4] {'dp'}, dimensions={0} | all-to-all | bytes 1572864 | tf_op jit(solution)/shard_map/all_to_all | solution.py:109
  29.9 0.0 collective-permute-start.2
  29.9 0.1 reshape.50
  30.0 0.1 slice.29
  30.0 1.6 %collective-permute-start = (bf16[320,1024]{1,0:T(8,128)(2,1)S(1)}, bf16[320,1024]{1,0:T(8,128)(2,1)S(1)}, u32[]{:S(2)}, u32[]{:S(2)}) collective-permute-start(bf16[320,1024]{1,0:T(8,128)(2,1)S(1)} %bitcast.22), channel_id=1, source_target_pairs={{0,2},{1,3},{2,0},{3,1},{4,6},{5,7},{6,4},{7,5},{8,10},{9,11},{10,... | collective-permute-start | bytes 1966088 | tf_op jit(solution)/shard_map/ppermute | solution.py:120
  31.6 0.6 collective-permute-start.1
  32.2 0.6 %fusion = f32[384]{0:T(512)S(1)} fusion(bf16[384,1024]{1,0:T(8,128)(2,1)S(1)} %bitcast.17, s32[384]{0:T(512)S(1)} %reshape.50, pred[384]{0:T(512)(128)(4,1)S(1)} %broadcast_compare_fusion), kind=kOutput, calls=%fused_computation.4 | convolution fusion | flops 302874240 | bytes 789888 | tf_op jit(solution)/shard_map/id,jd->ij/dot_general | solution.py:17
  32.9 0.0 collective-permute-done.2
  32.9 0.1 reshape.51
  33.0 0.6 fusion.1
  33.6 13.7 %collective-permute-done.1 = bf16[8,128]{1,0:T(8,128)(2,1)S(1)} collective-permute-done((bf16[8,128]{1,0:T(8,128)(2,1)S(1)}, bf16[8,128]{1,0:T(8,128)(2,1)S(1)}, u32[]{:S(2)}, u32[]{:S(2)}) %collective-permute-start.1) | collective-permute-done | bytes 2080 | tf_op jit(solution)/shard_map/ppermute | solution.py:120
  47.3 0.0 collective-permute-done
  47.3 0.0 collective-permute-start.4
  47.3 0.5 collective-permute-start.3
  47.8 0.1 reshape.52
  47.9 0.5 fusion.2
  48.5 1.0 %collective-permute-done.3 = bf16[8,128]{1,0:T(8,128)(2,1)S(1)} collective-permute-done((bf16[8,128]{1,0:T(8,128)(2,1)S(1)}, bf16[8,128]{1,0:T(8,128)(2,1)S(1)}, u32[]{:S(2)}, u32[]{:S(2)}) %collective-permute-start.3) | collective-permute-done | bytes 2080 | tf_op jit(solution)/shard_map/ppermute | solution.py:127
  49.4 0.1 reshape.53
  49.5 0.0 collective-permute-done.4
  49.5 0.5 fusion.3
  50.1 0.1 reshape.49
  50.2 10.1 %all_to_all.11 = f32[8,8,128]{2,1,0:T(8,128)S(1)} all-to-all(f32[8,8,128]{2,1,0:T(8,128)S(1)} %pad.4), channel_id=1, replica_groups=mesh['dp'=8,'pair'=4] {'dp'}, dimensions={0} | all-to-all | bytes 65536 | tf_op jit(solution)/shard_map/all_to_all | solution.py:151
  60.2 0.1 broadcast_in_dim.33
  60.3 0.0 copy-start
  60.3 0.7 %copy-done = s32[1,128]{1,0:T(1,128)S(1)} copy-done((s32[1,128]{1,0:T(1,128)S(1)}, s32[1,128]{1,0:T(1,128)}, u32[]{:S(2)}) %copy-start) | copy-done | bytes 536
  61.0 0.6 %select_reduce_fusion = f32[128]{0:T(128)} fusion(f32[384]{0:T(512)S(1)} %broadcast_in_dim.33, s32[128]{0:T(128)S(1)} %bitcast.25), kind=kLoop, calls=%fused_computation.10 | loop fusion | flops 147328 | bytes 2560 | tf_op jit(solution)/shard_map/reduce_sum | solution.py:153
  (11 shorter events, 0.1 us)
Async XLA Ops:
  29.9 3.0 %collective-permute-start.2 = (bf16[8,48,1024]{2,1,0:T(8,128)(2,1)S(1)}, bf16[8,48,1024]{2,1,0:T(8,128)(2,1)S(1)}, u32[]{:S(2)}, u32[]{:S(2)}) collective-permute-start(bf16[8,48,1024]{2,1,0:T(8,128)(2,1)S(1)} %all_to_all.10), channel_id=1, source_target_pairs={{0,1},{1,0},{2,3},{3,2},{4,5},{5,4},{6,7},{7,6},{8,9},{9,8},{10,11... | collective-permute-start | bytes 2359304 | tf_op jit(solution)/shard_map/ppermute | solution.py:127
  30.0 17.3 %collective-permute-start = (bf16[320,1024]{1,0:T(8,128)(2,1)S(1)}, bf16[320,1024]{1,0:T(8,128)(2,1)S(1)}, u32[]{:S(2)}, u32[]{:S(2)}) collective-permute-start(bf16[320,1024]{1,0:T(8,128)(2,1)S(1)} %bitcast.22), channel_id=1, source_target_pairs={{0,2},{1,3},{2,0},{3,1},{4,6},{5,7},{6,4},{7,5},{8,10},{9,11},{10,... | collective-permute-start | bytes 1966088 | tf_op jit(solution)/shard_map/ppermute | solution.py:120
  31.6 15.7 %collective-permute-start.1 = (bf16[8,128]{1,0:T(8,128)(2,1)S(1)}, bf16[8,128]{1,0:T(8,128)(2,1)S(1)}, u32[]{:S(2)}, u32[]{:S(2)}) collective-permute-start(bf16[8,128]{1,0:T(8,128)(2,1)S(1)} %bitcast.23), channel_id=1, source_target_pairs={{0,2},{1,3},{2,0},{3,1},{4,6},{5,7},{6,4},{7,5},{8,10},{9,11},{10,... | collective-permute-start | bytes 6152 | tf_op jit(solution)/shard_map/ppermute | solution.py:120
  47.3 2.2 %collective-permute-start.4 = (bf16[320,1024]{1,0:T(8,128)(2,1)S(1)}, bf16[320,1024]{1,0:T(8,128)(2,1)S(1)}, u32[]{:S(2)}, u32[]{:S(2)}) collective-permute-start(bf16[320,1024]{1,0:T(8,128)(2,1)S(1)} %collective-permute-done), channel_id=1, source_target_pairs={{0,1},{1,0},{2,3},{3,2},{4,5},{5,4},{6,7},{7,6},{8,9},{9,8},{10,11... | collective-permute-start | bytes 1966088 | tf_op jit(solution)/shard_map/ppermute | solution.py:127
  47.3 2.1 %collective-permute-start.3 = (bf16[8,128]{1,0:T(8,128)(2,1)S(1)}, bf16[8,128]{1,0:T(8,128)(2,1)S(1)}, u32[]{:S(2)}, u32[]{:S(2)}) collective-permute-start(bf16[8,128]{1,0:T(8,128)(2,1)S(1)} %collective-permute-done.1), channel_id=1, source_target_pairs={{0,1},{1,0},{2,3},{3,2},{4,5},{5,4},{6,7},{7,6},{8,9},{9,8},{10,11... | collective-permute-start | bytes 6152 | tf_op jit(solution)/shard_map/ppermute | solution.py:127
  60.3 0.7 %copy-start = (s32[1,128]{1,0:T(1,128)S(1)}, s32[1,128]{1,0:T(1,128)}, u32[]{:S(2)}) copy-start(s32[1,128]{1,0:T(1,128)} %get-tuple-element.10) | copy-start | bytes 1540

commit v12 on v11

--- a/solution.py
+++ b/solution.py
@@ -106,18 +106,26 @@
         outgoing = jnp.where(
             (row_id == capacity)[None, :, None], tag_row.astype(jnp.bfloat16)[:, None, :], outgoing
         )
+    top = peers // 2
+    lanes = -(-chunk // 128) * 128
+    me = lax.axis_index("dp")
+    pair_perm = [(p, p ^ top) for p in range(peers)]
+    early = None
+    if top:
+        own = lax.dynamic_index_in_dim(outgoing, me, axis=0, keepdims=False)
+        early = lax.ppermute((own[:capacity], own[capacity:capacity + 1, :lanes]), "pair", pair_perm)
     block = lax.all_to_all(outgoing, "dp", split_axis=0, concat_axis=0, tiled=True)
-    top = peers // 2
     left = block.reshape(slots, width)
     left_labels = chunk_labels(block, capacity, chunk)
-    lanes = -(-chunk // 128) * 128
-    far = None
+    late = None
     if top:
-        compact = (
-            block[:, :capacity, :].reshape(groups * capacity, width),
-            block[:, capacity, :lanes],
+        others = (me + 1 + jnp.arange(groups - 1, dtype=jnp.int32)) % groups
+        rest = block[others]
+        late = (
+            rest[:, :capacity, :].reshape((groups - 1) * capacity, width),
+            rest[:, capacity, :lanes],
         )
-        far = lax.ppermute(compact, "pair", [(p, p ^ top) for p in range(peers)])
+        late = lax.ppermute(late, "pair", pair_perm)
 
     def spread(x):
         pieces = [x]
@@ -136,7 +144,7 @@
                 right_labels = chunk_labels(piece, capacity, chunk)
             else:
                 right = piece[0]
-                right_labels = piece[1][:, :capacity].astype(jnp.int32).reshape(groups * capacity)
+                right_labels = piece[1][:, :capacity].astype(jnp.int32).reshape(right.shape[0])
             piece_max = piece_best(
                 left, left_labels, right, right_labels, first_is_own and index == 0
             )
@@ -144,9 +152,10 @@
         return best
 
     best = best_over(spread(block), True)
-    if far is not None:
-        far, best = lax.optimization_barrier((far, best))
-        best = jnp.maximum(best, best_over(spread(far), False))
+    if top:
+        best = jnp.maximum(best, best_over(spread(early), False))
+        late, best = lax.optimization_barrier((late, best))
+        best = jnp.maximum(best, best_over(spread(late), False))
     sent = jnp.pad(best.reshape(groups, 1, chunk), ((0, 0), (0, 7), (0, lanes - chunk)))
     returned = lax.all_to_all(sent, "dp", split_axis=0, concat_axis=0, tiled=True)
     returned = returned[:, 0, :chunk].reshape(slots)

time: 61.9 us -> 61.9 us (level)
  blocking collectives: 37.5 us -> 10.1 us
  waiting for transfers between devices: 14.7 us -> 29.6 us
  starting transfers between devices: 2.67 us -> 12 us
  local copies, waits for them, and re-layouts: 1.24 us -> 3.61 us
  matrix products: 2.32 us -> 2.94 us
    all_to_all x1 -> x0, blocking collectives: 27.4 us -> none  [shards(): lax.all_to_all(outgoing, 'dp', split_axis=0, concat_axis=0, tiled=True)]
    all_to_all x0 -> x1, waiting for transfers between devices: none -> 12.4 us  [shards(): lax.all_to_all(outgoing, 'dp', split_axis=0, concat_axis=0, tiled=True)]
    all_to_all x0 -> x1, starting transfers between devices: none -> 7.29 us  [shards(): lax.all_to_all(outgoing, 'dp', split_axis=0, concat_axis=0, tiled=True)]
    ppermute x2 -> x4, starting transfers between devices: 2.16 us -> 4.18 us  [the longest x2 2.09 us: shards(): lax.ppermute((own[:capacity], own[capacity:capacity + 1, :lanes]), 'pair'...]
    ppermute x2 -> x4, waiting for transfers between devices: 13.7 us -> 15.2 us  [the longest x2 12.5 us: shards(): late = lax.ppermute(late, 'pair', pair_perm)]
    ppermute x3 -> x5, waiting for transfers between devices: 0.96 us -> 2.05 us  [spread(): pieces = pieces + [lax.ppermute(y, 'pair', perm) for y in pieces]]
    squeeze x0 -> x1, local copies, waits for them, and re-layouts: none -> 0.9 us  [shards(): own = lax.dynamic_index_in_dim(outgoing, me, axis=0, keepdims=False)]
    slice x2 -> x4, local copies, waits for them, and re-layouts: 0.06 us -> 0.94 us  [the longest x1 0.89 us: shards(): own[:capacity]]
  transfers between devices with their start and end apart: 5 -> 10, of which waited for: 2 -> 7; matrix products, arithmetic and copies ran while one was open for 4% -> 9% of each run, Pallas kernels for 0% -> 0%
where the time goes in v12:
time: 61.9 us; the launch traced here: 61.6 us
  waiting for transfers between devices  29.6 us (48%)
  starting transfers between devices  12 us (19%)
  blocking collectives  10.1 us (16%)
  local copies, waits for them, and re-layouts  3.61 us (6%)
  matrix products  2.94 us (5%)
  Pallas kernels  2.45 us (4%)
  other arithmetic  0.74 us (1%)
    ppermute x2, waiting for transfers between devices, shards(): late = lax.ppermute(late, 'pair', pair_perm)  12.5 us
    all_to_all x1, waiting for transfers between devices, shards(): lax.all_to_all(outgoing, 'dp', split_axis=0, concat_axis=0, tiled=True)  12.4 us
    all_to_all x1, blocking collectives, shards(): lax.all_to_all(sent, 'dp', split_axis=0, concat_axis=0, tiled=True)  10.1 us
    all_to_all x1, starting transfers between devices, shards(): lax.all_to_all(outgoing, 'dp', split_axis=0, concat_axis=0, tiled=True)  7.29 us
    dot_general x6, matrix products, piece_best(): jnp.einsum('id,jd->ij', left, right, preferred_element_type=jnp.float32)  2.94 us
    ppermute x2, waiting for transfers between devices, shards(): lax.ppermute((own[:capacity], own[capacity:capacity + 1, :lanes]), 'pair'...  2.75 us
    pallas_call x1, Pallas kernels, prepare(): pl.pallas_call(functools.partial(prepare_kernel, groups=groups, chunk=chu...  2.45 us
    ppermute x2, starting transfers between devices, shards(): lax.ppermute((own[:capacity], own[capacity:capacity + 1, :lanes]), 'pair'...  2.09 us
  transfers between devices with their start and end apart: 10, of which 7 were waited for; matrix products, arithmetic and copies ran while one was open for 9% of the time, Pallas kernels for 0%

profile of v12, /device:TPU:0, one launch (start us, length us, event | category | flops | bytes accessed | tf_op | source)
XLA Modules:
  0.0 61.6 jit_solution(12409032139424275049)
XLA Ops:
  0.0 2.4 %shard_map.28 = (bf16[384,1024]{1,0:T(8,128)(2,1)}, s32[1,128]{1,0:T(1,128)}) custom-call(f32[128,1024]{1,0:T(8,128)} %emb_ref.1, s32[1,128]{1,0:T(1,128)} %bitcast.44), custom_call_target="tpu_custom_call" | custom-call | flops 101187584 | bytes 1310720 | tf_op jit(solution)/shard_map/pallas_call | solution.py:64
  2.4 7.3 %all-to-all-start = ((bf16[8,48,1024]{2,1,0:T(8,128)(2,1)}), bf16[8,48,1024]{2,1,0:T(8,128)(2,1)S(1)}, u32[]{:S(2)}, u32[]{:S(2)}) async-start(bf16[8,48,1024]{2,1,0:T(8,128)(2,1)} %bitcast.39), calls=%async_computation | async-start | bytes 1572864 | tf_op jit(solution)/shard_map/all_to_all | solution.py:117
  9.7 0.9 %dynamic-slice_bitcast_fusion = bf16[48,1024]{1,0:T(8,128)(2,1)S(1)} fusion(bf16[8,48,1024]{2,1,0:T(8,128)(2,1)} %bitcast.40, s32[]{:T(128)S(6)} %select_n.57), kind=kLoop, calls=%fused_computation.17 | loop fusion | bytes 196612 | tf_op jit(solution)/shard_map/jit(dynamic_index_in_dim)/squeeze | solution.py:115
  10.6 1.6 %collective-permute-start.3 = (bf16[1,128]{1,0:T(2,128)(2,1)S(1)}, bf16[1,128]{1,0:T(2,128)(2,1)S(1)}, u32[]{:S(2)}, u32[]{:S(2)}) collective-permute-start(bf16[1,128]{1,0:T(2,128)(2,1)S(1)} %slice.55), channel_id=1, source_target_pairs={{0,2},{1,3},{2,0},{3,1},{4,6},{5,7},{6,4},{7,5},{8,10},{9,11},{10,... | collective-permute-start | bytes 776 | tf_op jit(solution)/shard_map/ppermute | solution.py:116
  12.2 0.9 %dynamic-slice_bitcast_fusion.1 = bf16[40,1024]{1,0:T(8,128)(2,1)S(1)} fusion(bf16[8,48,1024]{2,1,0:T(8,128)(2,1)} %bitcast.41, s32[]{:T(128)S(6)} %select_n.57), kind=kLoop, calls=%fused_computation.18 | loop fusion | bytes 163844 | tf_op jit(solution)/shard_map/slice | solution.py:116
  13.1 0.5 collective-permute-start.4
  13.7 0.6 collective-permute-done.3
  14.3 0.0 collective-permute-start.5
  14.3 1.1 %collective-permute-done.5 = bf16[1,128]{1,0:T(2,128)(2,1)S(1)} collective-permute-done((bf16[1,128]{1,0:T(2,128)(2,1)S(1)}, bf16[1,128]{1,0:T(2,128)(2,1)S(1)}, u32[]{:S(2)}, u32[]{:S(2)}) %collective-permute-start.5) | collective-permute-done | bytes 288 | tf_op jit(solution)/shard_map/ppermute | solution.py:135
  15.4 2.2 %collective-permute-done.4 = bf16[40,1024]{1,0:T(8,128)(2,1)S(1)} collective-permute-done((bf16[40,1024]{1,0:T(8,128)(2,1)S(1)}, bf16[40,1024]{1,0:T(8,128)(2,1)S(1)}, u32[]{:S(2)}, u32[]{:S(2)}) %collective-permute-start.4) | collective-permute-done | bytes 81952 | tf_op jit(solution)/shard_map/ppermute | solution.py:116
  17.5 0.0 collective-permute-start.6
  17.5 12.4 %all-to-all-done = bf16[8,48,1024]{2,1,0:T(8,128)(2,1)S(1)} async-done(((bf16[8,48,1024]{2,1,0:T(8,128)(2,1)}), bf16[8,48,1024]{2,1,0:T(8,128)(2,1)S(1)}, u32[]{:S(2)}, u32[]{:S(2)}) %all-to-all-start) | async-done | bytes 786464 | tf_op jit(solution)/shard_map/all_to_all | solution.py:117
  29.9 0.0 collective-permute-start.2
  29.9 0.6 gather_fusion
  30.6 0.1 reshape.100
  30.7 1.6 %collective-permute-start.1 = (bf16[7,128]{1,0:T(8,128)(2,1)S(1)}, bf16[7,128]{1,0:T(8,128)(2,1)S(1)}, u32[]{:S(2)}, u32[]{:S(2)}) collective-permute-start(bf16[7,128]{1,0:T(8,128)(2,1)S(1)} %bitcast.43), channel_id=1, source_target_pairs={{0,2},{1,3},{2,0},{3,1},{4,6},{5,7},{6,4},{7,5},{8,10},{9,11},{10,... | collective-permute-start | bytes 5384 | tf_op jit(solution)/shard_map/ppermute | solution.py:128
  32.2 0.5 collective-permute-start
  32.8 0.6 fusion
  33.4 0.4 fusion.4
  33.8 0.0 collective-permute-done.6
  33.8 0.4 fusion.5
  34.1 0.0 collective-permute-done.2
  34.2 0.1 reshape.101
  34.3 0.6 fusion.1
  34.9 0.0 collective-permute-done.1
  34.9 12.5 %collective-permute-done = bf16[280,1024]{1,0:T(8,128)(2,1)S(1)} collective-permute-done((bf16[280,1024]{1,0:T(8,128)(2,1)S(1)}, bf16[280,1024]{1,0:T(8,128)(2,1)S(1)}, u32[]{:S(2)}, u32[]{:S(2)}) %collective-permute-start) | collective-permute-done | bytes 573472 | tf_op jit(solution)/shard_map/ppermute | solution.py:128
  47.4 0.0 collective-permute-start.7
  47.4 0.5 collective-permute-start.8
  47.9 0.1 reshape.104
  48.0 0.5 fusion.2
  48.5 0.1 collective-permute-done.7
  48.5 0.1 reshape.105
  48.6 0.9 %collective-permute-done.8 = bf16[280,1024]{1,0:T(8,128)(2,1)S(1)} collective-permute-done((bf16[280,1024]{1,0:T(8,128)(2,1)S(1)}, bf16[280,1024]{1,0:T(8,128)(2,1)S(1)}, u32[]{:S(2)}, u32[]{:S(2)}) %collective-permute-start.8) | collective-permute-done | bytes 573472 | tf_op jit(solution)/shard_map/ppermute | solution.py:135
  49.5 0.5 fusion.3
  50.0 0.1 reshape.99
  50.1 10.1 %all_to_all.10 = f32[8,8,128]{2,1,0:T(8,128)S(1)} all-to-all(f32[8,8,128]{2,1,0:T(8,128)S(1)} %pad.4), channel_id=1, replica_groups=mesh['dp'=8,'pair'=4] {'dp'}, dimensions={0} | all-to-all | bytes 65536 | tf_op jit(solution)/shard_map/all_to_all | solution.py:160
  60.2 0.1 broadcast_in_dim.40
  60.3 0.0 copy-start
  60.3 0.7 %copy-done = s32[1,128]{1,0:T(1,128)S(1)} copy-done((s32[1,128]{1,0:T(1,128)S(1)}, s32[1,128]{1,0:T(1,128)}, u32[]{:S(2)}) %copy-start) | copy-done | bytes 536
  60.9 0.6 %select_reduce_fusion = f32[128]{0:T(128)} fusion(f32[384]{0:T(512)S(1)} %broadcast_in_dim.40, s32[128]{0:T(128)S(1)} %bitcast.45), kind=kLoop, calls=%fused_computation.15 | loop fusion | flops 147328 | bytes 2560 | tf_op jit(solution)/shard_map/reduce_sum | solution.py:162
  (17 shorter events, 0.2 us)
Async XLA Ops:
  2.4 27.5 %all-to-all-start = ((bf16[8,48,1024]{2,1,0:T(8,128)(2,1)}), bf16[8,48,1024]{2,1,0:T(8,128)(2,1)S(1)}, u32[]{:S(2)}, u32[]{:S(2)}) async-start(bf16[8,48,1024]{2,1,0:T(8,128)(2,1)} %bitcast.39), calls=%async_computation | async-start | bytes 1572864 | tf_op jit(solution)/shard_map/all_to_all | solution.py:117
  10.6 3.6 %collective-permute-start.3 = (bf16[1,128]{1,0:T(2,128)(2,1)S(1)}, bf16[1,128]{1,0:T(2,128)(2,1)S(1)}, u32[]{:S(2)}, u32[]{:S(2)}) collective-permute-start(bf16[1,128]{1,0:T(2,128)(2,1)S(1)} %slice.55), channel_id=1, source_target_pairs={{0,2},{1,3},{2,0},{3,1},{4,6},{5,7},{6,4},{7,5},{8,10},{9,11},{10,... | collective-permute-start | bytes 776 | tf_op jit(solution)/shard_map/ppermute | solution.py:116
  13.1 4.4 %collective-permute-start.4 = (bf16[40,1024]{1,0:T(8,128)(2,1)S(1)}, bf16[40,1024]{1,0:T(8,128)(2,1)S(1)}, u32[]{:S(2)}, u32[]{:S(2)}) collective-permute-start(bf16[40,1024]{1,0:T(8,128)(2,1)S(1)} %dynamic-slice_bitcast_fusion.1), channel_id=1, source_target_pairs={{0,2},{1,3},{2,0},{3,1},{4,6},{5,7},{6,4},{7,5},{8,10},{9,11},{10,... | collective-permute-start | bytes 245768 | tf_op jit(solution)/shard_map/ppermute | solution.py:116
  14.3 1.1 %collective-permute-start.5 = (bf16[1,128]{1,0:T(2,128)(2,1)S(1)}, bf16[1,128]{1,0:T(2,128)(2,1)S(1)}, u32[]{:S(2)}, u32[]{:S(2)}) collective-permute-start(bf16[1,128]{1,0:T(2,128)(2,1)S(1)} %collective-permute-done.3), channel_id=1, source_target_pairs={{0,1},{1,0},{2,3},{3,2},{4,5},{5,4},{6,7},{7,6},{8,9},{9,8},{10,11... | collective-permute-start | bytes 776 | tf_op jit(solution)/shard_map/ppermute | solution.py:135
  17.5 16.2 %collective-permute-start.6 = (bf16[40,1024]{1,0:T(8,128)(2,1)S(1)}, bf16[40,1024]{1,0:T(8,128)(2,1)S(1)}, u32[]{:S(2)}, u32[]{:S(2)}) collective-permute-start(bf16[40,1024]{1,0:T(8,128)(2,1)S(1)} %collective-permute-done.4), channel_id=1, source_target_pairs={{0,1},{1,0},{2,3},{3,2},{4,5},{5,4},{6,7},{7,6},{8,9},{9,8},{10,11... | collective-permute-start | bytes 245768 | tf_op jit(solution)/shard_map/ppermute | solution.py:135
  29.9 4.2 %collective-permute-start.2 = (bf16[8,48,1024]{2,1,0:T(8,128)(2,1)S(1)}, bf16[8,48,1024]{2,1,0:T(8,128)(2,1)S(1)}, u32[]{:S(2)}, u32[]{:S(2)}) collective-permute-start(bf16[8,48,1024]{2,1,0:T(8,128)(2,1)S(1)} %all-to-all-done), channel_id=1, source_target_pairs={{0,1},{1,0},{2,3},{3,2},{4,5},{5,4},{6,7},{7,6},{8,9},{9,8},{10,11... | collective-permute-start | bytes 2359304 | tf_op jit(solution)/shard_map/ppermute | solution.py:135
  30.7 4.2 %collective-permute-start.1 = (bf16[7,128]{1,0:T(8,128)(2,1)S(1)}, bf16[7,128]{1,0:T(8,128)(2,1)S(1)}, u32[]{:S(2)}, u32[]{:S(2)}) collective-permute-start(bf16[7,128]{1,0:T(8,128)(2,1)S(1)} %bitcast.43), channel_id=1, source_target_pairs={{0,2},{1,3},{2,0},{3,1},{4,6},{5,7},{6,4},{7,5},{8,10},{9,11},{10,... | collective-permute-start | bytes 5384 | tf_op jit(solution)/shard_map/ppermute | solution.py:128
  32.2 15.1 %collective-permute-start = (bf16[280,1024]{1,0:T(8,128)(2,1)S(1)}, bf16[280,1024]{1,0:T(8,128)(2,1)S(1)}, u32[]{:S(2)}, u32[]{:S(2)}) collective-permute-start(bf16[280,1024]{1,0:T(8,128)(2,1)S(1)} %bitcast.42), channel_id=1, source_target_pairs={{0,2},{1,3},{2,0},{3,1},{4,6},{5,7},{6,4},{7,5},{8,10},{9,11},{10,... | collective-permute-start | bytes 1720328 | tf_op jit(solution)/shard_map/ppermute | solution.py:128
  47.4 1.2 %collective-permute-start.7 = (bf16[7,128]{1,0:T(8,128)(2,1)S(1)}, bf16[7,128]{1,0:T(8,128)(2,1)S(1)}, u32[]{:S(2)}, u32[]{:S(2)}) collective-permute-start(bf16[7,128]{1,0:T(8,128)(2,1)S(1)} %collective-permute-done.1), channel_id=1, source_target_pairs={{0,1},{1,0},{2,3},{3,2},{4,5},{5,4},{6,7},{7,6},{8,9},{9,8},{10,11... | collective-permute-start | bytes 5384 | tf_op jit(solution)/shard_map/ppermute | solution.py:135
  47.4 2.1 %collective-permute-start.8 = (bf16[280,1024]{1,0:T(8,128)(2,1)S(1)}, bf16[280,1024]{1,0:T(8,128)(2,1)S(1)}, u32[]{:S(2)}, u32[]{:S(2)}) collective-permute-start(bf16[280,1024]{1,0:T(8,128)(2,1)S(1)} %collective-permute-done), channel_id=1, source_target_pairs={{0,1},{1,0},{2,3},{3,2},{4,5},{5,4},{6,7},{7,6},{8,9},{9,8},{10,11... | collective-permute-start | bytes 1720328 | tf_op jit(solution)/shard_map/ppermute | solution.py:135
  60.3 0.7 %copy-start = (s32[1,128]{1,0:T(1,128)S(1)}, s32[1,128]{1,0:T(1,128)}, u32[]{:S(2)}) copy-start(s32[1,128]{1,0:T(1,128)} %get-tuple-element.10) | copy-start | bytes 1540

commit v13 on v10

v13 whole, which is shorter than its diff:
```python
import functools

import jax
import jax.numpy as jnp
from jax import lax
from jax.experimental import pallas as pl
from jax.experimental.pallas import tpu as pltpu
from jax.sharding import PartitionSpec as P

CPO = 4


floor_value = -2.0


def piece_best(left, left_labels, right, right_labels, exclude_self):
    score = jnp.einsum("id,jd->ij", left, right, preferred_element_type=jnp.float32)
    same = (left_labels[:, None] == right_labels[None, :]) & (left_labels[:, None] >= 0)
    if exclude_self:
        lane = jnp.arange(left.shape[0], dtype=jnp.int32)
        same = same & (lane[:, None] != lane[None, :])
    return jnp.max(jnp.where(same, score, floor_value), axis=1)


def prepare_kernel(emb_ref, lrow_ref, out_ref, slot_ref, *, groups, capacity):
    rows, width = emb_ref.shape
    slots = groups * capacity
    shift = CPO.bit_length() - 1
    e = emb_ref[...]
    norm = jnp.sqrt(jnp.sum(e * e, axis=1, keepdims=True) + 1e-06)
    unit = (e * (1.0 / norm)).astype(jnp.bfloat16)
    lrow = lrow_ref[...]
    orow = lax.shift_right_logical(lrow, shift)
    first = lax.broadcasted_iota(jnp.int32, (rows, rows), 0)
    second = lax.broadcasted_iota(jnp.int32, (rows, rows), 1)
    diagonal = first == second
    ocol = jnp.sum(jnp.where(diagonal, orow, 0), axis=1, keepdims=True)
    lcol = jnp.sum(jnp.where(diagonal, lrow, 0), axis=1, keepdims=True)
    same = ocol == orow
    rank_row = jnp.sum(jnp.where(same & (first < second), 1, 0), axis=0, keepdims=True)
    slot_row = orow * capacity + rank_row
    slot_ref[...] = slot_row
    place = (lax.broadcasted_iota(jnp.int32, (slots, rows), 0) == slot_row).astype(jnp.bfloat16)
    out_ref[:, :width] = jnp.dot(place, unit, preferred_element_type=jnp.float32).astype(jnp.bfloat16)
    tag_source = jnp.where(
        lax.broadcasted_iota(jnp.int32, (rows, 128), 1) == 0, jnp.bitwise_and(lcol, CPO - 1) + 1, 0
    ).astype(jnp.bfloat16)
    tags = jnp.dot(place, tag_source, preferred_element_type=jnp.float32) - 1.0
    out_ref[:, width:] = tags.astype(jnp.bfloat16)


def prepare(embeddings, labels, groups, capacity):
    rows, width = embeddings.shape
    slots = groups * capacity
    vmem = pltpu.MemorySpace.VMEM
    return pl.pallas_call(
        functools.partial(prepare_kernel, groups=groups, capacity=capacity),
        out_shape=(
            jax.ShapeDtypeStruct((slots, width + 128), jnp.bfloat16),
            jax.ShapeDtypeStruct((1, rows), jnp.int32),
        ),
        in_specs=[pl.BlockSpec(memory_space=vmem)] * 2,
        out_specs=(pl.BlockSpec(memory_space=vmem), pl.BlockSpec(memory_space=vmem)),
        cost_estimate=pl.CostEstimate(
            flops=2 * slots * rows * (width + 128) + 4 * rows * width,
            transcendentals=rows,
            bytes_accessed=rows * width * 4 + slots * (width + 128) * 2,
        ),
    )(embeddings, labels[None, :])


def shards(embeddings, labels):
    rows, width = embeddings.shape
    groups = lax.axis_size("dp")
    peers = lax.axis_size("pair")
    capacity = 5 * rows // (2 * groups)
    slots = groups * capacity
    if groups <= 16:
        outgoing, slot = prepare(embeddings, labels, groups, capacity)
        slot = slot.reshape(rows)
    else:
        norm = jnp.sqrt(jnp.sum(embeddings * embeddings, axis=1, keepdims=True) + 1e-06)
        unit = (embeddings / norm).astype(jnp.bfloat16)
        owner = lax.shift_right_logical(labels, CPO.bit_length() - 1)
        local = jnp.bitwise_and(labels, CPO - 1)
        onehot = (owner[:, None] == jnp.arange(groups, dtype=jnp.int32)[None, :]).astype(jnp.int32)
        rank = jnp.sum(jnp.cumsum(onehot, axis=0) * onehot, axis=1) - 1
        slot = owner * capacity + rank
        tag_source = jnp.zeros((rows, 128), jnp.bfloat16).at[:, 0].set((local + 1).astype(jnp.bfloat16))
        source = jnp.concatenate([unit, tag_source], axis=1)
        place = slot[None, :] == jnp.arange(slots, dtype=jnp.int32)[:, None]
        outgoing = jnp.dot(place.astype(jnp.bfloat16), source, preferred_element_type=jnp.float32)
        outgoing = (outgoing - jnp.where(jnp.arange(width + 128) >= width, 1.0, 0.0)).astype(jnp.bfloat16)
    place = slot[None, :] == jnp.arange(slots, dtype=jnp.int32)[:, None]
    outgoing = outgoing.reshape(groups, capacity, width + 128)
    block = lax.all_to_all(outgoing, "dp", split_axis=0, concat_axis=0, tiled=True)
    block = block.reshape(slots, width + 128)
    top = peers // 2
    own = (block[:, :width], block[:, width])
    far = lax.ppermute(own, "pair", [(p, p ^ top) for p in range(peers)]) if top else None

    def spread(x):
        pieces = [x]
        bit = top // 2
        while bit >= 1:
            perm = [(p, p ^ bit) for p in range(peers)]
            pieces = pieces + [lax.ppermute(y, "pair", perm) for y in pieces]
            bit //= 2
        return pieces

    left, left_tags = own
    left_labels = left_tags.astype(jnp.int32)

    def best_over(pieces, first_is_own):
        best = None
        for index, (right, right_tags) in enumerate(pieces):
            piece_max = piece_best(
                left, left_labels, right, right_tags.astype(jnp.int32), first_is_own and index == 0
            )
            best = piece_max if best is None else jnp.maximum(best, piece_max)
        return best

    best = best_over(spread(own), True)
    if far is not None:
        far, best = lax.optimization_barrier((far, best))
        best = jnp.maximum(best, best_over(spread(far), False))
    lanes = -(-capacity // 128) * 128
    sent = jnp.pad(best.reshape(groups, 1, capacity), ((0, 0), (0, 7), (0, lanes - capacity)))
    returned = lax.all_to_all(sent, "dp", split_axis=0, concat_axis=0, tiled=True)
    returned = returned[:, 0, :capacity].reshape(slots)
    return jnp.sum(jnp.where(place, returned[:, None], 0.0), axis=0)


def solution(mesh):
    in_specs = (P(("dp", "pair"), None), P(("dp", "pair")))
    out_specs = P(("dp", "pair"))
    return jax.shard_map(shards, mesh=mesh, in_specs=in_specs, out_specs=out_specs, check_vma=False)
```

time: 64.7 us -> 60.6 us (0.937)
  waiting for transfers between devices: 18.6 us -> 14.4 us
  starting transfers between devices: 1.5 us -> 2.9 us
  blocking collectives: 37.5 us -> 36.4 us
    ppermute x1 -> x2, waiting for transfers between devices: 16.9 us -> 13.3 us  [shards(): lax.ppermute(own, 'pair', [(p, p ^ top) for p in range(peers)])]
    all_to_all x1, blocking collectives: 27.4 us -> 26.4 us  [shards(): lax.all_to_all(outgoing, 'dp', split_axis=0, concat_axis=0, tiled=True)]
    ppermute x2 -> x4, starting transfers between devices: 0.01 us -> 0.81 us  [spread(): pieces = pieces + [lax.ppermute(y, 'pair', perm) for y in pieces]]
    ppermute x1 -> x2, starting transfers between devices: 1.5 us -> 2.09 us  [shards(): lax.ppermute(own, 'pair', [(p, p ^ top) for p in range(peers)])]
    ppermute x2 -> x4, waiting for transfers between devices: 1.62 us -> 1.05 us  [spread(): pieces = pieces + [lax.ppermute(y, 'pair', perm) for y in pieces]]
  transfers between devices with their start and end apart: 3 -> 6, of which waited for: 3 -> 2; matrix products, arithmetic and copies ran while one was open for 3% -> 3% of each run, Pallas kernels for 0% -> 0%
where the time goes in v13:
time: 60.6 us; the launch traced here: 60.4 us
  blocking collectives  36.4 us (60%)
  waiting for transfers between devices  14.4 us (24%)
  starting transfers between devices  2.9 us (5%)
  Pallas kernels  2.41 us (4%)
  matrix products  2.16 us (4%)
  local copies, waits for them, and re-layouts  1.03 us (2%)
  other arithmetic  0.97 us (2%)
    all_to_all x1, blocking collectives, shards(): lax.all_to_all(outgoing, 'dp', split_axis=0, concat_axis=0, tiled=True)  26.4 us
    ppermute x2, waiting for transfers between devices, shards(): lax.ppermute(own, 'pair', [(p, p ^ top) for p in range(peers)])  13.3 us
    all_to_all x1, blocking collectives, shards(): lax.all_to_all(sent, 'dp', split_axis=0, concat_axis=0, tiled=True)  10 us
    pallas_call x1, Pallas kernels, prepare(): pl.pallas_call(functools.partial(prepare_kernel, groups=groups, capacity=...  2.41 us
    dot_general x4, matrix products, piece_best(): jnp.einsum('id,jd->ij', left, right, preferred_element_type=jnp.float32)  2.16 us
    ppermute x2, starting transfers between devices, shards(): lax.ppermute(own, 'pair', [(p, p ^ top) for p in range(peers)])  2.09 us
  transfers between devices with their start and end apart: 6, of which 2 were waited for; matrix products, arithmetic and copies ran while one was open for 3% of the time, Pallas kernels for 0%

profile of v13, /device:TPU:0, one launch (start us, length us, event | category | flops | bytes accessed | tf_op | source)
XLA Modules:
  0.0 60.4 jit_solution(10154239885664945019)
XLA Ops:
  0.0 2.4 %shard_map.28 = (bf16[320,1152]{1,0:T(8,128)(2,1)}, s32[1,128]{1,0:T(1,128)}) custom-call(f32[128,1024]{1,0:T(8,128)} %emb_ref.1, s32[1,128]{1,0:T(1,128)} %bitcast.16), custom_call_target="tpu_custom_call" | custom-call | flops 94896128 | bytes 1261568 | tf_op jit(solution)/shard_map/pallas_call | solution.py:56
  2.4 26.4 %all_to_all.10 = bf16[8,40,1152]{2,1,0:T(8,128)(2,1)S(1)} all-to-all(bf16[8,40,1152]{2,1,0:T(8,128)(2,1)} %bitcast.15), channel_id=1, replica_groups=mesh['dp'=8,'pair'=4] {'dp'}, dimensions={0} | all-to-all | bytes 1474560 | tf_op jit(solution)/shard_map/all_to_all | solution.py:96
  28.8 0.1 slice.12
  28.9 0.1 collective-permute-start.3
  29.0 1.6 %collective-permute-start = (bf16[320,1024]{1,0:T(8,128)(2,1)S(1)}, bf16[320,1024]{1,0:T(8,128)(2,1)S(1)}, u32[]{:S(2)}, u32[]{:S(2)}) collective-permute-start(bf16[320,1024]{1,0:T(8,128)(2,1)S(1)} %slice.12), channel_id=1, source_target_pairs={{0,2},{1,3},{2,0},{3,1},{4,6},{5,7},{6,4},{7,5},{8,10},{9,11},{10,... | collective-permute-start | bytes 1966088 | tf_op jit(solution)/shard_map/ppermute | solution.py:100
  30.5 0.1 slice_reduce_fusion
  30.7 0.2 collective-permute-start.2
  30.9 0.5 collective-permute-start.1
  31.4 0.1 convert_reduce_fusion
  31.6 0.2 fusion.3
  31.7 0.5 fusion
  32.3 0.0 collective-permute-done.2
  32.3 0.0 collective-permute-done.3
  32.3 0.5 select_reduce_fusion.1
  32.9 13.3 %collective-permute-done.1 = bf16[320]{0:T(512)(128)(2,1)S(1)} collective-permute-done((bf16[320]{0:T(512)(128)(2,1)S(1)}, bf16[320]{0:T(512)(128)(2,1)S(1)}, u32[]{:S(2)}, u32[]{:S(2)}) %collective-permute-start.1) | collective-permute-done | bytes 672 | tf_op jit(solution)/shard_map/ppermute | solution.py:100
  46.2 0.0 collective-permute-done
  46.2 0.0 collective-permute-start.5
  46.2 0.5 collective-permute-start.4
  46.7 0.5 fusion.1
  47.3 1.0 %collective-permute-done.4 = bf16[320]{0:T(512)(128)(2,1)S(1)} collective-permute-done((bf16[320]{0:T(512)(128)(2,1)S(1)}, bf16[320]{0:T(512)(128)(2,1)S(1)}, u32[]{:S(2)}, u32[]{:S(2)}) %collective-permute-start.4) | collective-permute-done | bytes 672 | tf_op jit(solution)/shard_map/ppermute | solution.py:107
  48.3 0.0 collective-permute-done.5
  48.3 0.5 select_reduce_fusion
  48.9 0.1 reshape.21
  49.0 10.0 %all_to_all.11 = f32[8,8,128]{2,1,0:T(8,128)S(1)} all-to-all(f32[8,8,128]{2,1,0:T(8,128)S(1)} %pad.4), channel_id=1, replica_groups=mesh['dp'=8,'pair'=4] {'dp'}, dimensions={0} | all-to-all | bytes 65536 | tf_op jit(solution)/shard_map/all_to_all | solution.py:129
  59.0 0.1 broadcast_in_dim.21
  59.1 0.0 copy-start
  59.1 0.7 %copy-done = s32[1,128]{1,0:T(1,128)S(1)} copy-done((s32[1,128]{1,0:T(1,128)S(1)}, s32[1,128]{1,0:T(1,128)}, u32[]{:S(2)}) %copy-start) | copy-done | bytes 536
  59.7 0.6 %select_reduce_fusion.2 = f32[128]{0:T(128)} fusion(f32[320]{0:T(512)S(1)} %broadcast_in_dim.21, s32[128]{0:T(128)S(1)} %bitcast.17), kind=kLoop, calls=%fused_computation.10 | loop fusion | flops 122752 | bytes 2304 | tf_op jit(solution)/shard_map/reduce_sum | solution.py:131
  (8 shorter events, 0.1 us)
Async XLA Ops:
  28.9 3.4 %collective-permute-start.3 = (bf16[320,1024]{1,0:T(8,128)(2,1)S(1)}, bf16[320,1024]{1,0:T(8,128)(2,1)S(1)}, u32[]{:S(2)}, u32[]{:S(2)}) collective-permute-start(bf16[320,1024]{1,0:T(8,128)(2,1)S(1)} %slice.12), channel_id=1, source_target_pairs={{0,1},{1,0},{2,3},{3,2},{4,5},{5,4},{6,7},{7,6},{8,9},{9,8},{10,11... | collective-permute-start | bytes 1966088 | tf_op jit(solution)/shard_map/ppermute | solution.py:107
  29.0 17.2 %collective-permute-start = (bf16[320,1024]{1,0:T(8,128)(2,1)S(1)}, bf16[320,1024]{1,0:T(8,128)(2,1)S(1)}, u32[]{:S(2)}, u32[]{:S(2)}) collective-permute-start(bf16[320,1024]{1,0:T(8,128)(2,1)S(1)} %slice.12), channel_id=1, source_target_pairs={{0,2},{1,3},{2,0},{3,1},{4,6},{5,7},{6,4},{7,5},{8,10},{9,11},{10,... | collective-permute-start | bytes 1966088 | tf_op jit(solution)/shard_map/ppermute | solution.py:100
  30.7 1.6 %collective-permute-start.2 = (bf16[320]{0:T(512)(128)(2,1)S(1)}, bf16[320]{0:T(512)(128)(2,1)S(1)}, u32[]{:S(2)}, u32[]{:S(2)}) collective-permute-start(bf16[320]{0:T(512)(128)(2,1)S(1)} %slice_reduce_fusion), channel_id=1, source_target_pairs={{0,1},{1,0},{2,3},{3,2},{4,5},{5,4},{6,7},{7,6},{8,9},{9,8},{10,11... | collective-permute-start | bytes 1928 | tf_op jit(solution)/shard_map/ppermute | solution.py:107
  30.9 15.3 %collective-permute-start.1 = (bf16[320]{0:T(512)(128)(2,1)S(1)}, bf16[320]{0:T(512)(128)(2,1)S(1)}, u32[]{:S(2)}, u32[]{:S(2)}) collective-permute-start(bf16[320]{0:T(512)(128)(2,1)S(1)} %slice_reduce_fusion), channel_id=1, source_target_pairs={{0,2},{1,3},{2,0},{3,1},{4,6},{5,7},{6,4},{7,5},{8,10},{9,11},{10,... | collective-permute-start | bytes 1928 | tf_op jit(solution)/shard_map/ppermute | solution.py:100
  46.2 2.1 %collective-permute-start.5 = (bf16[320,1024]{1,0:T(8,128)(2,1)S(1)}, bf16[320,1024]{1,0:T(8,128)(2,1)S(1)}, u32[]{:S(2)}, u32[]{:S(2)}) collective-permute-start(bf16[320,1024]{1,0:T(8,128)(2,1)S(1)} %collective-permute-done), channel_id=1, source_target_pairs={{0,1},{1,0},{2,3},{3,2},{4,5},{5,4},{6,7},{7,6},{8,9},{9,8},{10,11... | collective-permute-start | bytes 1966088 | tf_op jit(solution)/shard_map/ppermute | solution.py:107
  46.2 2.1 %collective-permute-start.4 = (bf16[320]{0:T(512)(128)(2,1)S(1)}, bf16[320]{0:T(512)(128)(2,1)S(1)}, u32[]{:S(2)}, u32[]{:S(2)}) collective-permute-start(bf16[320]{0:T(512)(128)(2,1)S(1)} %collective-permute-done.1), channel_id=1, source_target_pairs={{0,1},{1,0},{2,3},{3,2},{4,5},{5,4},{6,7},{7,6},{8,9},{9,8},{10,11... | collective-permute-start | bytes 1928 | tf_op jit(solution)/shard_map/ppermute | solution.py:107
  59.1 0.7 %copy-start = (s32[1,128]{1,0:T(1,128)S(1)}, s32[1,128]{1,0:T(1,128)}, u32[]{:S(2)}) copy-start(s32[1,128]{1,0:T(1,128)} %get-tuple-element.10) | copy-start | bytes 1540

commit v14 on v13

--- a/solution.py
+++ b/solution.py
@@ -8,6 +8,7 @@
 from jax.sharding import PartitionSpec as P
 
 CPO = 4
+TAG_LANES = 16
 
 
 floor_value = -2.0
@@ -43,7 +44,7 @@
     place = (lax.broadcasted_iota(jnp.int32, (slots, rows), 0) == slot_row).astype(jnp.bfloat16)
     out_ref[:, :width] = jnp.dot(place, unit, preferred_element_type=jnp.float32).astype(jnp.bfloat16)
     tag_source = jnp.where(
-        lax.broadcasted_iota(jnp.int32, (rows, 128), 1) == 0, jnp.bitwise_and(lcol, CPO - 1) + 1, 0
+        lax.broadcasted_iota(jnp.int32, (rows, TAG_LANES), 1) == 0, jnp.bitwise_and(lcol, CPO - 1) + 1, 0
     ).astype(jnp.bfloat16)
     tags = jnp.dot(place, tag_source, preferred_element_type=jnp.float32) - 1.0
     out_ref[:, width:] = tags.astype(jnp.bfloat16)
@@ -56,15 +57,15 @@
     return pl.pallas_call(
         functools.partial(prepare_kernel, groups=groups, capacity=capacity),
         out_shape=(
-            jax.ShapeDtypeStruct((slots, width + 128), jnp.bfloat16),
+            jax.ShapeDtypeStruct((slots, width + TAG_LANES), jnp.bfloat16),
             jax.ShapeDtypeStruct((1, rows), jnp.int32),
         ),
         in_specs=[pl.BlockSpec(memory_space=vmem)] * 2,
         out_specs=(pl.BlockSpec(memory_space=vmem), pl.BlockSpec(memory_space=vmem)),
         cost_estimate=pl.CostEstimate(
-            flops=2 * slots * rows * (width + 128) + 4 * rows * width,
+            flops=2 * slots * rows * (width + TAG_LANES) + 4 * rows * width,
             transcendentals=rows,
-            bytes_accessed=rows * width * 4 + slots * (width + 128) * 2,
+            bytes_accessed=rows * width * 4 + slots * (width + TAG_LANES) * 2,
         ),
     )(embeddings, labels[None, :])
 
@@ -86,15 +87,15 @@
         onehot = (owner[:, None] == jnp.arange(groups, dtype=jnp.int32)[None, :]).astype(jnp.int32)
         rank = jnp.sum(jnp.cumsum(onehot, axis=0) * onehot, axis=1) - 1
         slot = owner * capacity + rank
-        tag_source = jnp.zeros((rows, 128), jnp.bfloat16).at[:, 0].set((local + 1).astype(jnp.bfloat16))
+        tag_source = jnp.zeros((rows, TAG_LANES), jnp.bfloat16).at[:, 0].set((local + 1).astype(jnp.bfloat16))
         source = jnp.concatenate([unit, tag_source], axis=1)
         place = slot[None, :] == jnp.arange(slots, dtype=jnp.int32)[:, None]
         outgoing = jnp.dot(place.astype(jnp.bfloat16), source, preferred_element_type=jnp.float32)
-        outgoing = (outgoing - jnp.where(jnp.arange(width + 128) >= width, 1.0, 0.0)).astype(jnp.bfloat16)
+        outgoing = (outgoing - jnp.where(jnp.arange(width + TAG_LANES) >= width, 1.0, 0.0)).astype(jnp.bfloat16)
     place = slot[None, :] == jnp.arange(slots, dtype=jnp.int32)[:, None]
-    outgoing = outgoing.reshape(groups, capacity, width + 128)
+    outgoing = outgoing.reshape(groups, capacity, width + TAG_LANES)
     block = lax.all_to_all(outgoing, "dp", split_axis=0, concat_axis=0, tiled=True)
-    block = block.reshape(slots, width + 128)
+    block = block.reshape(slots, width + TAG_LANES)
     top = peers // 2
     own = (block[:, :width], block[:, width])
     far = lax.ppermute(own, "pair", [(p, p ^ top) for p in range(peers)]) if top else None

time: 60.6 us -> 60.6 us (level)
  no operation moved by 1% of the time
where the time goes in v14:
time: 60.6 us; the launch traced here: 60.4 us
  blocking collectives  36.4 us (60%)
  waiting for transfers between devices  14.4 us (24%)
  starting transfers between devices  2.9 us (5%)
  Pallas kernels  2.41 us (4%)
  matrix products  2.16 us (4%)
  local copies, waits for them, and re-layouts  1.03 us (2%)
  other arithmetic  0.97 us (2%)
    all_to_all x1, blocking collectives, shards(): lax.all_to_all(outgoing, 'dp', split_axis=0, concat_axis=0, tiled=True)  26.4 us
    ppermute x2, waiting for transfers between devices, shards(): lax.ppermute(own, 'pair', [(p, p ^ top) for p in range(peers)])  13.3 us
    all_to_all x1, blocking collectives, shards(): lax.all_to_all(sent, 'dp', split_axis=0, concat_axis=0, tiled=True)  10 us
    pallas_call x1, Pallas kernels, prepare(): pl.pallas_call(functools.partial(prepare_kernel, groups=groups, capacity=...  2.41 us
    dot_general x4, matrix products, piece_best(): jnp.einsum('id,jd->ij', left, right, preferred_element_type=jnp.float32)  2.16 us
    ppermute x2, starting transfers between devices, shards(): lax.ppermute(own, 'pair', [(p, p ^ top) for p in range(peers)])  2.09 us
  transfers between devices with their start and end apart: 6, of which 2 were waited for; matrix products, arithmetic and copies ran while one was open for 3% of the time, Pallas kernels for 0%

profile of v14, /device:TPU:0, one launch (start us, length us, event | category | flops | bytes accessed | tf_op | source)
XLA Modules:
  0.0 60.4 jit_solution(6912113479308713812)
XLA Ops:
  0.0 2.4 %shard_map.28 = (bf16[320,1040]{1,0:T(8,128)(2,1)}, s32[1,128]{1,0:T(1,128)}) custom-call(f32[128,1024]{1,0:T(8,128)} %emb_ref.1, s32[1,128]{1,0:T(1,128)} %bitcast.16), custom_call_target="tpu_custom_call" | custom-call | flops 85721088 | bytes 1189888 | tf_op jit(solution)/shard_map/pallas_call | solution.py:57
  2.4 26.4 %all_to_all.10 = bf16[8,40,1040]{2,1,0:T(8,128)(2,1)S(1)} all-to-all(bf16[8,40,1040]{2,1,0:T(8,128)(2,1)} %bitcast.15), channel_id=1, replica_groups=mesh['dp'=8,'pair'=4] {'dp'}, dimensions={0} | all-to-all | bytes 1331200 | tf_op jit(solution)/shard_map/all_to_all | solution.py:97
  28.8 0.1 slice.12
  28.9 0.1 collective-permute-start.3
  29.0 1.6 %collective-permute-start = (bf16[320,1024]{1,0:T(8,128)(2,1)S(1)}, bf16[320,1024]{1,0:T(8,128)(2,1)S(1)}, u32[]{:S(2)}, u32[]{:S(2)}) collective-permute-start(bf16[320,1024]{1,0:T(8,128)(2,1)S(1)} %slice.12), channel_id=1, source_target_pairs={{0,2},{1,3},{2,0},{3,1},{4,6},{5,7},{6,4},{7,5},{8,10},{9,11},{10,... | collective-permute-start | bytes 1966088 | tf_op jit(solution)/shard_map/ppermute | solution.py:101
  30.5 0.1 slice_reduce_fusion
  30.7 0.2 collective-permute-start.2
  30.9 0.5 collective-permute-start.1
  31.4 0.1 convert_reduce_fusion
  31.6 0.2 fusion.3
  31.7 0.5 fusion
  32.3 0.0 collective-permute-done.2
  32.3 0.0 collective-permute-done.3
  32.3 0.5 select_reduce_fusion.1
  32.9 13.3 %collective-permute-done.1 = bf16[320]{0:T(512)(128)(2,1)S(1)} collective-permute-done((bf16[320]{0:T(512)(128)(2,1)S(1)}, bf16[320]{0:T(512)(128)(2,1)S(1)}, u32[]{:S(2)}, u32[]{:S(2)}) %collective-permute-start.1) | collective-permute-done | bytes 672 | tf_op jit(solution)/shard_map/ppermute | solution.py:101
  46.2 0.0 collective-permute-done
  46.2 0.0 collective-permute-start.5
  46.2 0.5 collective-permute-start.4
  46.7 0.5 fusion.1
  47.3 1.0 %collective-permute-done.4 = bf16[320]{0:T(512)(128)(2,1)S(1)} collective-permute-done((bf16[320]{0:T(512)(128)(2,1)S(1)}, bf16[320]{0:T(512)(128)(2,1)S(1)}, u32[]{:S(2)}, u32[]{:S(2)}) %collective-permute-start.4) | collective-permute-done | bytes 672 | tf_op jit(solution)/shard_map/ppermute | solution.py:108
  48.3 0.0 collective-permute-done.5
  48.3 0.5 select_reduce_fusion
  48.9 0.1 reshape.21
  49.0 10.0 %all_to_all.11 = f32[8,8,128]{2,1,0:T(8,128)S(1)} all-to-all(f32[8,8,128]{2,1,0:T(8,128)S(1)} %pad.4), channel_id=1, replica_groups=mesh['dp'=8,'pair'=4] {'dp'}, dimensions={0} | all-to-all | bytes 65536 | tf_op jit(solution)/shard_map/all_to_all | solution.py:130
  59.0 0.1 broadcast_in_dim.21
  59.1 0.0 copy-start
  59.1 0.7 %copy-done = s32[1,128]{1,0:T(1,128)S(1)} copy-done((s32[1,128]{1,0:T(1,128)S(1)}, s32[1,128]{1,0:T(1,128)}, u32[]{:S(2)}) %copy-start) | copy-done | bytes 536
  59.7 0.6 %select_reduce_fusion.2 = f32[128]{0:T(128)} fusion(f32[320]{0:T(512)S(1)} %broadcast_in_dim.21, s32[128]{0:T(128)S(1)} %bitcast.17), kind=kLoop, calls=%fused_computation.10 | loop fusion | flops 122752 | bytes 2304 | tf_op jit(solution)/shard_map/reduce_sum | solution.py:132
  (8 shorter events, 0.1 us)
Async XLA Ops:
  28.9 3.4 %collective-permute-start.3 = (bf16[320,1024]{1,0:T(8,128)(2,1)S(1)}, bf16[320,1024]{1,0:T(8,128)(2,1)S(1)}, u32[]{:S(2)}, u32[]{:S(2)}) collective-permute-start(bf16[320,1024]{1,0:T(8,128)(2,1)S(1)} %slice.12), channel_id=1, source_target_pairs={{0,1},{1,0},{2,3},{3,2},{4,5},{5,4},{6,7},{7,6},{8,9},{9,8},{10,11... | collective-permute-start | bytes 1966088 | tf_op jit(solution)/shard_map/ppermute | solution.py:108
  29.0 17.2 %collective-permute-start = (bf16[320,1024]{1,0:T(8,128)(2,1)S(1)}, bf16[320,1024]{1,0:T(8,128)(2,1)S(1)}, u32[]{:S(2)}, u32[]{:S(2)}) collective-permute-start(bf16[320,1024]{1,0:T(8,128)(2,1)S(1)} %slice.12), channel_id=1, source_target_pairs={{0,2},{1,3},{2,0},{3,1},{4,6},{5,7},{6,4},{7,5},{8,10},{9,11},{10,... | collective-permute-start | bytes 1966088 | tf_op jit(solution)/shard_map/ppermute | solution.py:101
  30.7 1.6 %collective-permute-start.2 = (bf16[320]{0:T(512)(128)(2,1)S(1)}, bf16[320]{0:T(512)(128)(2,1)S(1)}, u32[]{:S(2)}, u32[]{:S(2)}) collective-permute-start(bf16[320]{0:T(512)(128)(2,1)S(1)} %slice_reduce_fusion), channel_id=1, source_target_pairs={{0,1},{1,0},{2,3},{3,2},{4,5},{5,4},{6,7},{7,6},{8,9},{9,8},{10,11... | collective-permute-start | bytes 1928 | tf_op jit(solution)/shard_map/ppermute | solution.py:108
  30.9 15.3 %collective-permute-start.1 = (bf16[320]{0:T(512)(128)(2,1)S(1)}, bf16[320]{0:T(512)(128)(2,1)S(1)}, u32[]{:S(2)}, u32[]{:S(2)}) collective-permute-start(bf16[320]{0:T(512)(128)(2,1)S(1)} %slice_reduce_fusion), channel_id=1, source_target_pairs={{0,2},{1,3},{2,0},{3,1},{4,6},{5,7},{6,4},{7,5},{8,10},{9,11},{10,... | collective-permute-start | bytes 1928 | tf_op jit(solution)/shard_map/ppermute | solution.py:101
  46.2 2.1 %collective-permute-start.5 = (bf16[320,1024]{1,0:T(8,128)(2,1)S(1)}, bf16[320,1024]{1,0:T(8,128)(2,1)S(1)}, u32[]{:S(2)}, u32[]{:S(2)}) collective-permute-start(bf16[320,1024]{1,0:T(8,128)(2,1)S(1)} %collective-permute-done), channel_id=1, source_target_pairs={{0,1},{1,0},{2,3},{3,2},{4,5},{5,4},{6,7},{7,6},{8,9},{9,8},{10,11... | collective-permute-start | bytes 1966088 | tf_op jit(solution)/shard_map/ppermute | solution.py:108
  46.2 2.1 %collective-permute-start.4 = (bf16[320]{0:T(512)(128)(2,1)S(1)}, bf16[320]{0:T(512)(128)(2,1)S(1)}, u32[]{:S(2)}, u32[]{:S(2)}) collective-permute-start(bf16[320]{0:T(512)(128)(2,1)S(1)} %collective-permute-done.1), channel_id=1, source_target_pairs={{0,1},{1,0},{2,3},{3,2},{4,5},{5,4},{6,7},{7,6},{8,9},{9,8},{10,11... | collective-permute-start | bytes 1928 | tf_op jit(solution)/shard_map/ppermute | solution.py:108
  59.1 0.7 %copy-start = (s32[1,128]{1,0:T(1,128)S(1)}, s32[1,128]{1,0:T(1,128)}, u32[]{:S(2)}) copy-start(s32[1,128]{1,0:T(1,128)} %get-tuple-element.10) | copy-start | bytes 1540

commit v15 on v13

--- a/solution.py
+++ b/solution.py
@@ -124,6 +124,7 @@
     if far is not None:
         far, best = lax.optimization_barrier((far, best))
         best = jnp.maximum(best, best_over(spread(far), False))
+    place, best = lax.optimization_barrier((place, best))
     lanes = -(-capacity // 128) * 128
     sent = jnp.pad(best.reshape(groups, 1, capacity), ((0, 0), (0, 7), (0, lanes - capacity)))
     returned = lax.all_to_all(sent, "dp", split_axis=0, concat_axis=0, tiled=True)

time: 60.6 us -> 60 us (0.990)
  waiting for transfers between devices: 14.4 us -> 13.6 us
    ppermute x4, waiting for transfers between devices: 1.05 us -> 0.29 us  [spread(): pieces = pieces + [lax.ppermute(y, 'pair', perm) for y in pieces]]
  transfers between devices with their start and end apart: 6 -> 6, of which waited for: 2 -> 2; matrix products, arithmetic and copies ran while one was open for 3% -> 4% of each run, Pallas kernels for 0% -> 0%
where the time goes in v15:
time: 60 us; the launch traced here: 59.7 us
  blocking collectives  36.4 us (61%)
  waiting for transfers between devices  13.6 us (23%)
  starting transfers between devices  2.97 us (5%)
  Pallas kernels  2.41 us (4%)
  matrix products  2.17 us (4%)
  local copies, waits for them, and re-layouts  1.03 us (2%)
  other arithmetic  1 us (2%)
    all_to_all x1, blocking collectives, shards(): lax.all_to_all(outgoing, 'dp', split_axis=0, concat_axis=0, tiled=True)  26.4 us
    ppermute x2, waiting for transfers between devices, shards(): lax.ppermute(own, 'pair', [(p, p ^ top) for p in range(peers)])  13.3 us
    all_to_all x1, blocking collectives, shards(): lax.all_to_all(sent, 'dp', split_axis=0, concat_axis=0, tiled=True)  10 us
    pallas_call x1, Pallas kernels, prepare(): pl.pallas_call(functools.partial(prepare_kernel, groups=groups, capacity=...  2.41 us
    dot_general x4, matrix products, piece_best(): jnp.einsum('id,jd->ij', left, right, preferred_element_type=jnp.float32)  2.17 us
    ppermute x2, starting transfers between devices, shards(): lax.ppermute(own, 'pair', [(p, p ^ top) for p in range(peers)])  2.09 us
  transfers between devices with their start and end apart: 6, of which 2 were waited for; matrix products, arithmetic and copies ran while one was open for 4% of the time, Pallas kernels for 0%

profile of v15, /device:TPU:0, one launch (start us, length us, event | category | flops | bytes accessed | tf_op | source)
XLA Modules:
  0.0 59.7 jit_solution(5256933813866285296)
XLA Ops:
  0.0 2.4 %shard_map.28 = (bf16[320,1152]{1,0:T(8,128)(2,1)}, s32[1,128]{1,0:T(1,128)}) custom-call(f32[128,1024]{1,0:T(8,128)} %emb_ref.1, s32[1,128]{1,0:T(1,128)} %bitcast.16), custom_call_target="tpu_custom_call" | custom-call | flops 94896128 | bytes 1261568 | tf_op jit(solution)/shard_map/pallas_call | solution.py:56
  2.4 26.4 %all_to_all.10 = bf16[8,40,1152]{2,1,0:T(8,128)(2,1)S(1)} all-to-all(bf16[8,40,1152]{2,1,0:T(8,128)(2,1)} %bitcast.15), channel_id=1, replica_groups=mesh['dp'=8,'pair'=4] {'dp'}, dimensions={0} | all-to-all | bytes 1474560 | tf_op jit(solution)/shard_map/all_to_all | solution.py:96
  28.8 0.1 slice.12
  28.9 0.1 collective-permute-start.3
  29.0 1.6 %collective-permute-start = (bf16[320,1024]{1,0:T(8,128)(2,1)S(1)}, bf16[320,1024]{1,0:T(8,128)(2,1)S(1)}, u32[]{:S(2)}, u32[]{:S(2)}) collective-permute-start(bf16[320,1024]{1,0:T(8,128)(2,1)S(1)} %slice.12), channel_id=1, source_target_pairs={{0,2},{1,3},{2,0},{3,1},{4,6},{5,7},{6,4},{7,5},{8,10},{9,11},{10,... | collective-permute-start | bytes 1966088 | tf_op jit(solution)/shard_map/ppermute | solution.py:100
  30.5 0.1 slice_reduce_fusion
  30.7 0.2 collective-permute-start.2
  30.9 0.5 collective-permute-start.1
  31.4 0.1 convert_reduce_fusion
  31.6 0.2 fusion.3
  31.7 0.5 fusion
  32.3 0.0 collective-permute-done.2
  32.3 0.0 collective-permute-done.3
  32.3 0.5 select_reduce_fusion.1
  32.9 13.3 %collective-permute-done.1 = bf16[320]{0:T(512)(128)(2,1)S(1)} collective-permute-done((bf16[320]{0:T(512)(128)(2,1)S(1)}, bf16[320]{0:T(512)(128)(2,1)S(1)}, u32[]{:S(2)}, u32[]{:S(2)}) %collective-permute-start.1) | collective-permute-done | bytes 672 | tf_op jit(solution)/shard_map/ppermute | solution.py:100
  46.2 0.0 collective-permute-done
  46.2 0.0 collective-permute-start.5
  46.2 0.0 copy-start
  46.2 0.7 %copy-done = s32[1,128]{1,0:T(1,128)S(1)} copy-done((s32[1,128]{1,0:T(1,128)S(1)}, s32[1,128]{1,0:T(1,128)}, u32[]{:S(2)}) %copy-start) | copy-done | bytes 536
  46.9 0.6 collective-permute-start.4
  47.5 0.5 fusion.1
  48.0 0.3 collective-permute-done.4
  48.3 0.0 collective-permute-done.5
  48.3 0.5 select_reduce_fusion
  48.9 0.1 reshape.21
  49.0 10.0 %all_to_all.11 = f32[8,8,128]{2,1,0:T(8,128)S(1)} all-to-all(f32[8,8,128]{2,1,0:T(8,128)S(1)} %pad.4), channel_id=1, replica_groups=mesh['dp'=8,'pair'=4] {'dp'}, dimensions={0} | all-to-all | bytes 65536 | tf_op jit(solution)/shard_map/all_to_all | solution.py:130
  59.0 0.1 broadcast_in_dim.21
  59.1 0.6 %select_reduce_fusion.2 = f32[128]{0:T(128)} fusion(pred[320,128]{1,0:T(8,128)(4,1)S(1)} %iota_compare_fusion.1, f32[320]{0:T(512)S(1)} %broadcast_in_dim.21), kind=kLoop, calls=%fused_computation.10 | loop fusion | flops 81792 | bytes 42752 | tf_op jit(solution)/shard_map/reduce_sum | solution.py:132
  (9 shorter events, 0.1 us)
Async XLA Ops:
  28.9 3.4 %collective-permute-start.3 = (bf16[320,1024]{1,0:T(8,128)(2,1)S(1)}, bf16[320,1024]{1,0:T(8,128)(2,1)S(1)}, u32[]{:S(2)}, u32[]{:S(2)}) collective-permute-start(bf16[320,1024]{1,0:T(8,128)(2,1)S(1)} %slice.12), channel_id=1, source_target_pairs={{0,1},{1,0},{2,3},{3,2},{4,5},{5,4},{6,7},{7,6},{8,9},{9,8},{10,11... | collective-permute-start | bytes 1966088 | tf_op jit(solution)/shard_map/ppermute | solution.py:107
  29.0 17.2 %collective-permute-start = (bf16[320,1024]{1,0:T(8,128)(2,1)S(1)}, bf16[320,1024]{1,0:T(8,128)(2,1)S(1)}, u32[]{:S(2)}, u32[]{:S(2)}) collective-permute-start(bf16[320,1024]{1,0:T(8,128)(2,1)S(1)} %slice.12), channel_id=1, source_target_pairs={{0,2},{1,3},{2,0},{3,1},{4,6},{5,7},{6,4},{7,5},{8,10},{9,11},{10,... | collective-permute-start | bytes 1966088 | tf_op jit(solution)/shard_map/ppermute | solution.py:100
  30.7 1.6 %collective-permute-start.2 = (bf16[320]{0:T(512)(128)(2,1)S(1)}, bf16[320]{0:T(512)(128)(2,1)S(1)}, u32[]{:S(2)}, u32[]{:S(2)}) collective-permute-start(bf16[320]{0:T(512)(128)(2,1)S(1)} %slice_reduce_fusion), channel_id=1, source_target_pairs={{0,1},{1,0},{2,3},{3,2},{4,5},{5,4},{6,7},{7,6},{8,9},{9,8},{10,11... | collective-permute-start | bytes 1928 | tf_op jit(solution)/shard_map/ppermute | solution.py:107
  30.9 15.3 %collective-permute-start.1 = (bf16[320]{0:T(512)(128)(2,1)S(1)}, bf16[320]{0:T(512)(128)(2,1)S(1)}, u32[]{:S(2)}, u32[]{:S(2)}) collective-permute-start(bf16[320]{0:T(512)(128)(2,1)S(1)} %slice_reduce_fusion), channel_id=1, source_target_pairs={{0,2},{1,3},{2,0},{3,1},{4,6},{5,7},{6,4},{7,5},{8,10},{9,11},{10,... | collective-permute-start | bytes 1928 | tf_op jit(solution)/shard_map/ppermute | solution.py:100
  46.2 2.1 %collective-permute-start.5 = (bf16[320,1024]{1,0:T(8,128)(2,1)S(1)}, bf16[320,1024]{1,0:T(8,128)(2,1)S(1)}, u32[]{:S(2)}, u32[]{:S(2)}) collective-permute-start(bf16[320,1024]{1,0:T(8,128)(2,1)S(1)} %collective-permute-done), channel_id=1, source_target_pairs={{0,1},{1,0},{2,3},{3,2},{4,5},{5,4},{6,7},{7,6},{8,9},{9,8},{10,11... | collective-permute-start | bytes 1966088 | tf_op jit(solution)/shard_map/ppermute | solution.py:107
  46.2 0.7 %copy-start = (s32[1,128]{1,0:T(1,128)S(1)}, s32[1,128]{1,0:T(1,128)}, u32[]{:S(2)}) copy-start(s32[1,128]{1,0:T(1,128)} %get-tuple-element.12) | copy-start | bytes 1540
  46.9 1.4 %collective-permute-start.4 = (bf16[320]{0:T(512)(128)(2,1)S(1)}, bf16[320]{0:T(512)(128)(2,1)S(1)}, u32[]{:S(2)}, u32[]{:S(2)}) collective-permute-start(bf16[320]{0:T(512)(128)(2,1)S(1)} %collective-permute-done.1), channel_id=1, source_target_pairs={{0,1},{1,0},{2,3},{3,2},{4,5},{5,4},{6,7},{7,6},{8,9},{9,8},{10,11... | collective-permute-start | bytes 1928 | tf_op jit(solution)/shard_map/ppermute | solution.py:107

commit v16 on v15

--- a/solution.py
+++ b/solution.py
@@ -97,7 +97,6 @@
     block = block.reshape(slots, width + 128)
     top = peers // 2
     own = (block[:, :width], block[:, width])
-    far = lax.ppermute(own, "pair", [(p, p ^ top) for p in range(peers)]) if top else None
 
     def spread(x):
         pieces = [x]
@@ -107,6 +106,19 @@
             pieces = pieces + [lax.ppermute(y, "pair", perm) for y in pieces]
             bit //= 2
         return pieces
+
+    masks = [0]
+    bit = top // 2
+    while bit >= 1:
+        masks = masks + [m ^ bit for m in masks]
+        bit //= 2
+    far = None
+    if top:
+        far_tags = [
+            lax.ppermute(own[1], "pair", [(p, p ^ top ^ m) for p in range(peers)]) for m in masks
+        ]
+        far_rows = lax.ppermute(own[0], "pair", [(p, p ^ top) for p in range(peers)])
+        far = (far_rows, far_tags)
 
     left, left_tags = own
     left_labels = left_tags.astype(jnp.int32)
@@ -123,7 +135,8 @@
     best = best_over(spread(own), True)
     if far is not None:
         far, best = lax.optimization_barrier((far, best))
-        best = jnp.maximum(best, best_over(spread(far), False))
+        far_rows, far_tags = far
+        best = jnp.maximum(best, best_over(list(zip(spread(far_rows), far_tags)), False))
     place, best = lax.optimization_barrier((place, best))
     lanes = -(-capacity // 128) * 128
     sent = jnp.pad(best.reshape(groups, 1, capacity), ((0, 0), (0, 7), (0, lanes - capacity)))

time: 60 us -> 60 us (level)
  starting transfers between devices: 2.97 us -> 3.62 us
    ppermute x2 -> x3, starting transfers between devices: 2.09 us -> 3.25 us  [the longest x2 1.69 us: shards(): lax.ppermute(own[1], 'pair', [(p, p ^ top ^ m) for p in range(peers)])]
    ppermute x2 -> x3, waiting for transfers between devices: 13.3 us -> 12.2 us  [the longest x2 12.2 us: shards(): lax.ppermute(own[1], 'pair', [(p, p ^ top ^ m) for p in range(peers)])]
  transfers between devices with their start and end apart: 6 -> 6, of which waited for: 2 -> 2; matrix products, arithmetic and copies ran while one was open for 4% -> 3% of each run, Pallas kernels for 0% -> 0%
where the time goes in v16:
time: 60 us; the launch traced here: 59.7 us
  blocking collectives  36.4 us (61%)
  waiting for transfers between devices  13 us (22%)
  starting transfers between devices  3.62 us (6%)
  Pallas kernels  2.41 us (4%)
  matrix products  2.14 us (4%)
  local copies, waits for them, and re-layouts  1.03 us (2%)
  other arithmetic  1.01 us (2%)
    all_to_all x1, blocking collectives, shards(): lax.all_to_all(outgoing, 'dp', split_axis=0, concat_axis=0, tiled=True)  26.4 us
    ppermute x2, waiting for transfers between devices, shards(): lax.ppermute(own[1], 'pair', [(p, p ^ top ^ m) for p in range(peers)])  12.2 us
    all_to_all x1, blocking collectives, shards(): lax.all_to_all(sent, 'dp', split_axis=0, concat_axis=0, tiled=True)  10 us
    pallas_call x1, Pallas kernels, prepare(): pl.pallas_call(functools.partial(prepare_kernel, groups=groups, capacity=...  2.41 us
    dot_general x4, matrix products, piece_best(): jnp.einsum('id,jd->ij', left, right, preferred_element_type=jnp.float32)  2.14 us
    ppermute x2, starting transfers between devices, shards(): lax.ppermute(own[1], 'pair', [(p, p ^ top ^ m) for p in range(peers)])  1.69 us
    ppermute x1, starting transfers between devices, shards(): lax.ppermute(own[0], 'pair', [(p, p ^ top) for p in range(peers)])  1.56 us
  transfers between devices with their start and end apart: 6, of which 2 were waited for; matrix products, arithmetic and copies ran while one was open for 3% of the time, Pallas kernels for 0%

profile of v16, /device:TPU:0, one launch (start us, length us, event | category | flops | bytes accessed | tf_op | source)
XLA Modules:
  0.0 59.7 jit_solution(12196533481915956584)
XLA Ops:
  0.0 2.4 %shard_map.28 = (bf16[320,1152]{1,0:T(8,128)(2,1)}, s32[1,128]{1,0:T(1,128)}) custom-call(f32[128,1024]{1,0:T(8,128)} %emb_ref.1, s32[1,128]{1,0:T(1,128)} %bitcast.16), custom_call_target="tpu_custom_call" | custom-call | flops 94896128 | bytes 1261568 | tf_op jit(solution)/shard_map/pallas_call | solution.py:56
  2.4 26.4 %all_to_all.10 = bf16[8,40,1152]{2,1,0:T(8,128)(2,1)S(1)} all-to-all(bf16[8,40,1152]{2,1,0:T(8,128)(2,1)} %bitcast.15), channel_id=1, replica_groups=mesh['dp'=8,'pair'=4] {'dp'}, dimensions={0} | all-to-all | bytes 1474560 | tf_op jit(solution)/shard_map/all_to_all | solution.py:96
  28.8 0.1 slice.12
  28.9 0.1 collective-permute-start.4
  29.0 1.6 %collective-permute-start = (bf16[320,1024]{1,0:T(8,128)(2,1)S(1)}, bf16[320,1024]{1,0:T(8,128)(2,1)S(1)}, u32[]{:S(2)}, u32[]{:S(2)}) collective-permute-start(bf16[320,1024]{1,0:T(8,128)(2,1)S(1)} %slice.12), channel_id=1, source_target_pairs={{0,2},{1,3},{2,0},{3,1},{4,6},{5,7},{6,4},{7,5},{8,10},{9,11},{10,... | collective-permute-start | bytes 1966088 | tf_op jit(solution)/shard_map/ppermute | solution.py:120
  30.5 0.1 slice_reduce_fusion
  30.7 0.2 collective-permute-start.3
  30.9 0.5 collective-permute-start.1
  31.4 1.2 %collective-permute-start.2 = (bf16[320]{0:T(512)(128)(2,1)S(1)}, bf16[320]{0:T(512)(128)(2,1)S(1)}, u32[]{:S(2)}, u32[]{:S(2)}) collective-permute-start(bf16[320]{0:T(512)(128)(2,1)S(1)} %slice_reduce_fusion), channel_id=1, source_target_pairs={{0,3},{1,2},{2,1},{3,0},{4,7},{5,6},{6,5},{7,4},{8,11},{9,10},{10,... | collective-permute-start | bytes 1928 | tf_op jit(solution)/shard_map/ppermute | solution.py:118
  32.6 0.1 convert_reduce_fusion
  32.7 0.2 fusion.4
  32.9 0.5 fusion
  33.4 0.0 collective-permute-done.3
  33.5 0.0 collective-permute-done.4
  33.5 0.5 select_reduce_fusion
  34.0 12.2 %collective-permute-done.1 = bf16[320]{0:T(512)(128)(2,1)S(1)} collective-permute-done((bf16[320]{0:T(512)(128)(2,1)S(1)}, bf16[320]{0:T(512)(128)(2,1)S(1)}, u32[]{:S(2)}, u32[]{:S(2)}) %collective-permute-start.1) | collective-permute-done | bytes 672 | tf_op jit(solution)/shard_map/ppermute | solution.py:118
  46.2 0.0 collective-permute-done.2
  46.2 0.0 collective-permute-done
  46.2 0.1 collective-permute-start.5
  46.3 0.0 copy-start
  46.3 0.7 %copy-done = s32[1,128]{1,0:T(1,128)S(1)} copy-done((s32[1,128]{1,0:T(1,128)S(1)}, s32[1,128]{1,0:T(1,128)}, u32[]{:S(2)}) %copy-start) | copy-done | bytes 536
  47.0 0.5 fusion.1
  47.5 0.8 %collective-permute-done.5 = bf16[320,1024]{1,0:T(8,128)(2,1)S(1)} collective-permute-done((bf16[320,1024]{1,0:T(8,128)(2,1)S(1)}, bf16[320,1024]{1,0:T(8,128)(2,1)S(1)}, u32[]{:S(2)}, u32[]{:S(2)}) %collective-permute-start.5) | collective-permute-done | bytes 655392 | tf_op jit(solution)/shard_map/ppermute | solution.py:106
  48.3 0.5 fusion.2
  48.9 0.1 reshape.21
  49.0 10.0 %all_to_all.11 = f32[8,8,128]{2,1,0:T(8,128)S(1)} all-to-all(f32[8,8,128]{2,1,0:T(8,128)S(1)} %pad.4), channel_id=1, replica_groups=mesh['dp'=8,'pair'=4] {'dp'}, dimensions={0} | all-to-all | bytes 65536 | tf_op jit(solution)/shard_map/all_to_all | solution.py:143
  59.0 0.1 broadcast_in_dim.21
  59.1 0.6 %select_reduce_fusion.1 = f32[128]{0:T(128)} fusion(pred[320,128]{1,0:T(8,128)(4,1)S(1)} %iota_compare_fusion.1, f32[320]{0:T(512)S(1)} %broadcast_in_dim.21), kind=kLoop, calls=%fused_computation.11 | loop fusion | flops 81792 | bytes 42752 | tf_op jit(solution)/shard_map/reduce_sum | solution.py:145
  (9 shorter events, 0.1 us)
Async XLA Ops:
  28.9 4.6 %collective-permute-start.4 = (bf16[320,1024]{1,0:T(8,128)(2,1)S(1)}, bf16[320,1024]{1,0:T(8,128)(2,1)S(1)}, u32[]{:S(2)}, u32[]{:S(2)}) collective-permute-start(bf16[320,1024]{1,0:T(8,128)(2,1)S(1)} %slice.12), channel_id=1, source_target_pairs={{0,1},{1,0},{2,3},{3,2},{4,5},{5,4},{6,7},{7,6},{8,9},{9,8},{10,11... | collective-permute-start | bytes 1966088 | tf_op jit(solution)/shard_map/ppermute | solution.py:106
  29.0 17.2 %collective-permute-start = (bf16[320,1024]{1,0:T(8,128)(2,1)S(1)}, bf16[320,1024]{1,0:T(8,128)(2,1)S(1)}, u32[]{:S(2)}, u32[]{:S(2)}) collective-permute-start(bf16[320,1024]{1,0:T(8,128)(2,1)S(1)} %slice.12), channel_id=1, source_target_pairs={{0,2},{1,3},{2,0},{3,1},{4,6},{5,7},{6,4},{7,5},{8,10},{9,11},{10,... | collective-permute-start | bytes 1966088 | tf_op jit(solution)/shard_map/ppermute | solution.py:120
  30.7 2.8 %collective-permute-start.3 = (bf16[320]{0:T(512)(128)(2,1)S(1)}, bf16[320]{0:T(512)(128)(2,1)S(1)}, u32[]{:S(2)}, u32[]{:S(2)}) collective-permute-start(bf16[320]{0:T(512)(128)(2,1)S(1)} %slice_reduce_fusion), channel_id=1, source_target_pairs={{0,1},{1,0},{2,3},{3,2},{4,5},{5,4},{6,7},{7,6},{8,9},{9,8},{10,11... | collective-permute-start | bytes 1928 | tf_op jit(solution)/shard_map/ppermute | solution.py:106
  30.9 15.3 %collective-permute-start.1 = (bf16[320]{0:T(512)(128)(2,1)S(1)}, bf16[320]{0:T(512)(128)(2,1)S(1)}, u32[]{:S(2)}, u32[]{:S(2)}) collective-permute-start(bf16[320]{0:T(512)(128)(2,1)S(1)} %slice_reduce_fusion), channel_id=1, source_target_pairs={{0,2},{1,3},{2,0},{3,1},{4,6},{5,7},{6,4},{7,5},{8,10},{9,11},{10,... | collective-permute-start | bytes 1928 | tf_op jit(solution)/shard_map/ppermute | solution.py:118
  31.4 14.8 %collective-permute-start.2 = (bf16[320]{0:T(512)(128)(2,1)S(1)}, bf16[320]{0:T(512)(128)(2,1)S(1)}, u32[]{:S(2)}, u32[]{:S(2)}) collective-permute-start(bf16[320]{0:T(512)(128)(2,1)S(1)} %slice_reduce_fusion), channel_id=1, source_target_pairs={{0,3},{1,2},{2,1},{3,0},{4,7},{5,6},{6,5},{7,4},{8,11},{9,10},{10,... | collective-permute-start | bytes 1928 | tf_op jit(solution)/shard_map/ppermute | solution.py:118
  46.2 2.1 %collective-permute-start.5 = (bf16[320,1024]{1,0:T(8,128)(2,1)S(1)}, bf16[320,1024]{1,0:T(8,128)(2,1)S(1)}, u32[]{:S(2)}, u32[]{:S(2)}) collective-permute-start(bf16[320,1024]{1,0:T(8,128)(2,1)S(1)} %collective-permute-done), channel_id=1, source_target_pairs={{0,1},{1,0},{2,3},{3,2},{4,5},{5,4},{6,7},{7,6},{8,9},{9,8},{10,11... | collective-permute-start | bytes 1966088 | tf_op jit(solution)/shard_map/ppermute | solution.py:106
  46.3 0.7 %copy-start = (s32[1,128]{1,0:T(1,128)S(1)}, s32[1,128]{1,0:T(1,128)}, u32[]{:S(2)}) copy-start(s32[1,128]{1,0:T(1,128)} %get-tuple-element.13) | copy-start | bytes 1540

commit v17 on v13

--- a/solution.py
+++ b/solution.py
@@ -100,30 +100,36 @@
     far = lax.ppermute(own, "pair", [(p, p ^ top) for p in range(peers)]) if top else None
 
     def spread(x):
-        pieces = [x]
+        pieces, masks = [x], [0]
         bit = top // 2
         while bit >= 1:
             perm = [(p, p ^ bit) for p in range(peers)]
             pieces = pieces + [lax.ppermute(y, "pair", perm) for y in pieces]
+            masks = masks + [m ^ bit for m in masks]
             bit //= 2
-        return pieces
+        return pieces, masks
 
     left, left_tags = own
     left_labels = left_tags.astype(jnp.int32)
-
-    def best_over(pieces, first_is_own):
-        best = None
-        for index, (right, right_tags) in enumerate(pieces):
-            piece_max = piece_best(
-                left, left_labels, right, right_tags.astype(jnp.int32), first_is_own and index == 0
-            )
-            best = piece_max if best is None else jnp.maximum(best, piece_max)
-        return best
-
-    best = best_over(spread(own), True)
+    near, masks = spread(own)
+    best = None
+    for index, (right, right_tags) in enumerate(near):
+        piece_max = piece_best(left, left_labels, right, right_tags.astype(jnp.int32), index == 0)
+        best = piece_max if best is None else jnp.maximum(best, piece_max)
+    late_labels, best = lax.optimization_barrier((labels, best))
+    owner = lax.shift_right_logical(late_labels, CPO.bit_length() - 1)
+    onehot = (owner[:, None] == jnp.arange(groups, dtype=jnp.int32)[None, :]).astype(jnp.int32)
+    rank = jnp.sum(jnp.cumsum(onehot, axis=0) * onehot, axis=1) - 1
+    place = (owner * capacity + rank)[None, :] == jnp.arange(slots, dtype=jnp.int32)[:, None]
     if far is not None:
-        far, best = lax.optimization_barrier((far, best))
-        best = jnp.maximum(best, best_over(spread(far), False))
+        far, near, best, place = lax.optimization_barrier((far, near, best, place))
+        far_rows, far_tags = far
+        far_labels = far_tags.astype(jnp.int32)
+        for (rows_j, tags_j), m in zip(near, masks):
+            piece_max = piece_best(rows_j, tags_j.astype(jnp.int32), far_rows, far_labels, False)
+            if m:
+                piece_max = lax.ppermute(piece_max, "pair", [(p, p ^ m) for p in range(peers)])
+            best = jnp.maximum(best, piece_max)
     lanes = -(-capacity // 128) * 128
     sent = jnp.pad(best.reshape(groups, 1, capacity), ((0, 0), (0, 7), (0, lanes - capacity)))
     returned = lax.all_to_all(sent, "dp", split_axis=0, concat_axis=0, tiled=True)

time: 60.6 us -> 60.5 us (level)
    ppermute x4 -> x2, waiting for transfers between devices: 1.05 us -> 0.01 us  [spread(): pieces = pieces + [lax.ppermute(y, 'pair', perm) for y in pieces]]
  transfers between devices with their start and end apart: 6 -> 5, of which waited for: 2 -> 2; matrix products, arithmetic and copies ran while one was open for 3% -> 4% of each run, Pallas kernels for 0% -> 0%
where the time goes in v17:
time: 60.5 us; the launch traced here: 60.3 us
  blocking collectives  36.4 us (60%)
  waiting for transfers between devices  13.9 us (23%)
  starting transfers between devices  2.73 us (5%)
  Pallas kernels  2.41 us (4%)
  matrix products  2.16 us (4%)
  other arithmetic  1.46 us (2%)
  local copies, waits for them, and re-layouts  1.02 us (2%)
    all_to_all x1, blocking collectives, shards(): lax.all_to_all(outgoing, 'dp', split_axis=0, concat_axis=0, tiled=True)  26.4 us
    ppermute x2, waiting for transfers between devices, shards(): lax.ppermute(own, 'pair', [(p, p ^ top) for p in range(peers)])  13.3 us
    all_to_all x1, blocking collectives, shards(): lax.all_to_all(sent, 'dp', split_axis=0, concat_axis=0, tiled=True)  10 us
    pallas_call x1, Pallas kernels, prepare(): pl.pallas_call(functools.partial(prepare_kernel, groups=groups, capacity=...  2.41 us
    dot_general x4, matrix products, piece_best(): jnp.einsum('id,jd->ij', left, right, preferred_element_type=jnp.float32)  2.16 us
    ppermute x2, starting transfers between devices, shards(): lax.ppermute(own, 'pair', [(p, p ^ top) for p in range(peers)])  2.03 us
  transfers between devices with their start and end apart: 5, of which 2 were waited for; matrix products, arithmetic and copies ran while one was open for 4% of the time, Pallas kernels for 0%

profile of v17, /device:TPU:0, one launch (start us, length us, event | category | flops | bytes accessed | tf_op | source)
XLA Modules:
  0.0 60.3 jit_solution(1996021461417463363)
XLA Ops:
  0.0 2.4 %shard_map.28 = (bf16[320,1152]{1,0:T(8,128)(2,1)}, s32[1,128]{1,0:T(1,128)}) custom-call(f32[128,1024]{1,0:T(8,128)} %emb_ref.1, s32[1,128]{1,0:T(1,128)} %bitcast.15), custom_call_target="tpu_custom_call" | custom-call | flops 94896128 | bytes 1261568 | tf_op jit(solution)/shard_map/pallas_call | solution.py:56
  2.4 26.4 %all_to_all.10 = bf16[8,40,1152]{2,1,0:T(8,128)(2,1)S(1)} all-to-all(bf16[8,40,1152]{2,1,0:T(8,128)(2,1)} %bitcast.14), channel_id=1, replica_groups=mesh['dp'=8,'pair'=4] {'dp'}, dimensions={0} | all-to-all | bytes 1474560 | tf_op jit(solution)/shard_map/all_to_all | solution.py:96
  28.8 0.1 slice.12
  28.9 0.1 collective-permute-start.2
  29.0 0.1 slice_reduce_fusion
  29.1 0.6 collective-permute-start.3
  29.7 1.5 %collective-permute-start.1 = (bf16[320]{0:T(512)(128)(2,1)S(1)}, bf16[320]{0:T(512)(128)(2,1)S(1)}, u32[]{:S(2)}, u32[]{:S(2)}) collective-permute-start(bf16[320]{0:T(512)(128)(2,1)S(1)} %slice_reduce_fusion), channel_id=1, source_target_pairs={{0,2},{1,3},{2,0},{3,1},{4,6},{5,7},{6,4},{7,5},{8,10},{9,11},{10,... | collective-permute-start | bytes 1928 | tf_op jit(solution)/shard_map/ppermute | solution.py:100
  31.2 0.5 collective-permute-start
  31.7 0.1 convert_reduce_fusion
  31.8 0.2 fusion.4
  32.0 0.5 fusion
  32.5 0.0 collective-permute-done.3
  32.6 0.0 collective-permute-done.2
  32.6 0.5 select_reduce_fusion
  33.1 0.0 copy-start
  33.1 0.6 %copy-done = s32[128]{0:T(128)S(1)} copy-done((s32[128]{0:T(128)S(1)}, s32[128]{0:T(128)}, u32[]{:S(2)}) %copy-start) | copy-done | bytes 536
  33.8 0.1 fusion.5
  33.9 0.2 reduce_window_sum.11
  34.0 0.2 select_reduce_fusion.2
  34.3 0.0 collective-permute-done.1
  34.3 13.3 %collective-permute-done = bf16[320,1024]{1,0:T(8,128)(2,1)S(1)} collective-permute-done((bf16[320,1024]{1,0:T(8,128)(2,1)S(1)}, bf16[320,1024]{1,0:T(8,128)(2,1)S(1)}, u32[]{:S(2)}, u32[]{:S(2)}) %collective-permute-start) | collective-permute-done | bytes 655392 | tf_op jit(solution)/shard_map/ppermute | solution.py:100
  47.7 0.5 fusion.2
  48.2 0.1 collective-permute-start.4
  48.3 0.5 fusion.1
  48.8 0.6 collective-permute-done.4
  49.4 0.1 reshape.28
  49.5 10.0 %all_to_all.11 = f32[8,8,128]{2,1,0:T(8,128)S(1)} all-to-all(f32[8,8,128]{2,1,0:T(8,128)S(1)} %pad.4), channel_id=1, replica_groups=mesh['dp'=8,'pair'=4] {'dp'}, dimensions={0} | all-to-all | bytes 65536 | tf_op jit(solution)/shard_map/all_to_all | solution.py:135
  59.6 0.1 broadcast_in_dim.21
  59.6 0.6 %select_reduce_fusion.1 = f32[128]{0:T(128)} fusion(pred[320,128]{1,0:T(8,128)(4,1)S(1)} %iota_compare_fusion.1, f32[320]{0:T(512)S(1)} %broadcast_in_dim.21), kind=kLoop, calls=%fused_computation.11 | loop fusion | flops 81792 | bytes 42752 | tf_op jit(solution)/shard_map/reduce_sum | solution.py:137
  (14 shorter events, 0.1 us)
Async XLA Ops:
  28.9 3.7 %collective-permute-start.2 = (bf16[320,1024]{1,0:T(8,128)(2,1)S(1)}, bf16[320,1024]{1,0:T(8,128)(2,1)S(1)}, u32[]{:S(2)}, u32[]{:S(2)}) collective-permute-start(bf16[320,1024]{1,0:T(8,128)(2,1)S(1)} %slice.12), channel_id=1, source_target_pairs={{0,1},{1,0},{2,3},{3,2},{4,5},{5,4},{6,7},{7,6},{8,9},{9,8},{10,11... | collective-permute-start | bytes 1966088 | tf_op jit(solution)/shard_map/ppermute | solution.py:107
  29.1 3.4 %collective-permute-start.3 = (bf16[320]{0:T(512)(128)(2,1)S(1)}, bf16[320]{0:T(512)(128)(2,1)S(1)}, u32[]{:S(2)}, u32[]{:S(2)}) collective-permute-start(bf16[320]{0:T(512)(128)(2,1)S(1)} %slice_reduce_fusion), channel_id=1, source_target_pairs={{0,1},{1,0},{2,3},{3,2},{4,5},{5,4},{6,7},{7,6},{8,9},{9,8},{10,11... | collective-permute-start | bytes 1928 | tf_op jit(solution)/shard_map/ppermute | solution.py:107
  29.7 4.6 %collective-permute-start.1 = (bf16[320]{0:T(512)(128)(2,1)S(1)}, bf16[320]{0:T(512)(128)(2,1)S(1)}, u32[]{:S(2)}, u32[]{:S(2)}) collective-permute-start(bf16[320]{0:T(512)(128)(2,1)S(1)} %slice_reduce_fusion), channel_id=1, source_target_pairs={{0,2},{1,3},{2,0},{3,1},{4,6},{5,7},{6,4},{7,5},{8,10},{9,11},{10,... | collective-permute-start | bytes 1928 | tf_op jit(solution)/shard_map/ppermute | solution.py:100
  31.2 16.4 %collective-permute-start = (bf16[320,1024]{1,0:T(8,128)(2,1)S(1)}, bf16[320,1024]{1,0:T(8,128)(2,1)S(1)}, u32[]{:S(2)}, u32[]{:S(2)}) collective-permute-start(bf16[320,1024]{1,0:T(8,128)(2,1)S(1)} %slice.12), channel_id=1, source_target_pairs={{0,2},{1,3},{2,0},{3,1},{4,6},{5,7},{6,4},{7,5},{8,10},{9,11},{10,... | collective-permute-start | bytes 1966088 | tf_op jit(solution)/shard_map/ppermute | solution.py:100
  33.1 0.7 %copy-start = (s32[128]{0:T(128)S(1)}, s32[128]{0:T(128)}, u32[]{:S(2)}) copy-start(s32[128]{0:T(128)} %param.3) | copy-start | bytes 1540
  48.2 1.2 %collective-permute-start.4 = (f32[320]{0:T(512)S(1)}, f32[320]{0:T(512)S(1)}, u32[]{:S(2)}, u32[]{:S(2)}) collective-permute-start(f32[320]{0:T(512)S(1)} %fusion.2), channel_id=1, source_target_pairs={{0,1},{1,0},{2,3},{3,2},{4,5},{5,4},{6,7},{7,6},{8,9},{9,8},{10,11... | collective-permute-start | bytes 3848 | tf_op jit(solution)/shard_map/ppermute | solution.py:131

commit v18 on v13

--- a/solution.py
+++ b/solution.py
@@ -42,8 +42,11 @@
     slot_ref[...] = slot_row
     place = (lax.broadcasted_iota(jnp.int32, (slots, rows), 0) == slot_row).astype(jnp.bfloat16)
     out_ref[:, :width] = jnp.dot(place, unit, preferred_element_type=jnp.float32).astype(jnp.bfloat16)
+    tag_lane = lax.broadcasted_iota(jnp.int32, (rows, 128), 1)
     tag_source = jnp.where(
-        lax.broadcasted_iota(jnp.int32, (rows, 128), 1) == 0, jnp.bitwise_and(lcol, CPO - 1) + 1, 0
+        tag_lane == 0,
+        jnp.bitwise_and(lcol, CPO - 1) + 1,
+        jnp.where(tag_lane == 1, lax.broadcasted_iota(jnp.int32, (rows, 128), 0) + 1, 0),
     ).astype(jnp.bfloat16)
     tags = jnp.dot(place, tag_source, preferred_element_type=jnp.float32) - 1.0
     out_ref[:, width:] = tags.astype(jnp.bfloat16)
@@ -87,16 +90,17 @@
         rank = jnp.sum(jnp.cumsum(onehot, axis=0) * onehot, axis=1) - 1
         slot = owner * capacity + rank
         tag_source = jnp.zeros((rows, 128), jnp.bfloat16).at[:, 0].set((local + 1).astype(jnp.bfloat16))
+        tag_source = tag_source.at[:, 1].set((jnp.arange(rows) + 1).astype(jnp.bfloat16))
         source = jnp.concatenate([unit, tag_source], axis=1)
         place = slot[None, :] == jnp.arange(slots, dtype=jnp.int32)[:, None]
         outgoing = jnp.dot(place.astype(jnp.bfloat16), source, preferred_element_type=jnp.float32)
         outgoing = (outgoing - jnp.where(jnp.arange(width + 128) >= width, 1.0, 0.0)).astype(jnp.bfloat16)
-    place = slot[None, :] == jnp.arange(slots, dtype=jnp.int32)[:, None]
     outgoing = outgoing.reshape(groups, capacity, width + 128)
     block = lax.all_to_all(outgoing, "dp", split_axis=0, concat_axis=0, tiled=True)
     block = block.reshape(slots, width + 128)
     top = peers // 2
     own = (block[:, :width], block[:, width])
+    source_row = block[:, width + 1].astype(jnp.int32).reshape(groups, capacity)
     far = lax.ppermute(own, "pair", [(p, p ^ top) for p in range(peers)]) if top else None
 
     def spread(x):
@@ -124,11 +128,11 @@
     if far is not None:
         far, best = lax.optimization_barrier((far, best))
         best = jnp.maximum(best, best_over(spread(far), False))
-    lanes = -(-capacity // 128) * 128
-    sent = jnp.pad(best.reshape(groups, 1, capacity), ((0, 0), (0, 7), (0, lanes - capacity)))
+    at_row = source_row[:, :, None] == jnp.arange(rows, dtype=jnp.int32)[None, None, :]
+    by_row = jnp.sum(jnp.where(at_row, best.reshape(groups, capacity, 1), 0.0), axis=1)
+    sent = jnp.pad(by_row[:, None, :], ((0, 0), (0, 7), (0, 0)))
     returned = lax.all_to_all(sent, "dp", split_axis=0, concat_axis=0, tiled=True)
-    returned = returned[:, 0, :capacity].reshape(slots)
-    return jnp.sum(jnp.where(place, returned[:, None], 0.0), axis=0)
+    return jnp.sum(returned[:, 0, :], axis=0)
 
 
 def solution(mesh):

time: 60.6 us -> 59.9 us (0.988)
  local copies, waits for them, and re-layouts: 1.03 us -> 0.35 us
    unnamed x2 -> x0, local copies, waits for them, and re-layouts: 0.66 us -> none
  transfers between devices with their start and end apart: 6 -> 6, of which waited for: 2 -> 2; matrix products, arithmetic and copies ran while one was open for 3% -> 4% of each run, Pallas kernels for 0% -> 0%
where the time goes in v18:
time: 59.9 us; the launch traced here: 59.7 us
  blocking collectives  36.4 us (61%)
  waiting for transfers between devices  14.2 us (24%)
  starting transfers between devices  2.91 us (5%)
  Pallas kernels  2.41 us (4%)
  matrix products  2.17 us (4%)
  other arithmetic  1.15 us (2%)
    all_to_all x1, blocking collectives, shards(): lax.all_to_all(outgoing, 'dp', split_axis=0, concat_axis=0, tiled=True)  26.4 us
    ppermute x2, waiting for transfers between devices, shards(): lax.ppermute(own, 'pair', [(p, p ^ top) for p in range(peers)])  13.2 us
    all_to_all x1, blocking collectives, shards(): lax.all_to_all(sent, 'dp', split_axis=0, concat_axis=0, tiled=True)  10 us
    pallas_call x1, Pallas kernels, prepare(): pl.pallas_call(functools.partial(prepare_kernel, groups=groups, capacity=...  2.41 us
    dot_general x4, matrix products, piece_best(): jnp.einsum('id,jd->ij', left, right, preferred_element_type=jnp.float32)  2.17 us
    ppermute x2, starting transfers between devices, shards(): lax.ppermute(own, 'pair', [(p, p ^ top) for p in range(peers)])  2.09 us
  transfers between devices with their start and end apart: 6, of which 2 were waited for; matrix products, arithmetic and copies ran while one was open for 4% of the time, Pallas kernels for 0%

profile of v18, /device:TPU:0, one launch (start us, length us, event | category | flops | bytes accessed | tf_op | source)
XLA Modules:
  0.0 59.7 jit_solution(8687509074834351448)
XLA Ops:
  0.0 2.4 %shard_map.28 = (bf16[320,1152]{1,0:T(8,128)(2,1)}, s32[1,128]{1,0:T(1,128)}) custom-call(f32[128,1024]{1,0:T(8,128)} %emb_ref.1, s32[1,128]{1,0:T(1,128)} %bitcast.19), custom_call_target="tpu_custom_call" | custom-call | flops 94896128 | bytes 1261568 | tf_op jit(solution)/shard_map/pallas_call | solution.py:59
  2.4 26.4 %all_to_all.10 = bf16[8,40,1152]{2,1,0:T(8,128)(2,1)S(1)} all-to-all(bf16[8,40,1152]{2,1,0:T(8,128)(2,1)} %bitcast.17), channel_id=1, replica_groups=mesh['dp'=8,'pair'=4] {'dp'}, dimensions={0} | all-to-all | bytes 1474560 | tf_op jit(solution)/shard_map/all_to_all | solution.py:99
  28.8 0.1 slice.17
  28.9 0.1 collective-permute-start.3
  29.0 1.6 %collective-permute-start = (bf16[320,1024]{1,0:T(8,128)(2,1)S(1)}, bf16[320,1024]{1,0:T(8,128)(2,1)S(1)}, u32[]{:S(2)}, u32[]{:S(2)}) collective-permute-start(bf16[320,1024]{1,0:T(8,128)(2,1)S(1)} %slice.17), channel_id=1, source_target_pairs={{0,2},{1,3},{2,0},{3,1},{4,6},{5,7},{6,4},{7,5},{8,10},{9,11},{10,... | collective-permute-start | bytes 1966088 | tf_op jit(solution)/shard_map/ppermute | solution.py:104
  30.5 0.1 slice_reduce_fusion
  30.7 0.2 collective-permute-start.2
  30.9 0.5 collective-permute-start.1
  31.4 0.1 fusion.3
  31.6 0.3 convert_reduce_fusion.1
  31.9 0.5 fusion
  32.4 0.0 collective-permute-done.2
  32.4 0.0 collective-permute-done.3
  32.4 0.5 select_reduce_fusion.1
  33.0 13.2 %collective-permute-done.1 = bf16[320]{0:T(512)(128)(2,1)S(1)} collective-permute-done((bf16[320]{0:T(512)(128)(2,1)S(1)}, bf16[320]{0:T(512)(128)(2,1)S(1)}, u32[]{:S(2)}, u32[]{:S(2)}) %collective-permute-start.1) | collective-permute-done | bytes 672 | tf_op jit(solution)/shard_map/ppermute | solution.py:104
  46.2 0.0 collective-permute-done
  46.2 0.0 collective-permute-start.5
  46.2 0.1 reshape.26
  46.3 0.5 collective-permute-start.4
  46.8 0.5 fusion.1
  47.3 1.0 %collective-permute-done.4 = bf16[320]{0:T(512)(128)(2,1)S(1)} collective-permute-done((bf16[320]{0:T(512)(128)(2,1)S(1)}, bf16[320]{0:T(512)(128)(2,1)S(1)}, u32[]{:S(2)}, u32[]{:S(2)}) %collective-permute-start.4) | collective-permute-done | bytes 672 | tf_op jit(solution)/shard_map/ppermute | solution.py:111
  48.3 0.0 collective-permute-done.5
  48.3 0.5 select_reduce_fusion
  48.9 0.1 broadcast_in_dim.44
  48.9 0.2 select_reduce_fusion.2
  49.1 10.0 %all_to_all.11 = f32[8,8,128]{2,1,0:T(8,128)S(1)} all-to-all(f32[8,8,128]{2,1,0:T(8,128)S(1)} %pad.4.clone), channel_id=1, replica_groups=mesh['dp'=8,'pair'=4] {'dp'}, dimensions={0} | all-to-all | bytes 65536 | tf_op jit(solution)/shard_map/all_to_all | solution.py:134
  59.2 0.5 slice_reduce_fusion.1
  (7 shorter events, 0.0 us)
Async XLA Ops:
  28.9 3.5 %collective-permute-start.3 = (bf16[320,1024]{1,0:T(8,128)(2,1)S(1)}, bf16[320,1024]{1,0:T(8,128)(2,1)S(1)}, u32[]{:S(2)}, u32[]{:S(2)}) collective-permute-start(bf16[320,1024]{1,0:T(8,128)(2,1)S(1)} %slice.17), channel_id=1, source_target_pairs={{0,1},{1,0},{2,3},{3,2},{4,5},{5,4},{6,7},{7,6},{8,9},{9,8},{10,11... | collective-permute-start | bytes 1966088 | tf_op jit(solution)/shard_map/ppermute | solution.py:111
  29.0 17.2 %collective-permute-start = (bf16[320,1024]{1,0:T(8,128)(2,1)S(1)}, bf16[320,1024]{1,0:T(8,128)(2,1)S(1)}, u32[]{:S(2)}, u32[]{:S(2)}) collective-permute-start(bf16[320,1024]{1,0:T(8,128)(2,1)S(1)} %slice.17), channel_id=1, source_target_pairs={{0,2},{1,3},{2,0},{3,1},{4,6},{5,7},{6,4},{7,5},{8,10},{9,11},{10,... | collective-permute-start | bytes 1966088 | tf_op jit(solution)/shard_map/ppermute | solution.py:104
  30.7 1.8 %collective-permute-start.2 = (bf16[320]{0:T(512)(128)(2,1)S(1)}, bf16[320]{0:T(512)(128)(2,1)S(1)}, u32[]{:S(2)}, u32[]{:S(2)}) collective-permute-start(bf16[320]{0:T(512)(128)(2,1)S(1)} %slice_reduce_fusion), channel_id=1, source_target_pairs={{0,1},{1,0},{2,3},{3,2},{4,5},{5,4},{6,7},{7,6},{8,9},{9,8},{10,11... | collective-permute-start | bytes 1928 | tf_op jit(solution)/shard_map/ppermute | solution.py:111
  30.9 15.3 %collective-permute-start.1 = (bf16[320]{0:T(512)(128)(2,1)S(1)}, bf16[320]{0:T(512)(128)(2,1)S(1)}, u32[]{:S(2)}, u32[]{:S(2)}) collective-permute-start(bf16[320]{0:T(512)(128)(2,1)S(1)} %slice_reduce_fusion), channel_id=1, source_target_pairs={{0,2},{1,3},{2,0},{3,1},{4,6},{5,7},{6,4},{7,5},{8,10},{9,11},{10,... | collective-permute-start | bytes 1928 | tf_op jit(solution)/shard_map/ppermute | solution.py:104
  46.2 2.1 %collective-permute-start.5 = (bf16[320,1024]{1,0:T(8,128)(2,1)S(1)}, bf16[320,1024]{1,0:T(8,128)(2,1)S(1)}, u32[]{:S(2)}, u32[]{:S(2)}) collective-permute-start(bf16[320,1024]{1,0:T(8,128)(2,1)S(1)} %collective-permute-done), channel_id=1, source_target_pairs={{0,1},{1,0},{2,3},{3,2},{4,5},{5,4},{6,7},{7,6},{8,9},{9,8},{10,11... | collective-permute-start | bytes 1966088 | tf_op jit(solution)/shard_map/ppermute | solution.py:111
  46.3 2.0 %collective-permute-start.4 = (bf16[320]{0:T(512)(128)(2,1)S(1)}, bf16[320]{0:T(512)(128)(2,1)S(1)}, u32[]{:S(2)}, u32[]{:S(2)}) collective-permute-start(bf16[320]{0:T(512)(128)(2,1)S(1)} %collective-permute-done.1), channel_id=1, source_target_pairs={{0,1},{1,0},{2,3},{3,2},{4,5},{5,4},{6,7},{7,6},{8,9},{9,8},{10,11... | collective-permute-start | bytes 1928 | tf_op jit(solution)/shard_map/ppermute | solution.py:111

commit v19 on v15

--- a/solution.py
+++ b/solution.py
@@ -34,8 +34,8 @@
     first = lax.broadcasted_iota(jnp.int32, (rows, rows), 0)
     second = lax.broadcasted_iota(jnp.int32, (rows, rows), 1)
     diagonal = first == second
-    ocol = jnp.sum(jnp.where(diagonal, orow, 0), axis=1, keepdims=True)
     lcol = jnp.sum(jnp.where(diagonal, lrow, 0), axis=1, keepdims=True)
+    ocol = lax.shift_right_logical(lcol, shift)
     same = ocol == orow
     rank_row = jnp.sum(jnp.where(same & (first < second), 1, 0), axis=0, keepdims=True)
     slot_row = orow * capacity + rank_row

time: 60 us -> 60 us (level)
  no operation moved by 1% of the time
where the time goes in v19:
time: 60 us; the launch traced here: 59.7 us
  blocking collectives  36.4 us (61%)
  waiting for transfers between devices  13.6 us (23%)
  starting transfers between devices  2.97 us (5%)
  Pallas kernels  2.4 us (4%)
  matrix products  2.17 us (4%)
  local copies, waits for them, and re-layouts  1.03 us (2%)
  other arithmetic  1 us (2%)
    all_to_all x1, blocking collectives, shards(): lax.all_to_all(outgoing, 'dp', split_axis=0, concat_axis=0, tiled=True)  26.4 us
    ppermute x2, waiting for transfers between devices, shards(): lax.ppermute(own, 'pair', [(p, p ^ top) for p in range(peers)])  13.3 us
    all_to_all x1, blocking collectives, shards(): lax.all_to_all(sent, 'dp', split_axis=0, concat_axis=0, tiled=True)  10 us
    pallas_call x1, Pallas kernels, prepare(): pl.pallas_call(functools.partial(prepare_kernel, groups=groups, capacity=...  2.4 us
    dot_general x4, matrix products, piece_best(): jnp.einsum('id,jd->ij', left, right, preferred_element_type=jnp.float32)  2.17 us
    ppermute x2, starting transfers between devices, shards(): lax.ppermute(own, 'pair', [(p, p ^ top) for p in range(peers)])  2.09 us
  transfers between devices with their start and end apart: 6, of which 2 were waited for; matrix products, arithmetic and copies ran while one was open for 4% of the time, Pallas kernels for 0%

profile of v19, /device:TPU:0, one launch (start us, length us, event | category | flops | bytes accessed | tf_op | source)
XLA Modules:
  0.0 59.7 jit_solution(9557195983847167844)
XLA Ops:
  0.0 2.4 %shard_map.28 = (bf16[320,1152]{1,0:T(8,128)(2,1)}, s32[1,128]{1,0:T(1,128)}) custom-call(f32[128,1024]{1,0:T(8,128)} %emb_ref.1, s32[1,128]{1,0:T(1,128)} %bitcast.16), custom_call_target="tpu_custom_call" | custom-call | flops 94896128 | bytes 1261568 | tf_op jit(solution)/shard_map/pallas_call | solution.py:56
  2.4 26.4 %all_to_all.10 = bf16[8,40,1152]{2,1,0:T(8,128)(2,1)S(1)} all-to-all(bf16[8,40,1152]{2,1,0:T(8,128)(2,1)} %bitcast.15), channel_id=1, replica_groups=mesh['dp'=8,'pair'=4] {'dp'}, dimensions={0} | all-to-all | bytes 1474560 | tf_op jit(solution)/shard_map/all_to_all | solution.py:96
  28.8 0.1 slice.12
  28.9 0.1 collective-permute-start.3
  29.0 1.6 %collective-permute-start = (bf16[320,1024]{1,0:T(8,128)(2,1)S(1)}, bf16[320,1024]{1,0:T(8,128)(2,1)S(1)}, u32[]{:S(2)}, u32[]{:S(2)}) collective-permute-start(bf16[320,1024]{1,0:T(8,128)(2,1)S(1)} %slice.12), channel_id=1, source_target_pairs={{0,2},{1,3},{2,0},{3,1},{4,6},{5,7},{6,4},{7,5},{8,10},{9,11},{10,... | collective-permute-start | bytes 1966088 | tf_op jit(solution)/shard_map/ppermute | solution.py:100
  30.5 0.1 slice_reduce_fusion
  30.6 0.2 collective-permute-start.2
  30.9 0.5 collective-permute-start.1
  31.4 0.1 convert_reduce_fusion
  31.6 0.2 fusion.3
  31.7 0.5 fusion
  32.3 0.0 collective-permute-done.2
  32.3 0.0 collective-permute-done.3
  32.3 0.5 select_reduce_fusion.1
  32.9 13.3 %collective-permute-done.1 = bf16[320]{0:T(512)(128)(2,1)S(1)} collective-permute-done((bf16[320]{0:T(512)(128)(2,1)S(1)}, bf16[320]{0:T(512)(128)(2,1)S(1)}, u32[]{:S(2)}, u32[]{:S(2)}) %collective-permute-start.1) | collective-permute-done | bytes 672 | tf_op jit(solution)/shard_map/ppermute | solution.py:100
  46.2 0.0 collective-permute-done
  46.2 0.0 collective-permute-start.5
  46.2 0.0 copy-start
  46.2 0.7 %copy-done = s32[1,128]{1,0:T(1,128)S(1)} copy-done((s32[1,128]{1,0:T(1,128)S(1)}, s32[1,128]{1,0:T(1,128)}, u32[]{:S(2)}) %copy-start) | copy-done | bytes 536
  46.9 0.6 collective-permute-start.4
  47.5 0.5 fusion.1
  48.0 0.3 collective-permute-done.4
  48.3 0.0 collective-permute-done.5
  48.3 0.5 select_reduce_fusion
  48.9 0.1 reshape.21
  49.0 10.0 %all_to_all.11 = f32[8,8,128]{2,1,0:T(8,128)S(1)} all-to-all(f32[8,8,128]{2,1,0:T(8,128)S(1)} %pad.4), channel_id=1, replica_groups=mesh['dp'=8,'pair'=4] {'dp'}, dimensions={0} | all-to-all | bytes 65536 | tf_op jit(solution)/shard_map/all_to_all | solution.py:130
  59.0 0.1 broadcast_in_dim.21
  59.1 0.6 %select_reduce_fusion.2 = f32[128]{0:T(128)} fusion(pred[320,128]{1,0:T(8,128)(4,1)S(1)} %iota_compare_fusion.1, f32[320]{0:T(512)S(1)} %broadcast_in_dim.21), kind=kLoop, calls=%fused_computation.10 | loop fusion | flops 81792 | bytes 42752 | tf_op jit(solution)/shard_map/reduce_sum | solution.py:132
  (9 shorter events, 0.1 us)
Async XLA Ops:
  28.9 3.4 %collective-permute-start.3 = (bf16[320,1024]{1,0:T(8,128)(2,1)S(1)}, bf16[320,1024]{1,0:T(8,128)(2,1)S(1)}, u32[]{:S(2)}, u32[]{:S(2)}) collective-permute-start(bf16[320,1024]{1,0:T(8,128)(2,1)S(1)} %slice.12), channel_id=1, source_target_pairs={{0,1},{1,0},{2,3},{3,2},{4,5},{5,4},{6,7},{7,6},{8,9},{9,8},{10,11... | collective-permute-start | bytes 1966088 | tf_op jit(solution)/shard_map/ppermute | solution.py:107
  29.0 17.2 %collective-permute-start = (bf16[320,1024]{1,0:T(8,128)(2,1)S(1)}, bf16[320,1024]{1,0:T(8,128)(2,1)S(1)}, u32[]{:S(2)}, u32[]{:S(2)}) collective-permute-start(bf16[320,1024]{1,0:T(8,128)(2,1)S(1)} %slice.12), channel_id=1, source_target_pairs={{0,2},{1,3},{2,0},{3,1},{4,6},{5,7},{6,4},{7,5},{8,10},{9,11},{10,... | collective-permute-start | bytes 1966088 | tf_op jit(solution)/shard_map/ppermute | solution.py:100
  30.6 1.6 %collective-permute-start.2 = (bf16[320]{0:T(512)(128)(2,1)S(1)}, bf16[320]{0:T(512)(128)(2,1)S(1)}, u32[]{:S(2)}, u32[]{:S(2)}) collective-permute-start(bf16[320]{0:T(512)(128)(2,1)S(1)} %slice_reduce_fusion), channel_id=1, source_target_pairs={{0,1},{1,0},{2,3},{3,2},{4,5},{5,4},{6,7},{7,6},{8,9},{9,8},{10,11... | collective-permute-start | bytes 1928 | tf_op jit(solution)/shard_map/ppermute | solution.py:107
  30.9 15.3 %collective-permute-start.1 = (bf16[320]{0:T(512)(128)(2,1)S(1)}, bf16[320]{0:T(512)(128)(2,1)S(1)}, u32[]{:S(2)}, u32[]{:S(2)}) collective-permute-start(bf16[320]{0:T(512)(128)(2,1)S(1)} %slice_reduce_fusion), channel_id=1, source_target_pairs={{0,2},{1,3},{2,0},{3,1},{4,6},{5,7},{6,4},{7,5},{8,10},{9,11},{10,... | collective-permute-start | bytes 1928 | tf_op jit(solution)/shard_map/ppermute | solution.py:100
  46.2 2.1 %collective-permute-start.5 = (bf16[320,1024]{1,0:T(8,128)(2,1)S(1)}, bf16[320,1024]{1,0:T(8,128)(2,1)S(1)}, u32[]{:S(2)}, u32[]{:S(2)}) collective-permute-start(bf16[320,1024]{1,0:T(8,128)(2,1)S(1)} %collective-permute-done), channel_id=1, source_target_pairs={{0,1},{1,0},{2,3},{3,2},{4,5},{5,4},{6,7},{7,6},{8,9},{9,8},{10,11... | collective-permute-start | bytes 1966088 | tf_op jit(solution)/shard_map/ppermute | solution.py:107
  46.2 0.7 %copy-start = (s32[1,128]{1,0:T(1,128)S(1)}, s32[1,128]{1,0:T(1,128)}, u32[]{:S(2)}) copy-start(s32[1,128]{1,0:T(1,128)} %get-tuple-element.12) | copy-start | bytes 1540
  46.9 1.4 %collective-permute-start.4 = (bf16[320]{0:T(512)(128)(2,1)S(1)}, bf16[320]{0:T(512)(128)(2,1)S(1)}, u32[]{:S(2)}, u32[]{:S(2)}) collective-permute-start(bf16[320]{0:T(512)(128)(2,1)S(1)} %collective-permute-done.1), channel_id=1, source_target_pairs={{0,1},{1,0},{2,3},{3,2},{4,5},{5,4},{6,7},{7,6},{8,9},{9,8},{10,11... | collective-permute-start | bytes 1928 | tf_op jit(solution)/shard_map/ppermute | solution.py:107

commit v20 on v19

--- a/solution.py
+++ b/solution.py
@@ -123,7 +123,10 @@
     best = best_over(spread(own), True)
     if far is not None:
         far, best = lax.optimization_barrier((far, best))
-        best = jnp.maximum(best, best_over(spread(far), False))
+        half = slots // 2
+        for part in (slice(0, half), slice(half, slots)):
+            rows_part = (far[0][part], far[1][part])
+            best = jnp.maximum(best, best_over(spread(rows_part), False))
     place, best = lax.optimization_barrier((place, best))
     lanes = -(-capacity // 128) * 128
     sent = jnp.pad(best.reshape(groups, 1, capacity), ((0, 0), (0, 7), (0, lanes - capacity)))

time: 60 us -> 61.3 us (1.022)
    dot_general x4 -> x6, matrix products: 2.17 us -> 2.78 us  [piece_best(): jnp.einsum('id,jd->ij', left, right, preferred_element_type=jnp.float32)]
    ppermute x4 -> x6, starting transfers between devices: 0.88 us -> 1.43 us  [spread(): pieces = pieces + [lax.ppermute(y, 'pair', perm) for y in pieces]]
  transfers between devices with their start and end apart: 6 -> 8, of which waited for: 2 -> 2; matrix products, arithmetic and copies ran while one was open for 4% -> 5% of each run, Pallas kernels for 0% -> 0%
where the time goes in v20:
time: 61.3 us; the launch traced here: 61 us
  blocking collectives  36.4 us (59%)
  waiting for transfers between devices  13.6 us (22%)
  starting transfers between devices  3.52 us (6%)
  matrix products  2.78 us (5%)
  Pallas kernels  2.4 us (4%)
  other arithmetic  1.09 us (2%)
  local copies, waits for them, and re-layouts  1.07 us (2%)
    all_to_all x1, blocking collectives, shards(): lax.all_to_all(outgoing, 'dp', split_axis=0, concat_axis=0, tiled=True)  26.4 us
    ppermute x2, waiting for transfers between devices, shards(): lax.ppermute(own, 'pair', [(p, p ^ top) for p in range(peers)])  13.3 us
    all_to_all x1, blocking collectives, shards(): lax.all_to_all(sent, 'dp', split_axis=0, concat_axis=0, tiled=True)  10 us
    dot_general x6, matrix products, piece_best(): jnp.einsum('id,jd->ij', left, right, preferred_element_type=jnp.float32)  2.78 us
    pallas_call x1, Pallas kernels, prepare(): pl.pallas_call(functools.partial(prepare_kernel, groups=groups, capacity=...  2.4 us
    ppermute x2, starting transfers between devices, shards(): lax.ppermute(own, 'pair', [(p, p ^ top) for p in range(peers)])  2.09 us
    ppermute x6, starting transfers between devices, spread(): pieces = pieces + [lax.ppermute(y, 'pair', perm) for y in pieces]  1.43 us
  transfers between devices with their start and end apart: 8, of which 2 were waited for; matrix products, arithmetic and copies ran while one was open for 5% of the time, Pallas kernels for 0%

profile of v20, /device:TPU:0, one launch (start us, length us, event | category | flops | bytes accessed | tf_op | source)
XLA Modules:
  0.0 61.0 jit_solution(2602754836924902668)
XLA Ops:
  0.0 2.4 %shard_map.28 = (bf16[320,1152]{1,0:T(8,128)(2,1)}, s32[1,128]{1,0:T(1,128)}) custom-call(f32[128,1024]{1,0:T(8,128)} %emb_ref.1, s32[1,128]{1,0:T(1,128)} %bitcast.18), custom_call_target="tpu_custom_call" | custom-call | flops 94896128 | bytes 1261568 | tf_op jit(solution)/shard_map/pallas_call | solution.py:56
  2.4 26.4 %all_to_all.10 = bf16[8,40,1152]{2,1,0:T(8,128)(2,1)S(1)} all-to-all(bf16[8,40,1152]{2,1,0:T(8,128)(2,1)} %bitcast.17), channel_id=1, replica_groups=mesh['dp'=8,'pair'=4] {'dp'}, dimensions={0} | all-to-all | bytes 1474560 | tf_op jit(solution)/shard_map/all_to_all | solution.py:96
  28.8 0.1 slice.28
  28.9 0.1 collective-permute-start.3
  29.0 0.0 copy-start
  29.0 0.6 %copy-done = s32[1,128]{1,0:T(1,128)S(1)} copy-done((s32[1,128]{1,0:T(1,128)S(1)}, s32[1,128]{1,0:T(1,128)}, u32[]{:S(2)}) %copy-start) | copy-done | bytes 536
  29.7 1.6 %collective-permute-start = (bf16[320,1024]{1,0:T(8,128)(2,1)S(1)}, bf16[320,1024]{1,0:T(8,128)(2,1)S(1)}, u32[]{:S(2)}, u32[]{:S(2)}) collective-permute-start(bf16[320,1024]{1,0:T(8,128)(2,1)S(1)} %slice.28), channel_id=1, source_target_pairs={{0,2},{1,3},{2,0},{3,1},{4,6},{5,7},{6,4},{7,5},{8,10},{9,11},{10,... | collective-permute-start | bytes 1966088 | tf_op jit(solution)/shard_map/ppermute | solution.py:100
  31.2 0.1 slice_reduce_fusion
  31.4 0.3 collective-permute-start.2
  31.6 0.5 collective-permute-start.1
  32.2 0.1 convert_reduce_fusion
  32.3 0.2 fusion.4
  32.5 0.5 fusion
  33.0 0.0 collective-permute-done.2
  33.0 0.0 collective-permute-done.3
  33.1 0.5 select_reduce_fusion
  33.6 13.3 %collective-permute-done.1 = bf16[320]{0:T(512)(128)(2,1)S(1)} collective-permute-done((bf16[320]{0:T(512)(128)(2,1)S(1)}, bf16[320]{0:T(512)(128)(2,1)S(1)}, u32[]{:S(2)}, u32[]{:S(2)}) %collective-permute-start.1) | collective-permute-done | bytes 672 | tf_op jit(solution)/shard_map/ppermute | solution.py:100
  46.9 0.0 collective-permute-done
  46.9 0.1 fusion.23
  47.1 0.1 collective-permute-start.4
  47.1 0.5 collective-permute-start.6
  47.6 0.1 collective-permute-start.5
  47.7 0.4 collective-permute-start.7
  48.1 0.4 fusion.1
  48.6 0.4 fusion.2
  49.0 0.0 collective-permute-done.4
  49.0 0.0 collective-permute-done.6
  49.0 0.2 collective-permute-done.5
  49.3 0.4 select_reduce_fusion.2
  49.7 0.0 collective-permute-done.7
  49.7 0.4 select_reduce_fusion.1
  50.2 0.1 reshape.23
  50.3 10.0 %all_to_all.11 = f32[8,8,128]{2,1,0:T(8,128)S(1)} all-to-all(f32[8,8,128]{2,1,0:T(8,128)S(1)} %pad.4), channel_id=1, replica_groups=mesh['dp'=8,'pair'=4] {'dp'}, dimensions={0} | all-to-all | bytes 65536 | tf_op jit(solution)/shard_map/all_to_all | solution.py:133
  60.3 0.1 broadcast_in_dim.27
  60.4 0.6 %select_reduce_fusion.3 = f32[128]{0:T(128)} fusion(pred[320,128]{1,0:T(8,128)(4,1)S(1)} %iota_compare_fusion.1, f32[320]{0:T(512)S(1)} %broadcast_in_dim.27), kind=kLoop, calls=%fused_computation.13 | loop fusion | flops 81792 | bytes 42752 | tf_op jit(solution)/shard_map/reduce_sum | solution.py:135
  (10 shorter events, 0.1 us)
Async XLA Ops:
  28.9 4.1 %collective-permute-start.3 = (bf16[320,1024]{1,0:T(8,128)(2,1)S(1)}, bf16[320,1024]{1,0:T(8,128)(2,1)S(1)}, u32[]{:S(2)}, u32[]{:S(2)}) collective-permute-start(bf16[320,1024]{1,0:T(8,128)(2,1)S(1)} %slice.28), channel_id=1, source_target_pairs={{0,1},{1,0},{2,3},{3,2},{4,5},{5,4},{6,7},{7,6},{8,9},{9,8},{10,11... | collective-permute-start | bytes 1966088 | tf_op jit(solution)/shard_map/ppermute | solution.py:107
  29.0 0.7 %copy-start = (s32[1,128]{1,0:T(1,128)S(1)}, s32[1,128]{1,0:T(1,128)}, u32[]{:S(2)}) copy-start(s32[1,128]{1,0:T(1,128)} %get-tuple-element.12) | copy-start | bytes 1540
  29.7 17.3 %collective-permute-start = (bf16[320,1024]{1,0:T(8,128)(2,1)S(1)}, bf16[320,1024]{1,0:T(8,128)(2,1)S(1)}, u32[]{:S(2)}, u32[]{:S(2)}) collective-permute-start(bf16[320,1024]{1,0:T(8,128)(2,1)S(1)} %slice.28), channel_id=1, source_target_pairs={{0,2},{1,3},{2,0},{3,1},{4,6},{5,7},{6,4},{7,5},{8,10},{9,11},{10,... | collective-permute-start | bytes 1966088 | tf_op jit(solution)/shard_map/ppermute | solution.py:100
  31.4 1.7 %collective-permute-start.2 = (bf16[320]{0:T(512)(128)(2,1)S(1)}, bf16[320]{0:T(512)(128)(2,1)S(1)}, u32[]{:S(2)}, u32[]{:S(2)}) collective-permute-start(bf16[320]{0:T(512)(128)(2,1)S(1)} %slice_reduce_fusion), channel_id=1, source_target_pairs={{0,1},{1,0},{2,3},{3,2},{4,5},{5,4},{6,7},{7,6},{8,9},{9,8},{10,11... | collective-permute-start | bytes 1928 | tf_op jit(solution)/shard_map/ppermute | solution.py:107
  31.6 15.3 %collective-permute-start.1 = (bf16[320]{0:T(512)(128)(2,1)S(1)}, bf16[320]{0:T(512)(128)(2,1)S(1)}, u32[]{:S(2)}, u32[]{:S(2)}) collective-permute-start(bf16[320]{0:T(512)(128)(2,1)S(1)} %slice_reduce_fusion), channel_id=1, source_target_pairs={{0,2},{1,3},{2,0},{3,1},{4,6},{5,7},{6,4},{7,5},{8,10},{9,11},{10,... | collective-permute-start | bytes 1928 | tf_op jit(solution)/shard_map/ppermute | solution.py:100
  47.1 1.9 %collective-permute-start.4 = (bf16[160]{0:T(256)(128)(2,1)S(1)}, bf16[160]{0:T(256)(128)(2,1)S(1)}, u32[]{:S(2)}, u32[]{:S(2)}) collective-permute-start(bf16[160]{0:T(256)(128)(2,1)S(1)} %get-tuple-element.21), channel_id=1, source_target_pairs={{0,1},{1,0},{2,3},{3,2},{4,5},{5,4},{6,7},{7,6},{8,9},{9,8},{10,11... | collective-permute-start | bytes 968 | tf_op jit(solution)/shard_map/ppermute | solution.py:107
  47.1 1.9 %collective-permute-start.6 = (bf16[160]{0:T(256)(128)(2,1)S(1)}, bf16[160]{0:T(256)(128)(2,1)S(1)}, u32[]{:S(2)}, u32[]{:S(2)}) collective-permute-start(bf16[160]{0:T(256)(128)(2,1)S(1)} %get-tuple-element.24), channel_id=1, source_target_pairs={{0,1},{1,0},{2,3},{3,2},{4,5},{5,4},{6,7},{7,6},{8,9},{9,8},{10,11... | collective-permute-start | bytes 968 | tf_op jit(solution)/shard_map/ppermute | solution.py:107
  47.6 1.6 %collective-permute-start.5 = (bf16[160,1024]{1,0:T(8,128)(2,1)S(1)}, bf16[160,1024]{1,0:T(8,128)(2,1)S(1)}, u32[]{:S(2)}, u32[]{:S(2)}) collective-permute-start(bf16[160,1024]{1,0:T(8,128)(2,1)S(1)} %get-tuple-element.19), channel_id=1, source_target_pairs={{0,1},{1,0},{2,3},{3,2},{4,5},{5,4},{6,7},{7,6},{8,9},{9,8},{10,11... | collective-permute-start | bytes 983048 | tf_op jit(solution)/shard_map/ppermute | solution.py:107
  47.7 2.0 %collective-permute-start.7 = (bf16[160,1024]{1,0:T(8,128)(2,1)S(1)}, bf16[160,1024]{1,0:T(8,128)(2,1)S(1)}, u32[]{:S(2)}, u32[]{:S(2)}) collective-permute-start(bf16[160,1024]{1,0:T(8,128)(2,1)S(1)} %get-tuple-element.20), channel_id=1, source_target_pairs={{0,1},{1,0},{2,3},{3,2},{4,5},{5,4},{6,7},{7,6},{8,9},{9,8},{10,11... | collective-permute-start | bytes 983048 | tf_op jit(solution)/shard_map/ppermute | solution.py:107

commit v21 on v19

--- a/solution.py
+++ b/solution.py
@@ -129,7 +129,9 @@
     sent = jnp.pad(best.reshape(groups, 1, capacity), ((0, 0), (0, 7), (0, lanes - capacity)))
     returned = lax.all_to_all(sent, "dp", split_axis=0, concat_axis=0, tiled=True)
     returned = returned[:, 0, :capacity].reshape(slots)
-    return jnp.sum(jnp.where(place, returned[:, None], 0.0), axis=0)
+    return jnp.dot(
+        returned[None, :], place.astype(jnp.float32), precision=lax.Precision.HIGHEST
+    ).reshape(rows)
 
 
 def solution(mesh):

time: 60 us -> 60 us (level)
  matrix products: 2.17 us -> 2.85 us
  other arithmetic: 1 us -> 0.36 us
    dot_general x0 -> x1, matrix products: none -> 0.68 us  [shards(): jnp.dot(returned[None, :], place.astype(jnp.float32), precision=lax.Preci...]
    reduce_sum x1 -> x0, other arithmetic: 0.64 us -> none  [shards(): return jnp.sum(jnp.where(place, returned[:, None], 0.0), axis=0)]
where the time goes in v21:
time: 60 us; the launch traced here: 59.8 us
  blocking collectives  36.4 us (61%)
  waiting for transfers between devices  13.6 us (23%)
  starting transfers between devices  2.97 us (5%)
  matrix products  2.85 us (5%)
  Pallas kernels  2.4 us (4%)
  local copies, waits for them, and re-layouts  1.03 us (2%)
    all_to_all x1, blocking collectives, shards(): lax.all_to_all(outgoing, 'dp', split_axis=0, concat_axis=0, tiled=True)  26.4 us
    ppermute x2, waiting for transfers between devices, shards(): lax.ppermute(own, 'pair', [(p, p ^ top) for p in range(peers)])  13.3 us
    all_to_all x1, blocking collectives, shards(): lax.all_to_all(sent, 'dp', split_axis=0, concat_axis=0, tiled=True)  10 us
    pallas_call x1, Pallas kernels, prepare(): pl.pallas_call(functools.partial(prepare_kernel, groups=groups, capacity=...  2.4 us
    dot_general x4, matrix products, piece_best(): jnp.einsum('id,jd->ij', left, right, preferred_element_type=jnp.float32)  2.17 us
    ppermute x2, starting transfers between devices, shards(): lax.ppermute(own, 'pair', [(p, p ^ top) for p in range(peers)])  2.09 us
  transfers between devices with their start and end apart: 6, of which 2 were waited for; matrix products, arithmetic and copies ran while one was open for 4% of the time, Pallas kernels for 0%

profile of v21, /device:TPU:0, one launch (start us, length us, event | category | flops | bytes accessed | tf_op | source)
XLA Modules:
  0.0 59.8 jit_solution(5034146443036834942)
XLA Ops:
  0.0 2.4 %shard_map.28 = (bf16[320,1152]{1,0:T(8,128)(2,1)}, s32[1,128]{1,0:T(1,128)}) custom-call(f32[128,1024]{1,0:T(8,128)} %emb_ref.1, s32[1,128]{1,0:T(1,128)} %bitcast.20), custom_call_target="tpu_custom_call" | custom-call | flops 94896128 | bytes 1261568 | tf_op jit(solution)/shard_map/pallas_call | solution.py:56
  2.4 26.4 %all_to_all.10 = bf16[8,40,1152]{2,1,0:T(8,128)(2,1)S(1)} all-to-all(bf16[8,40,1152]{2,1,0:T(8,128)(2,1)} %bitcast.19), channel_id=1, replica_groups=mesh['dp'=8,'pair'=4] {'dp'}, dimensions={0} | all-to-all | bytes 1474560 | tf_op jit(solution)/shard_map/all_to_all | solution.py:96
  28.8 0.1 slice.12
  28.9 0.1 collective-permute-start.3
  29.0 1.6 %collective-permute-start = (bf16[320,1024]{1,0:T(8,128)(2,1)S(1)}, bf16[320,1024]{1,0:T(8,128)(2,1)S(1)}, u32[]{:S(2)}, u32[]{:S(2)}) collective-permute-start(bf16[320,1024]{1,0:T(8,128)(2,1)S(1)} %slice.12), channel_id=1, source_target_pairs={{0,2},{1,3},{2,0},{3,1},{4,6},{5,7},{6,4},{7,5},{8,10},{9,11},{10,... | collective-permute-start | bytes 1966088 | tf_op jit(solution)/shard_map/ppermute | solution.py:100
  30.5 0.1 slice_reduce_fusion
  30.6 0.2 collective-permute-start.2
  30.9 0.5 collective-permute-start.1
  31.4 0.1 convert_reduce_fusion
  31.6 0.2 fusion.3
  31.7 0.5 fusion
  32.3 0.0 collective-permute-done.2
  32.3 0.0 collective-permute-done.3
  32.3 0.5 select_reduce_fusion.1
  32.9 13.3 %collective-permute-done.1 = bf16[320]{0:T(512)(128)(2,1)S(1)} collective-permute-done((bf16[320]{0:T(512)(128)(2,1)S(1)}, bf16[320]{0:T(512)(128)(2,1)S(1)}, u32[]{:S(2)}, u32[]{:S(2)}) %collective-permute-start.1) | collective-permute-done | bytes 672 | tf_op jit(solution)/shard_map/ppermute | solution.py:100
  46.2 0.0 collective-permute-done
  46.2 0.0 collective-permute-start.5
  46.2 0.0 copy-start
  46.2 0.7 %copy-done = s32[1,128]{1,0:T(1,128)S(1)} copy-done((s32[1,128]{1,0:T(1,128)S(1)}, s32[1,128]{1,0:T(1,128)}, u32[]{:S(2)}) %copy-start) | copy-done | bytes 536
  46.9 0.6 collective-permute-start.4
  47.5 0.5 fusion.1
  48.0 0.3 collective-permute-done.4
  48.3 0.0 collective-permute-done.5
  48.3 0.5 select_reduce_fusion
  48.9 0.1 reshape.27
  49.0 10.0 %all_to_all.11 = f32[8,8,128]{2,1,0:T(8,128)S(1)} all-to-all(f32[8,8,128]{2,1,0:T(8,128)S(1)} %pad.4), channel_id=1, replica_groups=mesh['dp'=8,'pair'=4] {'dp'}, dimensions={0} | all-to-all | bytes 65536 | tf_op jit(solution)/shard_map/all_to_all | solution.py:130
  59.0 0.1 reshape.29
  59.1 0.7 %convolution_bitcast_fusion = f32[128]{0:T(128)} fusion(f32[320,1]{0,1:T(1,128)S(1)} %reshape.29, pred[320,128]{1,0:T(32,128)(4,1)S(1)} %iota_compare_fusion.1), kind=kOutput, calls=%fused_computation.4 | convolution fusion | flops 491520 | bytes 42752 | tf_op jit(solution)/shard_map/dot_general | solution.py:132
  (9 shorter events, 0.1 us)
Async XLA Ops:
  28.9 3.4 %collective-permute-start.3 = (bf16[320,1024]{1,0:T(8,128)(2,1)S(1)}, bf16[320,1024]{1,0:T(8,128)(2,1)S(1)}, u32[]{:S(2)}, u32[]{:S(2)}) collective-permute-start(bf16[320,1024]{1,0:T(8,128)(2,1)S(1)} %slice.12), channel_id=1, source_target_pairs={{0,1},{1,0},{2,3},{3,2},{4,5},{5,4},{6,7},{7,6},{8,9},{9,8},{10,11... | collective-permute-start | bytes 1966088 | tf_op jit(solution)/shard_map/ppermute | solution.py:107
  29.0 17.2 %collective-permute-start = (bf16[320,1024]{1,0:T(8,128)(2,1)S(1)}, bf16[320,1024]{1,0:T(8,128)(2,1)S(1)}, u32[]{:S(2)}, u32[]{:S(2)}) collective-permute-start(bf16[320,1024]{1,0:T(8,128)(2,1)S(1)} %slice.12), channel_id=1, source_target_pairs={{0,2},{1,3},{2,0},{3,1},{4,6},{5,7},{6,4},{7,5},{8,10},{9,11},{10,... | collective-permute-start | bytes 1966088 | tf_op jit(solution)/shard_map/ppermute | solution.py:100
  30.6 1.6 %collective-permute-start.2 = (bf16[320]{0:T(512)(128)(2,1)S(1)}, bf16[320]{0:T(512)(128)(2,1)S(1)}, u32[]{:S(2)}, u32[]{:S(2)}) collective-permute-start(bf16[320]{0:T(512)(128)(2,1)S(1)} %slice_reduce_fusion), channel_id=1, source_target_pairs={{0,1},{1,0},{2,3},{3,2},{4,5},{5,4},{6,7},{7,6},{8,9},{9,8},{10,11... | collective-permute-start | bytes 1928 | tf_op jit(solution)/shard_map/ppermute | solution.py:107
  30.9 15.3 %collective-permute-start.1 = (bf16[320]{0:T(512)(128)(2,1)S(1)}, bf16[320]{0:T(512)(128)(2,1)S(1)}, u32[]{:S(2)}, u32[]{:S(2)}) collective-permute-start(bf16[320]{0:T(512)(128)(2,1)S(1)} %slice_reduce_fusion), channel_id=1, source_target_pairs={{0,2},{1,3},{2,0},{3,1},{4,6},{5,7},{6,4},{7,5},{8,10},{9,11},{10,... | collective-permute-start | bytes 1928 | tf_op jit(solution)/shard_map/ppermute | solution.py:100
  46.2 2.1 %collective-permute-start.5 = (bf16[320,1024]{1,0:T(8,128)(2,1)S(1)}, bf16[320,1024]{1,0:T(8,128)(2,1)S(1)}, u32[]{:S(2)}, u32[]{:S(2)}) collective-permute-start(bf16[320,1024]{1,0:T(8,128)(2,1)S(1)} %collective-permute-done), channel_id=1, source_target_pairs={{0,1},{1,0},{2,3},{3,2},{4,5},{5,4},{6,7},{7,6},{8,9},{9,8},{10,11... | collective-permute-start | bytes 1966088 | tf_op jit(solution)/shard_map/ppermute | solution.py:107
  46.2 0.7 %copy-start = (s32[1,128]{1,0:T(1,128)S(1)}, s32[1,128]{1,0:T(1,128)}, u32[]{:S(2)}) copy-start(s32[1,128]{1,0:T(1,128)} %get-tuple-element.12) | copy-start | bytes 1540
  46.9 1.4 %collective-permute-start.4 = (bf16[320]{0:T(512)(128)(2,1)S(1)}, bf16[320]{0:T(512)(128)(2,1)S(1)}, u32[]{:S(2)}, u32[]{:S(2)}) collective-permute-start(bf16[320]{0:T(512)(128)(2,1)S(1)} %collective-permute-done.1), channel_id=1, source_target_pairs={{0,1},{1,0},{2,3},{3,2},{4,5},{5,4},{6,7},{7,6},{8,9},{9,8},{10,11... | collective-permute-start | bytes 1928 | tf_op jit(solution)/shard_map/ppermute | solution.py:107
